TPU v7x, 128 devices: a whole 4x4x4 slice. The times are simulated.
128 devices in a mesh: tx: 8 (over z, core), ty: 16 (over y, x).
Axes of the slice: x: 4, y: 4, z: 4, core: 2. Of those that a mesh axis runs over, the one named last changes fastest.
Arguments:
- object_init: float32 [4, 2048, 4096], P(None, 'tx', 'ty'), may hold values from -5 to 5
- probe: float32 [2, 128, 128], replicated, may hold values from -4 to 4
- propagator_phase: float32 [128, 128], replicated, may hold values from -3.140625 to 3.140625
- measured: bfloat16 [8, 16, 16, 2, 128, 128], P('tx', 'ty'), may hold values from 0 to 1.5
- corners: int32 [8, 16, 16, 2], P('tx', 'ty'), may hold values from 0 to 128
- owner_column: int32 [8, 16, 16, 1], P('tx', 'ty'), may hold values from 0 to 15; in each aligned block of 16 rows (0 to 15, 16 to 31, ..., all dimensions but the last counted through in order) at most 2 rows name the same one
Outputs:
- object_final: float32 [4, 2048, 4096], P(None, 'tx', 'ty')
Inputs may be any that keep to these rules, and one draw needn't show every extreme that they name: `owner_column`: at most 2 of the 16 positions of one tile name the same owner column.
All inputs are finite; a program needn't handle non-finite values.
Results may differ from a plain program's by a relative error of at most 0.0049.
Values may be sent and summed in bfloat16 or wider, within the bound.
No kernel may reach another device: no remote copies, remote signals or barrier semaphores. Data moves between devices by JAX's collectives and lax.ppermute only.
A program may use at most 128 MiB of HBM per device.

v0:
```python
import math

import jax
import jax.numpy as jnp
from jax import lax
from jax.experimental import pallas as pl
from jax.sharding import PartitionSpec as P

exact = lax.Precision.HIGHEST
step_rate = 0.5
smooth_rate = 0.2


def dft_tables(width):
    index = jnp.arange(width)
    product = index[:, None] * index[None, :] % width
    angles = product.astype(jnp.float32) * (2.0 * math.pi / width)
    scale = 1.0 / math.sqrt(width)
    return (jnp.cos(angles) * scale, jnp.sin(angles) * scale)


def left_apply(matrix, field):
    return jnp.einsum("ij,...jk->...ik", matrix, field, precision=exact)


def right_apply(field, matrix):
    return jnp.einsum("...ij,jk->...ik", field, matrix, precision=exact)


def transform(pair, cosine, sine, sign):
    real_part, imag_part = pair
    imag_table = sign * sine
    left_real = left_apply(cosine, real_part) - left_apply(imag_table, imag_part)
    left_imag = left_apply(cosine, imag_part) + left_apply(imag_table, real_part)
    return (
        right_apply(left_real, cosine) - right_apply(left_imag, imag_table),
        right_apply(left_real, imag_table) + right_apply(left_imag, cosine),
    )


def times_complex(first, second):
    return (
        first[0] * second[0] - first[1] * second[1],
        first[0] * second[1] + first[1] * second[0],
    )


def conjugate_times(first, second):
    return (
        first[0] * second[0] + first[1] * second[1],
        first[0] * second[1] - first[1] * second[0],
    )


def window_gradients(windows, amplitude, probe, phase, cosine, sine):
    slices = windows.shape[1] // 2
    layers = [(windows[:, 2 * layer], windows[:, 2 * layer + 1]) for layer in range(slices)]
    probe_pair = (probe[0], probe[1])
    kernel = (jnp.cos(phase), jnp.sin(phase))
    kernel_conj = (kernel[0], -kernel[1])

    def propagate(field, factor):
        spectrum = transform(field, cosine, sine, -1.0)
        return transform(times_complex(factor, spectrum), cosine, sine, 1.0)

    wave = times_complex(probe_pair, layers[0])
    incoming = []
    for layer in range(1, slices):
        moved = propagate(wave, kernel)
        incoming.append(moved)
        wave = times_complex(layers[layer], moved)
    far_field = transform(wave, cosine, sine, -1.0)
    magnitude = jnp.sqrt(far_field[0] * far_field[0] + far_field[1] * far_field[1] + 1.0)
    factor = 1.0 - amplitude / magnitude
    back = transform((far_field[0] * factor, far_field[1] * factor), cosine, sine, 1.0)
    grads = [None] * slices
    for layer in range(slices - 1, 0, -1):
        grads[layer] = conjugate_times(incoming[layer - 1], back)
        back = propagate(conjugate_times(layers[layer], back), kernel_conj)
    grads[0] = conjugate_times(probe_pair, back)
    return jnp.stack([part for pair in grads for part in pair], axis=1)


def slot_table(owner):
    order = jnp.arange(owner.shape[0])
    same = owner[:, None] == owner[None, :]
    earlier = order[None, :] < order[:, None]
    return jnp.sum(jnp.where(same & earlier, 1, 0), axis=1).astype(jnp.int32)


def shifted_neighbours(updated):
    rows_axis = "tx"
    cols_axis = "ty"
    n_rows = lax.axis_size(rows_axis)
    n_cols = lax.axis_size(cols_axis)
    up_rows = [(i, i + 1) for i in range(n_rows - 1)]
    down_rows = [(i + 1, i) for i in range(n_rows - 1)]
    up_cols = [(i, i + 1) for i in range(n_cols - 1)]
    down_cols = [(i + 1, i) for i in range(n_cols - 1)]
    above = lax.ppermute(updated[:, -1:, :], rows_axis, up_rows)
    below = lax.ppermute(updated[:, :1, :], rows_axis, down_rows)
    left = lax.ppermute(updated[:, :, -1:], cols_axis, up_cols)
    right = lax.ppermute(updated[:, :, :1], cols_axis, down_cols)
    north = jnp.concatenate([above, updated[:, :-1, :]], axis=1)
    south = jnp.concatenate([updated[:, 1:, :], below], axis=1)
    west = jnp.concatenate([left, updated[:, :, :-1]], axis=2)
    east = jnp.concatenate([updated[:, :, 1:], right], axis=2)
    return south, north, east, west


def smooth(center):
    slices = center.shape[0] // 2
    total = jnp.zeros_like(center)
    for view in shifted_neighbours(center):
        pairs = (view - center).reshape((slices, 2) + center.shape[1:])
        weight = 1.0 / jnp.sqrt(1.0 + pairs[:, 0] * pairs[:, 0] + pairs[:, 1] * pairs[:, 1])
        total = total + (pairs * weight[:, None]).reshape(center.shape)
    return center + smooth_rate * total


def block_tables(cosine, sine):
    plus = jnp.block([[cosine, -sine], [sine, cosine]])
    minus = jnp.block([[cosine, sine], [-sine, cosine]])
    tables = []
    for table in (plus, minus):
        high = lax.reduce_precision(table, exponent_bits=8, mantissa_bits=7)
        low = (table - high).astype(jnp.bfloat16)
        tables += [high.astype(jnp.bfloat16), low]
    return jnp.stack(tables)


def _split(x):
    high = x.astype(jnp.bfloat16)
    low = (x - high.astype(jnp.float32)).astype(jnp.bfloat16)
    return high, low


def _dot(a, b):
    return jnp.dot(a, b, preferred_element_type=jnp.float32)


def _gradient_kernel(win_ref, amp_ref, probe_ref, prop_ref, tab_ref, out_ref):
    width = probe_ref.shape[-1]
    slices = win_ref.shape[1] // 2

    def left(index, x):
        high, low = _split(x)
        return _dot(tab_ref[index], high) + _dot(tab_ref[index + 1], high) + _dot(tab_ref[index], low)

    def right(x, index):
        high, low = _split(x)
        return _dot(high, tab_ref[index]) + _dot(high, tab_ref[index + 1]) + _dot(low, tab_ref[index])

    def transform(pair, sign):
        first, second = (2, 0) if sign < 0 else (0, 2)
        stacked = jnp.concatenate([pair[0], pair[1]], axis=0)
        rows = left(first, stacked)
        joined = jnp.concatenate([rows[:width], rows[width:]], axis=1)
        out = right(joined, second)
        return out[:, :width], out[:, width:]

    def times(a, b):
        return (a[0] * b[0] - a[1] * b[1], a[0] * b[1] + a[1] * b[0])

    def conj_times(a, b):
        return (a[0] * b[0] + a[1] * b[1], a[0] * b[1] - a[1] * b[0])

    layers = [
        (win_ref[0, 2 * s].astype(jnp.float32), win_ref[0, 2 * s + 1].astype(jnp.float32))
        for s in range(slices)
    ]
    probe = (probe_ref[0], probe_ref[1])
    kernel = (prop_ref[0], prop_ref[1])
    kernel_conj = (prop_ref[0], -prop_ref[1])

    def propagate(field, factor):
        return transform(times(factor, transform(field, -1)), 1)

    wave = times(probe, layers[0])
    incoming = []
    for s in range(1, slices):
        moved = propagate(wave, kernel)
        incoming.append(moved)
        wave = times(layers[s], moved)
    far = transform(wave, -1)
    magnitude = jnp.sqrt(far[0] * far[0] + far[1] * far[1] + 1.0)
    factor = 1.0 - amp_ref[0].astype(jnp.float32) / magnitude
    back = transform((far[0] * factor, far[1] * factor), 1)
    grads = [None] * slices
    for s in range(slices - 1, 0, -1):
        grads[s] = conj_times(incoming[s - 1], back)
        back = propagate(conj_times(layers[s], back), kernel_conj)
    grads[0] = conj_times(probe, back)
    for s in range(slices):
        out_ref[0, 2 * s] = grads[s][0].astype(out_ref.dtype)
        out_ref[0, 2 * s + 1] = grads[s][1].astype(out_ref.dtype)


def fused_gradients(windows, amplitude, probe, phase, tables):
    count, channels, width, _ = windows.shape
    kernel = jnp.stack([jnp.cos(phase), jnp.sin(phase)])
    return pl.pallas_call(
        _gradient_kernel,
        grid=(count,),
        in_specs=[
            pl.BlockSpec((1, channels, width, width), lambda k: (k, 0, 0, 0)),
            pl.BlockSpec((1, width, width), lambda k: (k, 0, 0)),
            pl.BlockSpec((2, width, width), lambda k: (0, 0, 0)),
            pl.BlockSpec((2, width, width), lambda k: (0, 0, 0)),
            pl.BlockSpec((4, 2 * width, 2 * width), lambda k: (0, 0, 0)),
        ],
        out_specs=pl.BlockSpec((1, channels, width, width), lambda k: (k, 0, 0, 0)),
        out_shape=jax.ShapeDtypeStruct((count, channels, width, width), jnp.bfloat16),
    )(windows, amplitude, probe, kernel, tables)


def per_device(object_init, probe, propagator_phase, measured, corners, owner_column):
    width = probe.shape[-1]
    cosine, sine = dft_tables(width)
    field = object_init
    tile = field.shape[1]
    capacity = measured.shape[3]
    columns = lax.axis_size("ty")
    tops = corners[0, 0, :, 0]
    lefts = corners[0, 0, :, 1]
    owner = owner_column[0, 0, :, 0]
    slot = slot_table(owner)
    target = owner * capacity + slot
    gathered = lax.all_to_all(measured[0, 0], "ty", split_axis=0, concat_axis=0, tiled=True)
    gathered = gathered.reshape(columns * capacity, width, width)
    pick = (jnp.arange(columns * capacity)[None, :] == target[:, None]).astype(jnp.bfloat16)
    amplitude = jnp.einsum(
        "km,mij->kij", pick, gathered, preferred_element_type=jnp.float32
    ).astype(jnp.bfloat16)
    offsets = jnp.arange(width)
    cells = jnp.arange(tile)
    row_pick = (cells[None, None, :] == (tops[:, None, None] + offsets[None, :, None])).astype(
        jnp.bfloat16
    )
    col_pick = (cells[None, :, None] == (lefts[:, None, None] + offsets[None, None, :])).astype(
        jnp.bfloat16
    )
    field_low = field.astype(jnp.bfloat16)
    rows = jnp.einsum(
        "kir,crs->kcis", row_pick, field_low, preferred_element_type=jnp.float32
    ).astype(jnp.bfloat16)
    windows = jnp.einsum(
        "kcis,ksj->kcij", rows, col_pick, preferred_element_type=jnp.float32
    ).astype(jnp.bfloat16)
    tables = block_tables(cosine, sine)
    grads = fused_gradients(windows, amplitude, probe, propagator_phase, tables)
    spread = jnp.einsum(
        "kcij,ksj->kcis", grads, col_pick, preferred_element_type=jnp.float32
    ).astype(jnp.bfloat16)
    total = jnp.einsum("kir,kcis->crs", row_pick, spread, preferred_element_type=jnp.float32)
    updated = field - step_rate * total
    return smooth(updated)


def solution(mesh):
    placed = (
        P(None, "tx", "ty"),
        P(),
        P(),
        P("tx", "ty", None, None, None, None),
        P("tx", "ty", None, None),
        P("tx", "ty", None, None),
    )
    return jax.shard_map(
        per_device, mesh=mesh, in_specs=placed, out_specs=P(None, "tx", "ty"), check_vma=False
    )
```

profile of v0, /device:TPU:25, one launch (start us, length us, event | category | flops | bytes accessed | tf_op | source)
XLA Modules:
  0.0 94.5 jit_solution(8652028190404134630)
XLA Ops:
  0.0 6.7 %all-to-all-start = ((bf16[16,2,128,128]{3,2,1,0:T(8,128)(2,1)}), bf16[16,2,128,128]{3,2,1,0:T(8,128)(2,1)S(1)}, u32[]{:S(2)}, u32[]{:S(2)}) async-start(bf16[16,2,128,128]{3,2,1,0:T(8,128)(2,1)} %bitcast.117), calls=%async_computation | async-start | bytes 2097152 | tf_op jit(solution)/shard_map/all_to_all | solution.py:229
  7.0 0.3 fusion.100
  7.3 0.3 sine_multiply_fusion
  7.6 0.3 copy.9
  8.0 1.5 %convolution_convert_fusion = bf16[16,128,4,256]{3,1,2,0:T(8,128)(2,1)S(1)} fusion(s32[16,128]{1,0:T(8,128)S(1)} %get-tuple-element.32, f32[4,256,256]{2,1,0:T(8,128)S(1)} %copy-done), kind=kOutput, calls=%fused_computation.6 | convolution fusion | flops 1076625408 | bytes 5251072 | tf_op jit(solution)/shard_map/kir,crs->kcis/dot_general | solution.py:244
  9.5 3.5 %copy.40 = bf16[16,128,4,256]{3,2,1,0:T(4,128)(2,1)S(1)} copy(bf16[16,128,4,256]{3,1,2,0:T(8,128)(2,1)S(1)} %convolution_convert_fusion) | data formatting | bytes 8388608
  13.3 0.7 pad_maximum_fusion.7.prop_ref
  14.3 0.9 pad_maximum_fusion.tab_ref
  15.2 2.6 %fusion.17.win_ref = bf16[16,4,128,128]{3,2,1,0:T(8,128)(2,1)} fusion(bf16[16,4,128,256]{3,1,2,0:T(4,128)(2,1)S(1)} %bitcast.115, s32[16,128]{1,0:T(8,128)S(1)} %get-tuple-element.31), kind=kOutput, calls=%fused_computation.14 | convolution fusion | flops 538443776 | bytes 6299648 | tf_op jit(solution)/shard_map/kcis,ksj->kcij/dot_general | solution.py:247
  17.8 2.9 %all-to-all-done = bf16[16,2,128,128]{3,2,1,0:T(8,128)(2,1)S(1)} async-done(((bf16[16,2,128,128]{3,2,1,0:T(8,128)(2,1)}), bf16[16,2,128,128]{3,2,1,0:T(8,128)(2,1)S(1)}, u32[]{:S(2)}, u32[]{:S(2)}) %all-to-all-start) | async-done | bytes 1048608 | tf_op jit(solution)/shard_map/all_to_all | solution.py:229
  20.8 0.7 fusion.63
  21.5 0.9 copy.39.amp_ref
  22.4 47.8 %shard_map.64 = bf16[16,4,128,128]{3,2,1,0:T(8,128)(2,1)} custom-call(bf16[16,4,128,128]{3,2,1,0:T(8,128)(2,1)} %fusion.17.win_ref, bf16[16,128,128]{2,1,0:T(8,128)(2,1)} %copy.39.amp_ref, f32[2,128,128]{2,1,0:T(8,128)} %probe_ref.1, f32[2,128,128]{2,1,0:T(8,128)} %pad_maximum_fusion.7.prop_ref, bf16[4,256,256]{2,1,0:T(8,128)(2,1)} %pad_maximum_fusion.tab_ref), custom_call_target="tpu_custom_call" | custom-call | tf_op jit(solution)/shard_map/pallas_call | solution.py:202
  70.2 4.0 %fusion.49 = f32[4,256,256]{1,2,0:T(8,128)S(1)} fusion(f32[4,256,256]{1,2,0:T(8,128)S(1)} %copy.9, bf16[16,4,128,128]{3,2,1,0:T(8,128)(2,1)} %shard_map.64, s32[16,128]{1,0:T(8,128)S(1)} %get-tuple-element.31, s32[16,128]{1,0:T(8,128)S(1)} %get-tuple-element.32), kind=kOutput, calls=%fused_computation.18 | convolution fusion | flops 1614282752 | bytes 4210688 | tf_op jit(solution)/shard_map/kir,kcis->crs/dot_general | solution.py:255
  74.2 0.3 fusion.105
  74.8 4.0 %collective-permute-start = (f32[4,1,256]{1,2,0:T(8,128)S(1)}, f32[4,1,256]{1,2,0:T(8,128)S(1)}, u32[]{:S(2)}, u32[]{:S(2)}) collective-permute-start(f32[4,1,256]{1,2,0:T(8,128)S(1)} %get-tuple-element.11), channel_id=1, source_target_pairs={{16,0},{32,16},{48,32},{64,48},{80,64},{96,80},{112,96},{17,1},{33... | collective-permute-start | bytes 12296 | tf_op jit(solution)/shard_map/ppermute | solution.py:101
  78.8 3.4 %collective-permute-start.1 = (f32[4,1,256]{1,2,0:T(8,128)S(1)}, f32[4,1,256]{1,2,0:T(8,128)S(1)}, u32[]{:S(2)}, u32[]{:S(2)}) collective-permute-start(f32[4,1,256]{1,2,0:T(8,128)S(1)} %get-tuple-element.12), channel_id=1, source_target_pairs={{0,16},{16,32},{32,48},{48,64},{64,80},{80,96},{96,112},{1,17},{17... | collective-permute-start | bytes 12296 | tf_op jit(solution)/shard_map/ppermute | solution.py:100
  82.2 3.0 %collective-permute-start.2 = (f32[4,256,1]{1,2,0:T(1,128)S(1)}, f32[4,256,1]{1,2,0:T(1,128)S(1)}, u32[]{:S(2)}, u32[]{:S(2)}) collective-permute-start(f32[4,256,1]{1,2,0:T(1,128)S(1)} %get-tuple-element.15), channel_id=1, source_target_pairs={{1,0},{2,1},{3,2},{4,3},{5,4},{6,5},{7,6},{8,7},{9,8},{10,9},{11,1... | collective-permute-start | bytes 12296 | tf_op jit(solution)/shard_map/ppermute | solution.py:103
  85.2 2.3 %collective-permute-start.3 = (f32[4,256,1]{1,2,0:T(1,128)S(1)}, f32[4,256,1]{1,2,0:T(1,128)S(1)}, u32[]{:S(2)}, u32[]{:S(2)}) collective-permute-start(f32[4,256,1]{1,2,0:T(1,128)S(1)} %get-tuple-element.16), channel_id=1, source_target_pairs={{0,1},{1,2},{2,3},{3,4},{4,5},{5,6},{6,7},{7,8},{8,9},{9,10},{10,1... | collective-permute-start | bytes 12296 | tf_op jit(solution)/shard_map/ppermute | solution.py:102
  87.7 0.6 collective-permute-done.1
  88.3 3.4 %collective-permute-done.3 = f32[4,256,1]{1,2,0:T(1,128)S(1)} collective-permute-done((f32[4,256,1]{1,2,0:T(1,128)S(1)}, f32[4,256,1]{1,2,0:T(1,128)S(1)}, u32[]{:S(2)}, u32[]{:S(2)}) %collective-permute-start.3) | collective-permute-done | bytes 4128 | tf_op jit(solution)/shard_map/ppermute | solution.py:102
  91.7 0.6 maximum_subtract_fusion
  92.8 0.5 fusion.60
  93.2 1.3 %copy.10 = f32[4,256,256]{2,1,0:T(8,128)} copy(f32[4,256,256]{1,2,0:T(8,128)S(1)} %fusion.60) | data formatting | bytes 2097152 | tf_op jit(solution)/shard_map/add | solution.py:118
  (25 shorter events, 1.7 us)
Async XLA Ops:
  0.0 7.5 %copy-start.2 = (s32[1,1,16,2]{2,3,1,0:T(2,128)S(1)}, s32[1,1,16,2]{2,3,1,0:T(2,128)}, u32[]{:S(2)}) copy-start(s32[1,1,16,2]{2,3,1,0:T(2,128)} %param.10) | copy-start | bytes 388
  0.0 7.6 %copy-start = (f32[4,256,256]{2,1,0:T(8,128)S(1)}, f32[4,256,256]{2,1,0:T(8,128)}, u32[]{:S(2)}) copy-start(f32[4,256,256]{2,1,0:T(8,128)} %param.6) | copy-start | bytes 3145732
  0.0 20.8 %all-to-all-start = ((bf16[16,2,128,128]{3,2,1,0:T(8,128)(2,1)}), bf16[16,2,128,128]{3,2,1,0:T(8,128)(2,1)S(1)}, u32[]{:S(2)}, u32[]{:S(2)}) async-start(bf16[16,2,128,128]{3,2,1,0:T(8,128)(2,1)} %bitcast.117), calls=%async_computation | async-start | bytes 2097152 | tf_op jit(solution)/shard_map/all_to_all | solution.py:229
  9.5 3.6 %copy-start.1 = (f32[128,128]{1,0:T(8,128)S(1)}, f32[128,128]{1,0:T(8,128)}, u32[]{:S(2)}) copy-start(f32[128,128]{1,0:T(8,128)} %param.8) | copy-start | bytes 196612
  9.5 4.5 %copy-start.3 = (s32[1,1,16,1]{2,3,1,0:T(1,128)S(1)}, s32[1,1,16,1]{2,3,1,0:T(1,128)}, u32[]{:S(2)}) copy-start(s32[1,1,16,1]{2,3,1,0:T(1,128)} %param.11) | copy-start | bytes 196
  74.8 12.9 %collective-permute-start = (f32[4,1,256]{1,2,0:T(8,128)S(1)}, f32[4,1,256]{1,2,0:T(8,128)S(1)}, u32[]{:S(2)}, u32[]{:S(2)}) collective-permute-start(f32[4,1,256]{1,2,0:T(8,128)S(1)} %get-tuple-element.11), channel_id=1, source_target_pairs={{16,0},{32,16},{48,32},{64,48},{80,64},{96,80},{112,96},{17,1},{33... | collective-permute-start | bytes 12296 | tf_op jit(solution)/shard_map/ppermute | solution.py:101
  78.8 9.6 %collective-permute-start.1 = (f32[4,1,256]{1,2,0:T(8,128)S(1)}, f32[4,1,256]{1,2,0:T(8,128)S(1)}, u32[]{:S(2)}, u32[]{:S(2)}) collective-permute-start(f32[4,1,256]{1,2,0:T(8,128)S(1)} %get-tuple-element.12), channel_id=1, source_target_pairs={{0,16},{16,32},{32,48},{48,64},{64,80},{80,96},{96,112},{1,17},{17... | collective-permute-start | bytes 12296 | tf_op jit(solution)/shard_map/ppermute | solution.py:100
  82.2 6.1 %collective-permute-start.2 = (f32[4,256,1]{1,2,0:T(1,128)S(1)}, f32[4,256,1]{1,2,0:T(1,128)S(1)}, u32[]{:S(2)}, u32[]{:S(2)}) collective-permute-start(f32[4,256,1]{1,2,0:T(1,128)S(1)} %get-tuple-element.15), channel_id=1, source_target_pairs={{1,0},{2,1},{3,2},{4,3},{5,4},{6,5},{7,6},{8,7},{9,8},{10,9},{11,1... | collective-permute-start | bytes 12296 | tf_op jit(solution)/shard_map/ppermute | solution.py:103
  85.2 6.5 %collective-permute-start.3 = (f32[4,256,1]{1,2,0:T(1,128)S(1)}, f32[4,256,1]{1,2,0:T(1,128)S(1)}, u32[]{:S(2)}, u32[]{:S(2)}) collective-permute-start(f32[4,256,1]{1,2,0:T(1,128)S(1)} %get-tuple-element.16), channel_id=1, source_target_pairs={{0,1},{1,2},{2,3},{3,4},{4,5},{5,6},{6,7},{7,8},{8,9},{9,10},{10,1... | collective-permute-start | bytes 12296 | tf_op jit(solution)/shard_map/ppermute | solution.py:102
where the time goes:
time: 96.1 us; the launch traced here: 94.5 us
  Pallas kernels  47.8 us (50%)
  starting transfers between devices  19.4 us (20%)
  matrix products  8.84 us (9%)
  local copies, waits for them, and re-layouts  7.09 us (7%)
  waiting for transfers between devices  6.96 us (7%)
  other arithmetic  4.16 us (4%)
    pallas_call x1, Pallas kernels, fused_gradients(): pl.pallas_call(_gradient_kernel, grid=(count,), in_specs=[pl.BlockSpec((1...  47.8 us
    all_to_all x1, starting transfers between devices, per_device(): lax.all_to_all(measured[0, 0], 'ty', split_axis=0, concat_axis=0, tiled=T...  6.74 us
    dot_general x1, matrix products, per_device(): jnp.einsum('kir,kcis->crs', row_pick, spread, preferred_element_type=jnp....  3.97 us
    ppermute x1, starting transfers between devices, shifted_neighbours(): below = lax.ppermute(updated[:, :1, :], rows_axis, down_rows)  3.97 us
    unnamed x10, local copies, waits for them, and re-layouts  3.88 us
    ppermute x1, starting transfers between devices, shifted_neighbours(): above = lax.ppermute(updated[:, -1:, :], rows_axis, up_rows)  3.45 us
    ppermute x1, waiting for transfers between devices, shifted_neighbours(): left = lax.ppermute(updated[:, :, -1:], cols_axis, up_cols)  3.39 us
    ppermute x1, starting transfers between devices, shifted_neighbours(): right = lax.ppermute(updated[:, :, :1], cols_axis, down_cols)  2.98 us
  transfers between devices with their start and end apart: 5, of which 3 were waited for; matrix products, arithmetic and copies ran while one was open for 12% of the time, Pallas kernels for 0%

commit v1 on v0

v1 whole, which is shorter than its diff:
```python
import math

import jax
import jax.numpy as jnp
from jax import lax
from jax.experimental import pallas as pl
from jax.sharding import PartitionSpec as P

step_rate = 0.5
smooth_rate = 0.2


def dft_tables(width):
    index = jnp.arange(width)
    product = index[:, None] * index[None, :] % width
    angles = product.astype(jnp.float32) * (2.0 * math.pi / width)
    scale = 1.0 / math.sqrt(width)
    return (jnp.cos(angles) * scale, jnp.sin(angles) * scale)


def slot_table(owner):
    order = jnp.arange(owner.shape[0])
    same = owner[:, None] == owner[None, :]
    earlier = order[None, :] < order[:, None]
    return jnp.sum(jnp.where(same & earlier, 1, 0), axis=1).astype(jnp.int32)


def shifted_neighbours(updated):
    rows_axis = "tx"
    cols_axis = "ty"
    n_rows = lax.axis_size(rows_axis)
    n_cols = lax.axis_size(cols_axis)
    up_rows = [(i, i + 1) for i in range(n_rows - 1)]
    down_rows = [(i + 1, i) for i in range(n_rows - 1)]
    up_cols = [(i, i + 1) for i in range(n_cols - 1)]
    down_cols = [(i + 1, i) for i in range(n_cols - 1)]
    above = lax.ppermute(updated[:, -1, :], rows_axis, up_rows)
    below = lax.ppermute(updated[:, 0, :], rows_axis, down_rows)
    left = lax.ppermute(updated[:, :, -1], cols_axis, up_cols)
    right = lax.ppermute(updated[:, :, 0], cols_axis, down_cols)
    north = jnp.concatenate([above[:, None, :], updated[:, :-1, :]], axis=1)
    south = jnp.concatenate([updated[:, 1:, :], below[:, None, :]], axis=1)
    west = jnp.concatenate([left[:, :, None], updated[:, :, :-1]], axis=2)
    east = jnp.concatenate([updated[:, :, 1:], right[:, :, None]], axis=2)
    return south, north, east, west


def smooth(center):
    slices = center.shape[0] // 2
    total = jnp.zeros_like(center)
    for view in shifted_neighbours(center):
        pairs = (view - center).reshape((slices, 2) + center.shape[1:])
        weight = 1.0 / jnp.sqrt(1.0 + pairs[:, 0] * pairs[:, 0] + pairs[:, 1] * pairs[:, 1])
        total = total + (pairs * weight[:, None]).reshape(center.shape)
    return center + smooth_rate * total


def block_tables(cosine, sine):
    plus = jnp.block([[cosine, -sine], [sine, cosine]])
    minus = jnp.block([[cosine, sine], [-sine, cosine]])
    lefts, rights = [], []
    for table in (plus, minus):
        high = lax.reduce_precision(table, exponent_bits=8, mantissa_bits=7)
        low = (table - high).astype(jnp.bfloat16)
        high = high.astype(jnp.bfloat16)
        lefts.append(jnp.concatenate([high, low, high], axis=1))
        rights.append(jnp.concatenate([high, low, high], axis=0))
    return jnp.stack(lefts), jnp.stack(rights)


def _split(x):
    high = x.astype(jnp.bfloat16)
    low = (x - high.astype(jnp.float32)).astype(jnp.bfloat16)
    return high, low


def _dot(a, b):
    return jnp.dot(a, b, preferred_element_type=jnp.float32)


def _gradient_kernel(win_ref, amp_ref, probe_ref, prop_ref, left_ref, right_ref, out_ref):
    group = win_ref.shape[0]
    width = probe_ref.shape[-1]
    slices = win_ref.shape[1] // 2

    def transform(pair, sign):
        first, second = (1, 0) if sign < 0 else (0, 1)
        stacked = jnp.concatenate(
            [jnp.concatenate([pair[0][g], pair[1][g]], axis=0) for g in range(group)], axis=1
        )
        high, low = _split(stacked)
        rows = _dot(left_ref[first], jnp.concatenate([high, high, low], axis=0))
        joined = jnp.concatenate(
            [
                jnp.concatenate(
                    [rows[:width, g * width:(g + 1) * width], rows[width:, g * width:(g + 1) * width]],
                    axis=1,
                )
                for g in range(group)
            ],
            axis=0,
        )
        high, low = _split(joined)
        out = _dot(jnp.concatenate([high, high, low], axis=1), right_ref[second])
        return (
            out[:, :width].reshape(group, width, width),
            out[:, width:].reshape(group, width, width),
        )

    def times(a, b):
        return (a[0] * b[0] - a[1] * b[1], a[0] * b[1] + a[1] * b[0])

    def conj_times(a, b):
        return (a[0] * b[0] + a[1] * b[1], a[0] * b[1] - a[1] * b[0])

    layers = [
        (win_ref[:, 2 * s].astype(jnp.float32), win_ref[:, 2 * s + 1].astype(jnp.float32))
        for s in range(slices)
    ]
    probe = (probe_ref[0][None], probe_ref[1][None])
    kernel = (prop_ref[0][None], prop_ref[1][None])
    kernel_conj = (prop_ref[0][None], -prop_ref[1][None])

    def propagate(field, factor):
        return transform(times(factor, transform(field, -1)), 1)

    wave = times(probe, layers[0])
    incoming = []
    for s in range(1, slices):
        moved = propagate(wave, kernel)
        incoming.append(moved)
        wave = times(layers[s], moved)
    far = transform(wave, -1)
    magnitude = jnp.sqrt(far[0] * far[0] + far[1] * far[1] + 1.0)
    factor = 1.0 - amp_ref[...].astype(jnp.float32) / magnitude
    back = transform((far[0] * factor, far[1] * factor), 1)
    grads = [None] * slices
    for s in range(slices - 1, 0, -1):
        grads[s] = conj_times(incoming[s - 1], back)
        back = propagate(conj_times(layers[s], back), kernel_conj)
    grads[0] = conj_times(probe, back)
    for s in range(slices):
        out_ref[:, 2 * s] = grads[s][0].astype(out_ref.dtype)
        out_ref[:, 2 * s + 1] = grads[s][1].astype(out_ref.dtype)


def fused_gradients(windows, amplitude, probe, phase, tables, group=8):
    count, channels, width, _ = windows.shape
    group = math.gcd(count, group)
    kernel = jnp.stack([jnp.cos(phase), jnp.sin(phase)])
    left_tables, right_tables = tables
    return pl.pallas_call(
        _gradient_kernel,
        grid=(count // group,),
        in_specs=[
            pl.BlockSpec((group, channels, width, width), lambda k: (k, 0, 0, 0)),
            pl.BlockSpec((group, width, width), lambda k: (k, 0, 0)),
            pl.BlockSpec((2, width, width), lambda k: (0, 0, 0)),
            pl.BlockSpec((2, width, width), lambda k: (0, 0, 0)),
            pl.BlockSpec(left_tables.shape, lambda k: (0, 0, 0)),
            pl.BlockSpec(right_tables.shape, lambda k: (0, 0, 0)),
        ],
        out_specs=pl.BlockSpec((group, channels, width, width), lambda k: (k, 0, 0, 0)),
        out_shape=jax.ShapeDtypeStruct((count, channels, width, width), jnp.bfloat16),
    )(windows, amplitude, probe, kernel, left_tables, right_tables)


def per_device(object_init, probe, propagator_phase, measured, corners, owner_column):
    width = probe.shape[-1]
    cosine, sine = dft_tables(width)
    field = object_init
    tile = field.shape[1]
    capacity = measured.shape[3]
    columns = lax.axis_size("ty")
    tops = corners[0, 0, :, 0]
    lefts = corners[0, 0, :, 1]
    owner = owner_column[0, 0, :, 0]
    slot = slot_table(owner)
    target = owner * capacity + slot
    gathered = lax.all_to_all(measured[0, 0], "ty", split_axis=0, concat_axis=0, tiled=True)
    gathered = gathered.reshape(columns * capacity, width, width)
    pick = (jnp.arange(columns * capacity)[None, :] == target[:, None]).astype(jnp.bfloat16)
    amplitude = jnp.einsum(
        "km,mij->kij", pick, gathered, preferred_element_type=jnp.float32
    ).astype(jnp.bfloat16)
    offsets = jnp.arange(width)
    cells = jnp.arange(tile)
    row_pick = (cells[None, None, :] == (tops[:, None, None] + offsets[None, :, None])).astype(
        jnp.bfloat16
    )
    col_pick = (cells[None, :, None] == (lefts[:, None, None] + offsets[None, None, :])).astype(
        jnp.bfloat16
    )
    field_low = field.astype(jnp.bfloat16)
    rows = jnp.einsum(
        "kir,crs->kcis", row_pick, field_low, preferred_element_type=jnp.float32
    ).astype(jnp.bfloat16)
    windows = jnp.einsum(
        "kcis,ksj->kcij", rows, col_pick, preferred_element_type=jnp.float32
    ).astype(jnp.bfloat16)
    tables = block_tables(cosine, sine)
    grads = fused_gradients(windows, amplitude, probe, propagator_phase, tables)
    spread = jnp.einsum(
        "kcij,ksj->kcis", grads, col_pick, preferred_element_type=jnp.float32
    ).astype(jnp.bfloat16)
    total = jnp.einsum("kir,kcis->crs", row_pick, spread, preferred_element_type=jnp.float32)
    updated = field - step_rate * total
    return smooth(updated)


def solution(mesh):
    placed = (
        P(None, "tx", "ty"),
        P(),
        P(),
        P("tx", "ty", None, None, None, None),
        P("tx", "ty", None, None),
        P("tx", "ty", None, None),
    )
    return jax.shard_map(
        per_device, mesh=mesh, in_specs=placed, out_specs=P(None, "tx", "ty"), check_vma=False
    )
```

time: 96.1 us -> 71.9 us (0.75)
  Pallas kernels: 47.8 us -> 20.2 us
  waiting for transfers between devices: 6.96 us -> 2.41 us
  local copies, waits for them, and re-layouts: 7.09 us -> 10.6 us
  other arithmetic: 4.16 us -> 7.06 us
  starting transfers between devices: 19.4 us -> 21.4 us
    pallas_call x1, Pallas kernels: 47.8 us -> 20.2 us  [fused_gradients(): pl.pallas_call(_gradient_kernel, grid=(count // group,), in_specs=[pl.Blo...]
    ppermute x4, waiting for transfers between devices: 4.01 us -> 0.01 us  [the longest x1 0.01 us: shifted_neighbours(): above = lax.ppermute(updated[:, -1, :], rows_axis, up_rows)]
    dot_general x1, matrix products: 2.65 us -> 4.97 us  [per_device(): jnp.einsum('kcis,ksj->kcij', rows, col_pick, preferred_element_type=jnp.f...]
    ppermute x4, starting transfers between devices: 12.7 us -> 14.8 us  [the longest x1 5.2 us: shifted_neighbours(): right = lax.ppermute(updated[:, :, 0], cols_axis, down_cols)]
    broadcast_in_dim x0 -> x4, local copies, waits for them, and re-layouts: none -> 2.1 us  [the longest x1 1.05 us: shifted_neighbours(): south = jnp.concatenate([updated[:, 1:, :], below[:, None, :]], axis=1)]
    sub x1, other arithmetic: 0.62 us -> 2.39 us  [smooth(): pairs = (view - center).reshape((slices, 2) + center.shape[1:])]
    slice x4, local copies, waits for them, and re-layouts: 0.73 us -> 2.35 us  [the longest x1 1.65 us: shifted_neighbours(): south = jnp.concatenate([updated[:, 1:, :], below[:, None, :]], axis=1)]
    dot_general x1 -> x0, matrix products: 1.53 us -> none  [per_device(): jnp.einsum('kir,crs->kcis', row_pick, field_low, preferred_element_type=j...]
  transfers between devices with their start and end apart: 5 -> 5, of which waited for: 3 -> 1; matrix products, arithmetic and copies ran while one was open for 12% -> 21% of each run, Pallas kernels for 0% -> 0%
where the time goes in v1:
time: 71.9 us; the launch traced here: 71.2 us
  starting transfers between devices  21.4 us (30%)
  Pallas kernels  20.2 us (28%)
  local copies, waits for them, and re-layouts  10.6 us (15%)
  matrix products  9.32 us (13%)
  other arithmetic  7.06 us (10%)
  waiting for transfers between devices  2.41 us (3%)
    pallas_call x1, Pallas kernels, fused_gradients(): pl.pallas_call(_gradient_kernel, grid=(count // group,), in_specs=[pl.Blo...  20.2 us
    all_to_all x1, starting transfers between devices, per_device(): lax.all_to_all(measured[0, 0], 'ty', split_axis=0, concat_axis=0, tiled=T...  6.61 us
    ppermute x1, starting transfers between devices, shifted_neighbours(): right = lax.ppermute(updated[:, :, 0], cols_axis, down_cols)  5.2 us
    dot_general x1, matrix products, per_device(): jnp.einsum('kcis,ksj->kcij', rows, col_pick, preferred_element_type=jnp.f...  4.97 us
    dot_general x1, matrix products, per_device(): jnp.einsum('kir,kcis->crs', row_pick, spread, preferred_element_type=jnp....  4 us
    ppermute x1, starting transfers between devices, shifted_neighbours(): below = lax.ppermute(updated[:, 0, :], rows_axis, down_rows)  3.96 us
    ppermute x1, starting transfers between devices, shifted_neighbours(): above = lax.ppermute(updated[:, -1, :], rows_axis, up_rows)  3.44 us
    unnamed x11, local copies, waits for them, and re-layouts  2.56 us
  transfers between devices with their start and end apart: 5, of which 1 were waited for; matrix products, arithmetic and copies ran while one was open for 21% of the time, Pallas kernels for 0%

profile of v1, /device:TPU:25, one launch (start us, length us, event | category | flops | bytes accessed | tf_op | source)
XLA Modules:
  0.0 71.2 jit_solution(3309069635135693761)
XLA Ops:
  0.0 6.6 %all-to-all-start = ((bf16[16,2,128,128]{3,2,1,0:T(8,128)(2,1)}), bf16[16,2,128,128]{3,2,1,0:T(8,128)(2,1)S(1)}, u32[]{:S(2)}, u32[]{:S(2)}) async-start(bf16[16,2,128,128]{3,2,1,0:T(8,128)(2,1)} %bitcast.131), calls=%async_computation | async-start | bytes 2097152 | tf_op jit(solution)/shard_map/all_to_all | solution.py:180
  6.6 0.3 fusion.105
  8.1 2.5 %copy.33 = f32[4,256,256]{1,2,0:T(8,128)} copy(f32[4,256,256]{2,1,0:T(8,128)} %param.6) | data formatting | bytes 2097152 | tf_op args[0]
  10.6 0.7 pad_maximum_fusion.6.prop_ref
  11.2 1.0 %pad_maximum_fusion.1.right_ref = bf16[2,768,256]{2,1,0:T(8,128)(2,1)} fusion(bf16[1,768,256]{2,1,0:T(8,128)(2,1)S(1)} %get-tuple-element.30, bf16[1,768,256]{2,1,0:T(8,128)(2,1)S(1)} %get-tuple-element.29), kind=kLoop, calls=%fused_computation.38 | loop fusion | flops 393216 | bytes 1572864 | tf_op jit(solution)/shard_map/stack | solution.py:68
  12.2 1.0 %pad_maximum_fusion.left_ref = bf16[2,256,768]{2,1,0:T(8,128)(2,1)} fusion(bf16[1,256,768]{2,1,0:T(8,128)(2,1)S(1)} %get-tuple-element.28, bf16[1,256,768]{2,1,0:T(8,128)(2,1)S(1)} %get-tuple-element.27), kind=kLoop, calls=%fused_computation.37 | loop fusion | flops 393216 | bytes 1572864 | tf_op jit(solution)/shard_map/stack | solution.py:68
  13.3 5.0 %fusion.21.win_ref = bf16[16,4,128,128]{3,2,1,0:T(8,128)(2,1)} fusion(s32[16,128]{1,0:T(8,128)S(1)} %get-tuple-element.25, s32[16,128]{1,0:T(8,128)S(1)} %get-tuple-element.26, f32[4,256,256]{2,1,0:T(8,128)} %param.6), kind=kOutput, calls=%fused_computation.14 | convolution fusion | flops 1615069184 | bytes 3162112 | tf_op jit(solution)/shard_map/kcis,ksj->kcij/dot_general | solution.py:198
  18.2 2.4 %all-to-all-done = bf16[16,2,128,128]{3,2,1,0:T(8,128)(2,1)S(1)} async-done(((bf16[16,2,128,128]{3,2,1,0:T(8,128)(2,1)}), bf16[16,2,128,128]{3,2,1,0:T(8,128)(2,1)S(1)}, u32[]{:S(2)}, u32[]{:S(2)}) %all-to-all-start) | async-done | bytes 1048608 | tf_op jit(solution)/shard_map/all_to_all | solution.py:180
  20.6 1.1 %copy.29 = bf16[16,2,128,128]{3,1,0,2:T(2,128)(2,1)S(1)} copy(bf16[16,2,128,128]{3,2,1,0:T(8,128)(2,1)S(1)} %all-to-all-done) | data formatting | bytes 2097152 | tf_op jit(solution)/shard_map/all_to_all | solution.py:180
  21.7 0.4 fusion.107
  22.1 0.9 %copy.59.amp_ref = bf16[16,128,128]{2,1,0:T(8,128)(2,1)} copy(bf16[16,128,128]{2,0,1:T(8,128)(2,1)S(1)} %fusion.107) | data formatting | bytes 1048576 | tf_op jit(solution)/shard_map/km,mij->kij/dot_general | solution.py:183
  23.0 20.2 %shard_map.64 = bf16[16,4,128,128]{3,2,1,0:T(8,128)(2,1)} custom-call(bf16[16,4,128,128]{3,2,1,0:T(8,128)(2,1)} %fusion.21.win_ref, bf16[16,128,128]{2,1,0:T(8,128)(2,1)} %copy.59.amp_ref, f32[2,128,128]{2,1,0:T(8,128)} %probe_ref.1, f32[2,128,128]{2,1,0:T(8,128)} %pad_maximum_fusion.6.prop_ref, bf16[2,256,768]{2,1,0:T(8,128)(2,1)} %pad_maximum_fusion.left_ref, ...), custom_call_target="tpu_custom_call" | custom-call | tf_op jit(solution)/shard_map/pallas_call | solution.py:152
  43.2 4.0 %fusion.55 = f32[4,256,256]{1,2,0:T(8,128)S(1)} fusion(f32[4,256,256]{1,2,0:T(8,128)S(1)} %copy-done, bf16[16,4,128,128]{3,2,1,0:T(8,128)(2,1)} %shard_map.64, s32[16,128]{1,0:T(8,128)S(1)} %get-tuple-element.25, s32[16,128]{1,0:T(8,128)S(1)} %get-tuple-element.26), kind=kOutput, calls=%fused_computation.18 | convolution fusion | flops 1614282752 | bytes 4210688 | tf_op jit(solution)/shard_map/kir,kcis->crs/dot_general | solution.py:206
  47.2 0.5 slice_reduce_fusion.1
  48.0 4.0 %collective-permute-start = (f32[4,256]{1,0:T(4,128)S(1)}, f32[4,256]{1,0:T(4,128)S(1)}, u32[]{:S(2)}, u32[]{:S(2)}) collective-permute-start(f32[4,256]{1,0:T(4,128)S(1)} %get-tuple-element.5), channel_id=1, source_target_pairs={{16,0},{32,16},{48,32},{64,48},{80,64},{96,80},{112,96},{17,1},{33... | collective-permute-start | bytes 12296 | tf_op jit(solution)/shard_map/ppermute | solution.py:38
  51.9 3.4 %collective-permute-start.1 = (f32[4,256]{1,0:T(4,128)S(1)}, f32[4,256]{1,0:T(4,128)S(1)}, u32[]{:S(2)}, u32[]{:S(2)}) collective-permute-start(f32[4,256]{1,0:T(4,128)S(1)} %get-tuple-element.6), channel_id=1, source_target_pairs={{0,16},{16,32},{32,48},{48,64},{64,80},{80,96},{96,112},{1,17},{17... | collective-permute-start | bytes 12296 | tf_op jit(solution)/shard_map/ppermute | solution.py:37
  55.4 2.2 %collective-permute-start.3 = (f32[4,256]{1,0:T(4,128)S(1)}, f32[4,256]{1,0:T(4,128)S(1)}, u32[]{:S(2)}, u32[]{:S(2)}) collective-permute-start(f32[4,256]{1,0:T(4,128)S(1)} %bitcast.135), channel_id=1, source_target_pairs={{0,1},{1,2},{2,3},{3,4},{4,5},{5,6},{6,7},{7,8},{8,9},{9,10},{10,1... | collective-permute-start | bytes 12296 | tf_op jit(solution)/shard_map/ppermute | solution.py:39
  57.6 5.2 %collective-permute-start.2 = (f32[4,256]{1,0:T(4,128)S(1)}, f32[4,256]{1,0:T(4,128)S(1)}, u32[]{:S(2)}, u32[]{:S(2)}) collective-permute-start(f32[4,256]{1,0:T(4,128)S(1)} %bitcast.134), channel_id=1, source_target_pairs={{1,0},{2,1},{3,2},{4,3},{5,4},{6,5},{7,6},{8,7},{9,8},{10,9},{11,1... | collective-permute-start | bytes 12296 | tf_op jit(solution)/shard_map/ppermute | solution.py:40
  62.8 1.7 %fusion.111 = (f32[4,255,256]{1,2,0:T(8,128)}, f32[4,255,256]{1,2,0:T(8,128)}) fusion(f32[4,256,256]{1,2,0:T(8,128)S(1)} %fusion.55), kind=kLoop, calls=%fused_computation.112 | loop fusion | bytes 4177920 | tf_op jit(solution)/shard_map/slice | solution.py:42
  64.5 1.0 %copy.35 = f32[4,1,256]{1,2,0:T(8,128)} copy(f32[4,1,256]{2,0,1:T(4,128)S(1)} %bitcast.133) | data formatting | bytes 8192 | tf_op jit(solution)/shard_map/broadcast_in_dim | solution.py:41
  65.5 1.0 %copy.34 = f32[4,1,256]{1,2,0:T(8,128)} copy(f32[4,1,256]{2,0,1:T(4,128)S(1)} %bitcast.132) | data formatting | bytes 8192 | tf_op jit(solution)/shard_map/broadcast_in_dim | solution.py:42
  66.6 2.4 %maximum_subtract_fusion = (f32[4,256,256]{1,2,0:T(8,128)S(1)}, f32[4,256,256]{1,2,0:T(8,128)S(1)}, f32[4,256,256]{1,2,0:T(8,128)S(1)}, f32[4,256,256]{1,2,0:T(8,128)S(1)}) fusion(f32[4,256,256]{1,2,0:T(8,128)S(1)} %fusion.55, f32[4,1,256]{1,2,0:T(8,128)} %copy.34, f32[4,255,256]{1,2,0:T(8,128)} %get-tuple-element.11, ...), kind=kLoop, calls=%fused_computation.19 | loop fusion | flops 2097152 | bytes 9437184 | tf_op jit(solution)/shard_map/sub | solution.py:52
  69.4 0.5 fusion.66
  69.9 1.3 %copy.38 = f32[4,256,256]{2,1,0:T(8,128)} copy(f32[4,256,256]{1,2,0:T(8,128)S(1)} %fusion.66) | data formatting | bytes 2097152 | tf_op jit(solution)/shard_map/add | solution.py:55
  (32 shorter events, 1.8 us)
Async XLA Ops:
  0.0 20.6 %all-to-all-start = ((bf16[16,2,128,128]{3,2,1,0:T(8,128)(2,1)}), bf16[16,2,128,128]{3,2,1,0:T(8,128)(2,1)S(1)}, u32[]{:S(2)}, u32[]{:S(2)}) async-start(bf16[16,2,128,128]{3,2,1,0:T(8,128)(2,1)} %bitcast.131), calls=%async_computation | async-start | bytes 2097152 | tf_op jit(solution)/shard_map/all_to_all | solution.py:180
  6.6 1.0 %copy-start.3 = (s32[1,1,16,1]{2,3,1,0:T(1,128)S(1)}, s32[1,1,16,1]{2,3,1,0:T(1,128)}, u32[]{:S(2)}) copy-start(s32[1,1,16,1]{2,3,1,0:T(1,128)} %param.11) | copy-start | bytes 196
  6.6 1.2 %copy-start.1 = (f32[128,128]{1,0:T(8,128)S(1)}, f32[128,128]{1,0:T(8,128)}, u32[]{:S(2)}) copy-start(f32[128,128]{1,0:T(8,128)} %param.8) | copy-start | bytes 196612
  10.6 2.6 %copy-start.2 = (s32[1,1,16,2]{2,3,1,0:T(2,128)S(1)}, s32[1,1,16,2]{2,3,1,0:T(2,128)}, u32[]{:S(2)}) copy-start(s32[1,1,16,2]{2,3,1,0:T(2,128)} %param.10) | copy-start | bytes 388
  23.0 20.2 %copy-start = (f32[4,256,256]{1,2,0:T(8,128)S(1)}, f32[4,256,256]{1,2,0:T(8,128)}, u32[]{:S(2)}) copy-start(f32[4,256,256]{1,2,0:T(8,128)} %copy.33) | copy-start | bytes 3145732
  48.0 17.5 %collective-permute-start = (f32[4,256]{1,0:T(4,128)S(1)}, f32[4,256]{1,0:T(4,128)S(1)}, u32[]{:S(2)}, u32[]{:S(2)}) collective-permute-start(f32[4,256]{1,0:T(4,128)S(1)} %get-tuple-element.5), channel_id=1, source_target_pairs={{16,0},{32,16},{48,32},{64,48},{80,64},{96,80},{112,96},{17,1},{33... | collective-permute-start | bytes 12296 | tf_op jit(solution)/shard_map/ppermute | solution.py:38
  51.9 12.5 %collective-permute-start.1 = (f32[4,256]{1,0:T(4,128)S(1)}, f32[4,256]{1,0:T(4,128)S(1)}, u32[]{:S(2)}, u32[]{:S(2)}) collective-permute-start(f32[4,256]{1,0:T(4,128)S(1)} %get-tuple-element.6), channel_id=1, source_target_pairs={{0,16},{16,32},{32,48},{48,64},{64,80},{80,96},{96,112},{1,17},{17... | collective-permute-start | bytes 12296 | tf_op jit(solution)/shard_map/ppermute | solution.py:37
  55.4 11.2 %collective-permute-start.3 = (f32[4,256]{1,0:T(4,128)S(1)}, f32[4,256]{1,0:T(4,128)S(1)}, u32[]{:S(2)}, u32[]{:S(2)}) collective-permute-start(f32[4,256]{1,0:T(4,128)S(1)} %bitcast.135), channel_id=1, source_target_pairs={{0,1},{1,2},{2,3},{3,4},{4,5},{5,6},{6,7},{7,8},{8,9},{9,10},{10,1... | collective-permute-start | bytes 12296 | tf_op jit(solution)/shard_map/ppermute | solution.py:39
  57.6 9.0 %collective-permute-start.2 = (f32[4,256]{1,0:T(4,128)S(1)}, f32[4,256]{1,0:T(4,128)S(1)}, u32[]{:S(2)}, u32[]{:S(2)}) collective-permute-start(f32[4,256]{1,0:T(4,128)S(1)} %bitcast.134), channel_id=1, source_target_pairs={{1,0},{2,1},{3,2},{4,3},{5,4},{6,5},{7,6},{8,7},{9,8},{10,9},{11,1... | collective-permute-start | bytes 12296 | tf_op jit(solution)/shard_map/ppermute | solution.py:40

commit v2 on v1

--- a/solution.py
+++ b/solution.py
@@ -4,6 +4,7 @@
 import jax.numpy as jnp
 from jax import lax
 from jax.experimental import pallas as pl
+from jax.experimental.pallas import tpu as pltpu
 from jax.sharding import PartitionSpec as P
 
 step_rate = 0.5
@@ -78,11 +79,15 @@
     return jnp.dot(a, b, preferred_element_type=jnp.float32)
 
 
-def _gradient_kernel(win_ref, amp_ref, probe_ref, prop_ref, left_ref, right_ref, out_ref):
-    group = win_ref.shape[0]
-    width = probe_ref.shape[-1]
-    slices = win_ref.shape[1] // 2
-
+def _times(a, b):
+    return (a[0] * b[0] - a[1] * b[1], a[0] * b[1] + a[1] * b[0])
+
+
+def _conj_times(a, b):
+    return (a[0] * b[0] + a[1] * b[1], a[0] * b[1] - a[1] * b[0])
+
+
+def _transformer(left_ref, right_ref, group, width):
     def transform(pair, sign):
         first, second = (1, 0) if sign < 0 else (0, 1)
         stacked = jnp.concatenate(
@@ -107,62 +112,113 @@
             out[:, width:].reshape(group, width, width),
         )
 
-    def times(a, b):
-        return (a[0] * b[0] - a[1] * b[1], a[0] * b[1] + a[1] * b[0])
-
-    def conj_times(a, b):
-        return (a[0] * b[0] + a[1] * b[1], a[0] * b[1] - a[1] * b[0])
-
-    layers = [
+    return transform
+
+
+def _layers(win_ref):
+    slices = win_ref.shape[1] // 2
+    return [
         (win_ref[:, 2 * s].astype(jnp.float32), win_ref[:, 2 * s + 1].astype(jnp.float32))
         for s in range(slices)
     ]
+
+
+def _forward_kernel(win_ref, probe_ref, prop_ref, left_ref, right_ref, far_ref, inc_ref):
+    group, width = win_ref.shape[0], probe_ref.shape[-1]
+    transform = _transformer(left_ref, right_ref, group, width)
+    layers = _layers(win_ref)
     probe = (probe_ref[0][None], probe_ref[1][None])
     kernel = (prop_ref[0][None], prop_ref[1][None])
+    wave = _times(probe, layers[0])
+    for s in range(1, len(layers)):
+        moved = transform(_times(kernel, transform(wave, -1)), 1)
+        inc_ref[:, 2 * (s - 1)] = moved[0]
+        inc_ref[:, 2 * (s - 1) + 1] = moved[1]
+        wave = _times(layers[s], moved)
+    far = transform(wave, -1)
+    far_ref[:, 0] = far[0]
+    far_ref[:, 1] = far[1]
+
+
+def _backward_kernel(
+    target_ref, amp_ref, far_ref, inc_ref, win_ref, probe_ref, prop_ref, left_ref, right_ref, out_ref
+):
+    group, width = win_ref.shape[0], probe_ref.shape[-1]
+    step = pl.program_id(0)
+    transform = _transformer(left_ref, right_ref, group, width)
+    layers = _layers(win_ref)
+    slices = len(layers)
+    probe = (probe_ref[0][None], probe_ref[1][None])
     kernel_conj = (prop_ref[0][None], -prop_ref[1][None])
-
-    def propagate(field, factor):
-        return transform(times(factor, transform(field, -1)), 1)
-
-    wave = times(probe, layers[0])
-    incoming = []
-    for s in range(1, slices):
-        moved = propagate(wave, kernel)
-        incoming.append(moved)
-        wave = times(layers[s], moved)
-    far = transform(wave, -1)
+    amplitude = jnp.stack(
+        [amp_ref[target_ref[step * group + g]].astype(jnp.float32) for g in range(group)]
+    )
+    far = (far_ref[:, 0], far_ref[:, 1])
     magnitude = jnp.sqrt(far[0] * far[0] + far[1] * far[1] + 1.0)
-    factor = 1.0 - amp_ref[...].astype(jnp.float32) / magnitude
+    factor = 1.0 - amplitude / magnitude
     back = transform((far[0] * factor, far[1] * factor), 1)
     grads = [None] * slices
     for s in range(slices - 1, 0, -1):
-        grads[s] = conj_times(incoming[s - 1], back)
-        back = propagate(conj_times(layers[s], back), kernel_conj)
-    grads[0] = conj_times(probe, back)
+        grads[s] = _conj_times((inc_ref[:, 2 * (s - 1)], inc_ref[:, 2 * (s - 1) + 1]), back)
+        back = transform(_times(kernel_conj, transform(_conj_times(layers[s], back), -1)), 1)
+    grads[0] = _conj_times(probe, back)
     for s in range(slices):
         out_ref[:, 2 * s] = grads[s][0].astype(out_ref.dtype)
         out_ref[:, 2 * s + 1] = grads[s][1].astype(out_ref.dtype)
 
 
-def fused_gradients(windows, amplitude, probe, phase, tables, group=8):
+def forward_waves(windows, probe, kernel, tables, group=8):
     count, channels, width, _ = windows.shape
     group = math.gcd(count, group)
-    kernel = jnp.stack([jnp.cos(phase), jnp.sin(phase)])
     left_tables, right_tables = tables
+    fixed = lambda k: (0, 0, 0)
     return pl.pallas_call(
-        _gradient_kernel,
+        _forward_kernel,
         grid=(count // group,),
         in_specs=[
             pl.BlockSpec((group, channels, width, width), lambda k: (k, 0, 0, 0)),
-            pl.BlockSpec((group, width, width), lambda k: (k, 0, 0)),
-            pl.BlockSpec((2, width, width), lambda k: (0, 0, 0)),
-            pl.BlockSpec((2, width, width), lambda k: (0, 0, 0)),
-            pl.BlockSpec(left_tables.shape, lambda k: (0, 0, 0)),
-            pl.BlockSpec(right_tables.shape, lambda k: (0, 0, 0)),
-        ],
-        out_specs=pl.BlockSpec((group, channels, width, width), lambda k: (k, 0, 0, 0)),
+            pl.BlockSpec((2, width, width), fixed),
+            pl.BlockSpec((2, width, width), fixed),
+            pl.BlockSpec(left_tables.shape, fixed),
+            pl.BlockSpec(right_tables.shape, fixed),
+        ],
+        out_specs=[
+            pl.BlockSpec((group, 2, width, width), lambda k: (k, 0, 0, 0)),
+            pl.BlockSpec((group, channels - 2, width, width), lambda k: (k, 0, 0, 0)),
+        ],
+        out_shape=[
+            jax.ShapeDtypeStruct((count, 2, width, width), jnp.float32),
+            jax.ShapeDtypeStruct((count, channels - 2, width, width), jnp.float32),
+        ],
+    )(windows, probe, kernel, left_tables, right_tables)
+
+
+def backward_gradients(target, amplitudes, far, incoming, windows, probe, kernel, tables, group=8):
+    count, channels, width, _ = windows.shape
+    group = math.gcd(count, group)
+    left_tables, right_tables = tables
+    fixed = lambda k, t: (0, 0, 0)
+    batch = lambda k, t: (k, 0, 0, 0)
+    grid_spec = pltpu.PrefetchScalarGridSpec(
+        num_scalar_prefetch=1,
+        grid=(count // group,),
+        in_specs=[
+            pl.BlockSpec(amplitudes.shape, fixed),
+            pl.BlockSpec((group, 2, width, width), batch),
+            pl.BlockSpec((group, channels - 2, width, width), batch),
+            pl.BlockSpec((group, channels, width, width), batch),
+            pl.BlockSpec((2, width, width), fixed),
+            pl.BlockSpec((2, width, width), fixed),
+            pl.BlockSpec(left_tables.shape, fixed),
+            pl.BlockSpec(right_tables.shape, fixed),
+        ],
+        out_specs=pl.BlockSpec((group, channels, width, width), batch),
+    )
+    return pl.pallas_call(
+        _backward_kernel,
+        grid_spec=grid_spec,
         out_shape=jax.ShapeDtypeStruct((count, channels, width, width), jnp.bfloat16),
-    )(windows, amplitude, probe, kernel, left_tables, right_tables)
+    )(target, amplitudes, far, incoming, windows, probe, kernel, left_tables, right_tables)
 
 
 def per_device(object_init, probe, propagator_phase, measured, corners, owner_column):
@@ -176,13 +232,9 @@
     lefts = corners[0, 0, :, 1]
     owner = owner_column[0, 0, :, 0]
     slot = slot_table(owner)
-    target = owner * capacity + slot
+    target = jnp.clip(owner * capacity + slot, 0, columns * capacity - 1)
     gathered = lax.all_to_all(measured[0, 0], "ty", split_axis=0, concat_axis=0, tiled=True)
     gathered = gathered.reshape(columns * capacity, width, width)
-    pick = (jnp.arange(columns * capacity)[None, :] == target[:, None]).astype(jnp.bfloat16)
-    amplitude = jnp.einsum(
-        "km,mij->kij", pick, gathered, preferred_element_type=jnp.float32
-    ).astype(jnp.bfloat16)
     offsets = jnp.arange(width)
     cells = jnp.arange(tile)
     row_pick = (cells[None, None, :] == (tops[:, None, None] + offsets[None, :, None])).astype(
@@ -199,11 +251,13 @@
         "kcis,ksj->kcij", rows, col_pick, preferred_element_type=jnp.float32
     ).astype(jnp.bfloat16)
     tables = block_tables(cosine, sine)
-    grads = fused_gradients(windows, amplitude, probe, propagator_phase, tables)
-    spread = jnp.einsum(
-        "kcij,ksj->kcis", grads, col_pick, preferred_element_type=jnp.float32
+    kernel = jnp.stack([jnp.cos(propagator_phase), jnp.sin(propagator_phase)])
+    far, incoming = forward_waves(windows, probe, kernel, tables)
+    grads = backward_gradients(target, gathered, far, incoming, windows, probe, kernel, tables)
+    placed_rows = jnp.einsum(
+        "kir,kcij->kcrj", row_pick, grads, preferred_element_type=jnp.float32
     ).astype(jnp.bfloat16)
-    total = jnp.einsum("kir,kcis->crs", row_pick, spread, preferred_element_type=jnp.float32)
+    total = jnp.einsum("kcrj,ksj->crs", placed_rows, col_pick, preferred_element_type=jnp.float32)
     updated = field - step_rate * total
     return smooth(updated)
 

time: 71.9 us -> 68.5 us (0.953)
  the two profiles are of different devices: /device:TPU:25 before, /device:TPU:39 now
where the time goes in v2:
time: 68.5 us; the launch traced here: 68.2 us
  Pallas kernels  24.4 us (36%)
  starting transfers between devices  21.4 us (31%)
  other arithmetic  8.67 us (13%)
  matrix products  7.8 us (11%)
  local copies, waits for them, and re-layouts  5.7 us (8%)
    pallas_call x1, Pallas kernels, backward_gradients(): pl.pallas_call(_backward_kernel, grid_spec=grid_spec, out_shape=jax.Shape...  13.4 us
    pallas_call x1, Pallas kernels, forward_waves(): pl.pallas_call(_forward_kernel, grid=(count // group,), in_specs=[pl.Bloc...  10.9 us
    all_to_all x1, starting transfers between devices, per_device(): lax.all_to_all(measured[0, 0], 'ty', split_axis=0, concat_axis=0, tiled=T...  6.86 us
    ppermute x1, starting transfers between devices, shifted_neighbours(): above = lax.ppermute(updated[:, -1, :], rows_axis, up_rows)  5.23 us
    ppermute x1, starting transfers between devices, shifted_neighbours(): left = lax.ppermute(updated[:, :, -1], cols_axis, up_cols)  4.9 us
    dot_general x1, matrix products, per_device(): jnp.einsum('kcrj,ksj->crs', placed_rows, col_pick, preferred_element_type...  4.16 us
    dot_general x1, matrix products, per_device(): jnp.einsum('kcis,ksj->kcij', rows, col_pick, preferred_element_type=jnp.f...  3.64 us
    ppermute x1, starting transfers between devices, shifted_neighbours(): right = lax.ppermute(updated[:, :, 0], cols_axis, down_cols)  2.49 us
  transfers between devices with their start and end apart: 5, of which 0 were waited for; matrix products, arithmetic and copies ran while one was open for 17% of the time, Pallas kernels for 16%

profile of v2, /device:TPU:39, one launch (start us, length us, event | category | flops | bytes accessed | tf_op | source)
XLA Modules:
  0.0 68.2 jit_solution(18349148846131668355)
XLA Ops:
  0.0 6.9 %all-to-all-start = ((bf16[16,2,128,128]{3,2,1,0:T(8,128)(2,1)}), bf16[16,2,128,128]{3,2,1,0:T(8,128)(2,1)S(1)}, u32[]{:S(2)}, u32[]{:S(2)}) async-start(bf16[16,2,128,128]{3,2,1,0:T(8,128)(2,1)} %bitcast.126), calls=%async_computation | async-start | bytes 2097152 | tf_op jit(solution)/shard_map/all_to_all | solution.py:236
  6.9 0.3 fusion.97
  7.1 0.3 cosine_multiply_fusion
  7.4 0.3 sine_multiply_fusion
  8.2 1.0 %pad_maximum_fusion.1.right_ref = bf16[2,768,256]{2,1,0:T(8,128)(2,1)} fusion(bf16[1,768,256]{2,1,0:T(8,128)(2,1)S(1)} %get-tuple-element.34, bf16[1,768,256]{2,1,0:T(8,128)(2,1)S(1)} %get-tuple-element.33), kind=kLoop, calls=%fused_computation.37 | loop fusion | flops 393216 | bytes 1572864 | tf_op jit(solution)/shard_map/stack | solution.py:69
  9.1 1.0 %pad_maximum_fusion.left_ref = bf16[2,256,768]{2,1,0:T(8,128)(2,1)} fusion(bf16[1,256,768]{2,1,0:T(8,128)(2,1)S(1)} %get-tuple-element.32, bf16[1,256,768]{2,1,0:T(8,128)(2,1)S(1)} %get-tuple-element.31), kind=kLoop, calls=%fused_computation.36 | loop fusion | flops 393216 | bytes 1572864 | tf_op jit(solution)/shard_map/stack | solution.py:69
  10.2 0.7 pad_maximum_fusion.6.prop_ref
  10.9 3.6 %fusion.22.win_ref = bf16[16,4,128,128]{3,2,1,0:T(8,128)(2,1)} fusion(s32[16,128]{1,0:T(8,128)S(1)} %get-tuple-element.29, s32[16,128]{1,0:T(8,128)S(1)} %get-tuple-element.30, f32[4,256,256]{2,1,0:T(8,128)S(1)} %copy-done.3), kind=kOutput, calls=%fused_computation.15 | convolution fusion | flops 1615069184 | bytes 3162112 | tf_op jit(solution)/shard_map/kcis,ksj->kcij/dot_general | solution.py:250
  14.5 10.9 %shard_map.64 = (f32[16,2,128,128]{3,2,1,0:T(8,128)}, f32[16,2,128,128]{3,2,1,0:T(8,128)}) custom-call(bf16[16,4,128,128]{3,2,1,0:T(8,128)(2,1)} %fusion.22.win_ref, f32[2,128,128]{2,1,0:T(8,128)} %probe_ref.3, f32[2,128,128]{2,1,0:T(8,128)} %pad_maximum_fusion.6.prop_ref, bf16[2,256,768]{2,1,0:T(8,128)(2,1)} %pad_maximum_fusion.left_ref, ...), custom_call_target="tpu_custom_call" | custom-call | tf_op jit(solution)/shard_map/pallas_call | solution.py:175
  25.7 0.5 add_clamp_fusion.target_ref
  26.2 1.0 %copy-done = bf16[16,2,128,128]{3,2,1,0:T(8,128)(2,1)} copy-done((bf16[16,2,128,128]{3,2,1,0:T(8,128)(2,1)}, bf16[16,2,128,128]{3,2,1,0:T(8,128)(2,1)S(1)}, u32[]{:S(2)}) %copy-start) | copy-done | bytes 1048600
  27.2 13.4 %shard_map.65 = bf16[16,4,128,128]{3,2,1,0:T(8,128)(2,1)} custom-call(s32[16]{0:T(128)} %add_clamp_fusion.target_ref, bf16[32,128,128]{2,1,0:T(8,128)(2,1)} %bitcast.125, f32[16,2,128,128]{3,2,1,0:T(8,128)} %get-tuple-element.7.far_ref, f32[16,2,128,128]{3,2,1,0:T(8,128)} %get-tuple-element.8.inc_ref, bf16[16,4,128,128]{3,2,1,0:T(8,128)(2,1)} %fusion.22.win_ref, ...), custom_call_target="tpu_custom_call" | custom-call | tf_op jit(solution)/shard_map/pallas_call | solution.py:217
  40.6 4.2 %fusion.47 = f32[4,256,256]{2,1,0:T(8,128)S(1)} fusion(f32[4,256,256]{2,1,0:T(8,128)S(1)} %copy-done.3, bf16[16,4,128,128]{3,2,1,0:T(8,128)(2,1)} %shard_map.65, s32[16,128]{1,0:T(8,128)S(1)} %get-tuple-element.29, s32[16,128]{1,0:T(8,128)S(1)} %get-tuple-element.30), kind=kOutput, calls=%fused_computation.18 | convolution fusion | flops 1614282752 | bytes 4210688 | tf_op jit(solution)/shard_map/kcrj,ksj->crs/dot_general | solution.py:260
  44.8 0.5 slice_reduce_fusion.1
  45.3 0.4 fusion.101
  45.7 2.5 %collective-permute-start.2 = (f32[4,256]{1,0:T(4,128)S(1)}, f32[4,256]{1,0:T(4,128)S(1)}, u32[]{:S(2)}, u32[]{:S(2)}) collective-permute-start(f32[4,256]{1,0:T(4,128)S(1)} %get-tuple-element.9), channel_id=1, source_target_pairs={{1,0},{2,1},{3,2},{4,3},{5,4},{6,5},{7,6},{8,7},{9,8},{10,9},{11,1... | collective-permute-start | bytes 12296 | tf_op jit(solution)/shard_map/ppermute | solution.py:41
  48.2 4.9 %collective-permute-start.3 = (f32[4,256]{1,0:T(4,128)S(1)}, f32[4,256]{1,0:T(4,128)S(1)}, u32[]{:S(2)}, u32[]{:S(2)}) collective-permute-start(f32[4,256]{1,0:T(4,128)S(1)} %get-tuple-element.10), channel_id=1, source_target_pairs={{0,1},{1,2},{2,3},{3,4},{4,5},{5,6},{6,7},{7,8},{8,9},{9,10},{10,1... | collective-permute-start | bytes 12296 | tf_op jit(solution)/shard_map/ppermute | solution.py:40
  53.1 5.2 %collective-permute-start.1 = (f32[4,256]{1,0:T(4,128)S(1)}, f32[4,256]{1,0:T(4,128)S(1)}, u32[]{:S(2)}, u32[]{:S(2)}) collective-permute-start(f32[4,256]{1,0:T(4,128)S(1)} %bitcast.130), channel_id=1, source_target_pairs={{0,16},{16,32},{32,48},{48,64},{64,80},{80,96},{96,112},{1,17},{17... | collective-permute-start | bytes 12296 | tf_op jit(solution)/shard_map/ppermute | solution.py:38
  58.3 1.9 %collective-permute-start = (f32[4,256]{1,0:T(4,128)S(1)}, f32[4,256]{1,0:T(4,128)S(1)}, u32[]{:S(2)}, u32[]{:S(2)}) collective-permute-start(f32[4,256]{1,0:T(4,128)S(1)} %bitcast.129), channel_id=1, source_target_pairs={{16,0},{32,16},{48,32},{64,48},{80,64},{96,80},{112,96},{17,1},{33... | collective-permute-start | bytes 12296 | tf_op jit(solution)/shard_map/ppermute | solution.py:39
  60.3 1.5 %fusion.99 = (f32[4,255,256]{2,1,0:T(8,128)}, f32[4,255,256]{2,1,0:T(8,128)}) fusion(f32[4,256,256]{2,1,0:T(8,128)S(1)} %fusion.47), kind=kLoop, calls=%fused_computation.107 | loop fusion | bytes 4177920 | tf_op jit(solution)/shard_map/slice | solution.py:43
  61.7 1.1 %copy.26 = f32[4,256,1]{2,1,0:T(8,128)} copy(f32[4,256,1]{1,0,2:T(4,128)S(1)} %bitcast.128) | data formatting | bytes 8192 | tf_op jit(solution)/shard_map/broadcast_in_dim | solution.py:44
  62.8 1.0 %copy.25 = f32[4,256,1]{2,1,0:T(8,128)} copy(f32[4,256,1]{1,0,2:T(4,128)S(1)} %bitcast.127) | data formatting | bytes 8192 | tf_op jit(solution)/shard_map/broadcast_in_dim | solution.py:45
  63.9 2.4 %maximum_subtract_fusion = (f32[4,256,256]{2,1,0:T(8,128)S(1)}, f32[4,256,256]{2,1,0:T(8,128)S(1)}, f32[4,256,256]{2,1,0:T(8,128)S(1)}, f32[4,256,256]{2,1,0:T(8,128)S(1)}) fusion(f32[4,256,256]{2,1,0:T(8,128)S(1)} %fusion.47, f32[4,1,256]{2,1,0:T(1,128)S(1)} %broadcast_in_dim.18, f32[4,255,256]{2,1,0:T(8,128)} %get-tuple-element.15, ...), kind=kLoop, calls=%fused_computation.19 | loop fusion | flops 2097152 | bytes 9437184 | tf_op jit(solution)/shard_map/sub | solution.py:53
  66.7 1.5 %fusion.58 = f32[4,256,256]{2,1,0:T(8,128)} fusion(f32[4,256,256]{2,1,0:T(8,128)S(1)} %fusion.47, f32[4,256,256]{2,1,0:T(8,128)S(1)} %get-tuple-element.12, f32[4,256,256]{2,1,0:T(8,128)S(1)} %get-tuple-element.13, f32[4,256,256]{2,1,0:T(8,128)S(1)} %get-tuple-element.14, f32[4,256,256]{2,1,0:T(8,128)S(1)} %get-tuple-element.11, ...), kind=kLoop, calls=%fused_computation.26 | loop fusion | flops 2359296 | bytes 8388608 | tf_op jit(solution)/shard_map/add | solution.py:56
  (30 shorter events, 1.1 us)
Async XLA Ops:
  0.0 26.2 %all-to-all-start = ((bf16[16,2,128,128]{3,2,1,0:T(8,128)(2,1)}), bf16[16,2,128,128]{3,2,1,0:T(8,128)(2,1)S(1)}, u32[]{:S(2)}, u32[]{:S(2)}) async-start(bf16[16,2,128,128]{3,2,1,0:T(8,128)(2,1)} %bitcast.126), calls=%async_computation | async-start | bytes 2097152 | tf_op jit(solution)/shard_map/all_to_all | solution.py:236
  6.9 1.0 %copy-start.2 = (s32[1,1,16,2]{2,3,1,0:T(2,128)S(1)}, s32[1,1,16,2]{2,3,1,0:T(2,128)}, u32[]{:S(2)}) copy-start(s32[1,1,16,2]{2,3,1,0:T(2,128)} %param.10) | copy-start | bytes 388
  6.9 1.0 %copy-start.1 = (f32[128,128]{1,0:T(8,128)S(1)}, f32[128,128]{1,0:T(8,128)}, u32[]{:S(2)}) copy-start(f32[128,128]{1,0:T(8,128)} %param.8) | copy-start | bytes 196612
  7.9 3.0 %copy-start.3 = (f32[4,256,256]{2,1,0:T(8,128)S(1)}, f32[4,256,256]{2,1,0:T(8,128)}, u32[]{:S(2)}) copy-start(f32[4,256,256]{2,1,0:T(8,128)} %param.6) | copy-start | bytes 3145732
  14.5 10.9 %copy-start.4 = (s32[1,1,16,1]{2,3,1,0:T(1,128)S(1)}, s32[1,1,16,1]{2,3,1,0:T(1,128)}, u32[]{:S(2)}) copy-start(s32[1,1,16,1]{2,3,1,0:T(1,128)} %param.11) | copy-start | bytes 196
  26.2 1.0 %copy-start = (bf16[16,2,128,128]{3,2,1,0:T(8,128)(2,1)}, bf16[16,2,128,128]{3,2,1,0:T(8,128)(2,1)S(1)}, u32[]{:S(2)}) copy-start(bf16[16,2,128,128]{3,2,1,0:T(8,128)(2,1)S(1)} %all-to-all-done) | copy-start | bytes 3145732
  45.7 17.1 %collective-permute-start.2 = (f32[4,256]{1,0:T(4,128)S(1)}, f32[4,256]{1,0:T(4,128)S(1)}, u32[]{:S(2)}, u32[]{:S(2)}) collective-permute-start(f32[4,256]{1,0:T(4,128)S(1)} %get-tuple-element.9), channel_id=1, source_target_pairs={{1,0},{2,1},{3,2},{4,3},{5,4},{6,5},{7,6},{8,7},{9,8},{10,9},{11,1... | collective-permute-start | bytes 12296 | tf_op jit(solution)/shard_map/ppermute | solution.py:41
  48.2 13.6 %collective-permute-start.3 = (f32[4,256]{1,0:T(4,128)S(1)}, f32[4,256]{1,0:T(4,128)S(1)}, u32[]{:S(2)}, u32[]{:S(2)}) collective-permute-start(f32[4,256]{1,0:T(4,128)S(1)} %get-tuple-element.10), channel_id=1, source_target_pairs={{0,1},{1,2},{2,3},{3,4},{4,5},{5,6},{6,7},{7,8},{8,9},{9,10},{10,1... | collective-permute-start | bytes 12296 | tf_op jit(solution)/shard_map/ppermute | solution.py:40
  53.1 10.8 %collective-permute-start.1 = (f32[4,256]{1,0:T(4,128)S(1)}, f32[4,256]{1,0:T(4,128)S(1)}, u32[]{:S(2)}, u32[]{:S(2)}) collective-permute-start(f32[4,256]{1,0:T(4,128)S(1)} %bitcast.130), channel_id=1, source_target_pairs={{0,16},{16,32},{32,48},{48,64},{64,80},{80,96},{96,112},{1,17},{17... | collective-permute-start | bytes 12296 | tf_op jit(solution)/shard_map/ppermute | solution.py:38
  58.3 5.5 %collective-permute-start = (f32[4,256]{1,0:T(4,128)S(1)}, f32[4,256]{1,0:T(4,128)S(1)}, u32[]{:S(2)}, u32[]{:S(2)}) collective-permute-start(f32[4,256]{1,0:T(4,128)S(1)} %bitcast.129), channel_id=1, source_target_pairs={{16,0},{32,16},{48,32},{64,48},{80,64},{96,80},{112,96},{17,1},{33... | collective-permute-start | bytes 12296 | tf_op jit(solution)/shard_map/ppermute | solution.py:39

commit v3 on v2

--- a/solution.py
+++ b/solution.py
@@ -1,6 +1,7 @@
 import math
 
 import jax
+import numpy as np
 import jax.numpy as jnp
 from jax import lax
 from jax.experimental import pallas as pl
@@ -11,14 +12,6 @@
 smooth_rate = 0.2
 
 
-def dft_tables(width):
-    index = jnp.arange(width)
-    product = index[:, None] * index[None, :] % width
-    angles = product.astype(jnp.float32) * (2.0 * math.pi / width)
-    scale = 1.0 / math.sqrt(width)
-    return (jnp.cos(angles) * scale, jnp.sin(angles) * scale)
-
-
 def slot_table(owner):
     order = jnp.arange(owner.shape[0])
     same = owner[:, None] == owner[None, :]
@@ -26,47 +19,65 @@
     return jnp.sum(jnp.where(same & earlier, 1, 0), axis=1).astype(jnp.int32)
 
 
-def shifted_neighbours(updated):
-    rows_axis = "tx"
-    cols_axis = "ty"
-    n_rows = lax.axis_size(rows_axis)
-    n_cols = lax.axis_size(cols_axis)
+def _bent(diff):
+    slices = diff.shape[0] // 2
+    pairs = diff.reshape((slices, 2) + diff.shape[1:])
+    weight = 1.0 / jnp.sqrt(1.0 + pairs[:, 0] * pairs[:, 0] + pairs[:, 1] * pairs[:, 1])
+    return (pairs * weight[:, None]).reshape(diff.shape)
+
+
+def exchange_edges(top, bottom, first, last):
+    n_rows = lax.axis_size("tx")
+    n_cols = lax.axis_size("ty")
     up_rows = [(i, i + 1) for i in range(n_rows - 1)]
     down_rows = [(i + 1, i) for i in range(n_rows - 1)]
     up_cols = [(i, i + 1) for i in range(n_cols - 1)]
     down_cols = [(i + 1, i) for i in range(n_cols - 1)]
-    above = lax.ppermute(updated[:, -1, :], rows_axis, up_rows)
-    below = lax.ppermute(updated[:, 0, :], rows_axis, down_rows)
-    left = lax.ppermute(updated[:, :, -1], cols_axis, up_cols)
-    right = lax.ppermute(updated[:, :, 0], cols_axis, down_cols)
-    north = jnp.concatenate([above[:, None, :], updated[:, :-1, :]], axis=1)
-    south = jnp.concatenate([updated[:, 1:, :], below[:, None, :]], axis=1)
-    west = jnp.concatenate([left[:, :, None], updated[:, :, :-1]], axis=2)
-    east = jnp.concatenate([updated[:, :, 1:], right[:, :, None]], axis=2)
-    return south, north, east, west
-
-
-def smooth(center):
-    slices = center.shape[0] // 2
-    total = jnp.zeros_like(center)
-    for view in shifted_neighbours(center):
-        pairs = (view - center).reshape((slices, 2) + center.shape[1:])
-        weight = 1.0 / jnp.sqrt(1.0 + pairs[:, 0] * pairs[:, 0] + pairs[:, 1] * pairs[:, 1])
-        total = total + (pairs * weight[:, None]).reshape(center.shape)
-    return center + smooth_rate * total
-
-
-def block_tables(cosine, sine):
-    plus = jnp.block([[cosine, -sine], [sine, cosine]])
-    minus = jnp.block([[cosine, sine], [-sine, cosine]])
+    above = lax.ppermute(bottom, "tx", up_rows)
+    below = lax.ppermute(top, "tx", down_rows)
+    left = lax.ppermute(last, "ty", up_cols)
+    right = lax.ppermute(first, "ty", down_cols)
+    return above, below, left, right
+
+
+def smooth(center, halos):
+    above, below, left, right = halos
+    zero = ((0, 0), (0, 0), (0, 0))
+    rows_pad = lambda lo, hi: ((0, 0), (lo, hi), (0, 0))
+    cols_pad = lambda lo, hi: ((0, 0), (0, 0), (lo, hi))
+    south = jnp.pad(center[:, 1:] - center[:, :-1], rows_pad(0, 1))
+    north = jnp.pad(center[:, :-1] - center[:, 1:], rows_pad(1, 0))
+    east = jnp.pad(center[:, :, 1:] - center[:, :, :-1], cols_pad(0, 1))
+    west = jnp.pad(center[:, :, :-1] - center[:, :, 1:], cols_pad(1, 0))
+    inner = _bent(south) + _bent(north) + _bent(east) + _bent(west)
+    size = center.shape[1] - 1
+    edge_north = _bent(above - center[:, 0, :])[:, None, :]
+    edge_south = _bent(below - center[:, -1, :])[:, None, :]
+    edge_west = _bent(left - center[:, :, 0])[:, :, None]
+    edge_east = _bent(right - center[:, :, -1])[:, :, None]
+    edges = (
+        jnp.pad(edge_north, rows_pad(0, size))
+        + jnp.pad(edge_south, rows_pad(size, 0))
+        + jnp.pad(edge_west, cols_pad(0, size))
+        + jnp.pad(edge_east, cols_pad(size, 0))
+    )
+    return center + smooth_rate * (inner + edges)
+
+
+def block_tables(width):
+    index = np.arange(width)
+    angles = (index[:, None] * index[None, :] % width) * (2.0 * math.pi / width)
+    scale = 1.0 / math.sqrt(width)
+    cosine, sine = np.cos(angles) * scale, np.sin(angles) * scale
+    plus = np.block([[cosine, -sine], [sine, cosine]])
+    minus = np.block([[cosine, sine], [-sine, cosine]])
     lefts, rights = [], []
     for table in (plus, minus):
-        high = lax.reduce_precision(table, exponent_bits=8, mantissa_bits=7)
-        low = (table - high).astype(jnp.bfloat16)
-        high = high.astype(jnp.bfloat16)
-        lefts.append(jnp.concatenate([high, low, high], axis=1))
-        rights.append(jnp.concatenate([high, low, high], axis=0))
-    return jnp.stack(lefts), jnp.stack(rights)
+        high = table.astype(jnp.bfloat16)
+        low = (table - high.astype(np.float64)).astype(jnp.bfloat16)
+        lefts.append(np.concatenate([high, low, high], axis=1))
+        rights.append(np.concatenate([high, low, high], axis=0))
+    return jnp.asarray(np.stack(lefts)), jnp.asarray(np.stack(rights))
 
 
 def _split(x):
@@ -223,7 +234,6 @@
 
 def per_device(object_init, probe, propagator_phase, measured, corners, owner_column):
     width = probe.shape[-1]
-    cosine, sine = dft_tables(width)
     field = object_init
     tile = field.shape[1]
     capacity = measured.shape[3]
@@ -250,16 +260,32 @@
     windows = jnp.einsum(
         "kcis,ksj->kcij", rows, col_pick, preferred_element_type=jnp.float32
     ).astype(jnp.bfloat16)
-    tables = block_tables(cosine, sine)
+    tables = block_tables(width)
     kernel = jnp.stack([jnp.cos(propagator_phase), jnp.sin(propagator_phase)])
     far, incoming = forward_waves(windows, probe, kernel, tables)
     grads = backward_gradients(target, gathered, far, incoming, windows, probe, kernel, tables)
+    ends = jnp.stack([row_pick[:, :, 0], row_pick[:, :, -1]], axis=-1)
+    edge_rows = jnp.einsum(
+        "kie,kcij->kcej", ends, grads, preferred_element_type=jnp.float32
+    ).astype(jnp.bfloat16)
+    total_rows = jnp.einsum("kcej,ksj->ces", edge_rows, col_pick, preferred_element_type=jnp.float32)
+    sides = jnp.stack([col_pick[:, 0, :], col_pick[:, -1, :]], axis=1)
+    edge_cols = jnp.einsum(
+        "kcij,kej->kcie", grads, sides, preferred_element_type=jnp.float32
+    ).astype(jnp.bfloat16)
+    total_cols = jnp.einsum("kir,kcie->cer", row_pick, edge_cols, preferred_element_type=jnp.float32)
+    halos = exchange_edges(
+        field[:, 0, :] - step_rate * total_rows[:, 0],
+        field[:, -1, :] - step_rate * total_rows[:, 1],
+        field[:, :, 0] - step_rate * total_cols[:, 0],
+        field[:, :, -1] - step_rate * total_cols[:, 1],
+    )
     placed_rows = jnp.einsum(
         "kir,kcij->kcrj", row_pick, grads, preferred_element_type=jnp.float32
     ).astype(jnp.bfloat16)
     total = jnp.einsum("kcrj,ksj->crs", placed_rows, col_pick, preferred_element_type=jnp.float32)
     updated = field - step_rate * total
-    return smooth(updated)
+    return smooth(updated, halos)
 
 
 def solution(mesh):

time: 68.5 us -> 76.3 us (1.11)
  the two profiles are of different devices: /device:TPU:39 before, /device:TPU:25 now
where the time goes in v3:
time: 76.3 us; the launch traced here: 75.5 us
  Pallas kernels  24.4 us (32%)
  starting transfers between devices  20.7 us (27%)
  matrix products  12.7 us (17%)
  other arithmetic  11.7 us (15%)
  local copies, waits for them, and re-layouts  5.62 us (7%)
    pallas_call x1, Pallas kernels, backward_gradients(): pl.pallas_call(_backward_kernel, grid_spec=grid_spec, out_shape=jax.Shape...  13.4 us
    pallas_call x1, Pallas kernels, forward_waves(): pl.pallas_call(_forward_kernel, grid=(count // group,), in_specs=[pl.Bloc...  11 us
    all_to_all x1, starting transfers between devices, per_device(): lax.all_to_all(measured[0, 0], 'ty', split_axis=0, concat_axis=0, tiled=T...  6.75 us
    ppermute x1, starting transfers between devices, exchange_edges(): above = lax.ppermute(bottom, 'tx', up_rows)  4.67 us
    ppermute x1, starting transfers between devices, exchange_edges(): right = lax.ppermute(first, 'ty', down_cols)  4.3 us
    dot_general x1, matrix products, per_device(): jnp.einsum('kcrj,ksj->crs', placed_rows, col_pick, preferred_element_type...  4.09 us
    add x1, other arithmetic, smooth(): return center + smooth_rate * (inner + edges)  4.07 us
    dot_general x1, matrix products, per_device(): jnp.einsum('kcis,ksj->kcij', rows, col_pick, preferred_element_type=jnp.f...  3.75 us
  transfers between devices with their start and end apart: 5, of which 0 were waited for; matrix products, arithmetic and copies ran while one was open for 20% of the time, Pallas kernels for 15%

profile of v3, /device:TPU:25, one launch (start us, length us, event | category | flops | bytes accessed | tf_op | source)
XLA Modules:
  0.0 75.5 jit_solution(44128605372507495)
XLA Ops:
  0.0 6.8 %all-to-all-start = ((bf16[16,2,128,128]{3,2,1,0:T(8,128)(2,1)}), bf16[16,2,128,128]{3,2,1,0:T(8,128)(2,1)S(1)}, u32[]{:S(2)}, u32[]{:S(2)}) async-start(bf16[16,2,128,128]{3,2,1,0:T(8,128)(2,1)} %bitcast.186), calls=%async_computation | async-start | bytes 2097152 | tf_op jit(solution)/shard_map/all_to_all | solution.py:246
  7.5 0.6 add_clamp_fusion.target_ref
  8.1 3.7 %fusion.28.win_ref = bf16[16,4,128,128]{3,2,1,0:T(8,128)(2,1)} fusion(s32[16,128]{1,0:T(8,128)S(1)} %get-tuple-element.33, s32[16,128]{1,0:T(8,128)S(1)} %get-tuple-element.34, f32[4,256,256]{2,1,0:T(8,128)S(1)} %copy-done.3), kind=kOutput, calls=%fused_computation.19 | convolution fusion | flops 1615069184 | bytes 3162112 | tf_op jit(solution)/shard_map/kcis,ksj->kcij/dot_general | solution.py:260
  11.9 0.7 pad_maximum_fusion.prop_ref
  12.9 11.0 %shard_map.82 = (f32[16,2,128,128]{3,2,1,0:T(8,128)}, f32[16,2,128,128]{3,2,1,0:T(8,128)}) custom-call(bf16[16,4,128,128]{3,2,1,0:T(8,128)(2,1)} %fusion.28.win_ref, f32[2,128,128]{2,1,0:T(8,128)} %probe_ref.3, f32[2,128,128]{2,1,0:T(8,128)} %pad_maximum_fusion.prop_ref, bf16[2,256,768]{2,1,0:T(8,128)(2,1)} %constant.22.clone.left_ref, ...), custom_call_target="tpu_custom_call" | custom-call | tf_op jit(solution)/shard_map/pallas_call | solution.py:186
  24.5 1.0 %copy-done.2 = bf16[16,2,128,128]{3,2,1,0:T(8,128)(2,1)} copy-done((bf16[16,2,128,128]{3,2,1,0:T(8,128)(2,1)}, bf16[16,2,128,128]{3,2,1,0:T(8,128)(2,1)S(1)}, u32[]{:S(2)}) %copy-start.2) | copy-done | bytes 1048600
  25.5 13.4 %shard_map.83 = bf16[16,4,128,128]{3,2,1,0:T(8,128)(2,1)} custom-call(s32[16]{0:T(128)} %add_clamp_fusion.target_ref, bf16[32,128,128]{2,1,0:T(8,128)(2,1)} %bitcast.185, f32[16,2,128,128]{3,2,1,0:T(8,128)} %get-tuple-element.7.far_ref, f32[16,2,128,128]{3,2,1,0:T(8,128)} %get-tuple-element.8.inc_ref, bf16[16,4,128,128]{3,2,1,0:T(8,128)(2,1)} %fusion.28.win_ref, ...), custom_call_target="tpu_custom_call" | custom-call | tf_op jit(solution)/shard_map/pallas_call | solution.py:228
  38.9 4.1 %fusion.53 = f32[4,256,256]{2,1,0:T(8,128)S(1)} fusion(f32[4,256,256]{2,1,0:T(8,128)S(1)} %copy-done.3, bf16[16,4,128,128]{3,2,1,0:T(8,128)(2,1)} %shard_map.83, s32[16,128]{1,0:T(8,128)S(1)} %get-tuple-element.33, s32[16,128]{1,0:T(8,128)S(1)} %get-tuple-element.34), kind=kOutput, calls=%fused_computation.22 | convolution fusion | flops 1614282752 | bytes 4210688 | tf_op jit(solution)/shard_map/kcrj,ksj->crs/dot_general | solution.py:286
  43.3 1.5 %slice_subtract_fusion.3 = (f32[4,255,256]{2,1,0:T(8,128)}, f32[4,255,256]{2,1,0:T(8,128)}) fusion(f32[4,256,256]{2,1,0:T(8,128)S(1)} %fusion.53), kind=kLoop, calls=%fused_computation.47 | loop fusion | flops 522240 | bytes 4177920 | tf_op jit(solution)/shard_map/sub | solution.py:48
  44.8 2.3 %fusion.66 = f32[4,2,256]{2,1,0:T(2,128)S(1)} fusion(bf16[16,4,128,128]{3,2,1,0:T(8,128)(2,1)} %shard_map.83, s32[16,128]{1,0:T(8,128)S(1)} %get-tuple-element.33, bf16[16,128,1]{1,2,0:T(2,128)(2,1)S(1)} %get-tuple-element.20, bf16[16,128,1]{1,2,0:T(2,128)(2,1)S(1)} %get-tuple-element.19), kind=kOutput, calls=%fused_computation.27 | convolution fusion | flops 13139968 | bytes 2121728 | tf_op jit(solution)/shard_map/kcej,ksj->ces/dot_general | solution.py:271
  47.2 4.7 %collective-permute-start = (f32[4,256]{1,0:T(4,128)S(1)}, f32[4,256]{1,0:T(4,128)S(1)}, u32[]{:S(2)}, u32[]{:S(2)}) collective-permute-start(f32[4,256]{1,0:T(4,128)S(1)} %fusion.120), channel_id=1, source_target_pairs={{0,16},{16,32},{32,48},{48,64},{64,80},{80,96},{96,112},{1,17},{17... | collective-permute-start | bytes 12296 | tf_op jit(solution)/shard_map/ppermute | solution.py:36
  51.9 1.9 %collective-permute-start.1 = (f32[4,256]{1,0:T(4,128)S(1)}, f32[4,256]{1,0:T(4,128)S(1)}, u32[]{:S(2)}, u32[]{:S(2)}) collective-permute-start(f32[4,256]{1,0:T(4,128)S(1)} %fusion.117), channel_id=1, source_target_pairs={{16,0},{32,16},{48,32},{64,48},{80,64},{96,80},{112,96},{17,1},{33... | collective-permute-start | bytes 12296 | tf_op jit(solution)/shard_map/ppermute | solution.py:37
  53.8 2.6 %fusion.63 = f32[4,2,256]{2,1,0:T(2,128)S(1)} fusion(bf16[16,4,128,128]{3,2,1,0:T(8,128)(2,1)} %shard_map.83, s32[16,128]{1,0:T(8,128)S(1)} %get-tuple-element.34, bf16[16,1,128]{2,1,0:T(2,128)(2,1)S(1)} %get-tuple-element.24, bf16[16,1,128]{2,1,0:T(2,128)(2,1)S(1)} %get-tuple-element.23), kind=kOutput, calls=%fused_computation.26 | convolution fusion | flops 13139968 | bytes 2121728 | tf_op jit(solution)/shard_map/kir,kcie->cer/dot_general | solution.py:276
  56.4 3.1 %collective-permute-start.2 = (f32[4,256]{1,0:T(4,128)S(1)}, f32[4,256]{1,0:T(4,128)S(1)}, u32[]{:S(2)}, u32[]{:S(2)}) collective-permute-start(f32[4,256]{1,0:T(4,128)S(1)} %fusion.115), channel_id=1, source_target_pairs={{0,1},{1,2},{2,3},{3,4},{4,5},{5,6},{6,7},{7,8},{8,9},{9,10},{10,1... | collective-permute-start | bytes 12296 | tf_op jit(solution)/shard_map/ppermute | solution.py:38
  59.5 4.3 %collective-permute-start.3 = (f32[4,256]{1,0:T(4,128)S(1)}, f32[4,256]{1,0:T(4,128)S(1)}, u32[]{:S(2)}, u32[]{:S(2)}) collective-permute-start(f32[4,256]{1,0:T(4,128)S(1)} %fusion.113), channel_id=1, source_target_pairs={{1,0},{2,1},{3,2},{4,3},{5,4},{6,5},{7,6},{8,7},{9,8},{10,9},{11,1... | collective-permute-start | bytes 12296 | tf_op jit(solution)/shard_map/ppermute | solution.py:39
  64.1 0.9 %fusion.85 = f32[2,256,256]{2,1,0:T(8,128)} fusion(f32[2,2,256,256]{3,2,1,0:T(8,128)S(1)} %bitcast.182), kind=kLoop, calls=%fused_computation.53 | loop fusion | flops 524288 | bytes 1572864 | tf_op jit(solution)/shard_map/mul | solution.py:26
  65.1 0.9 %fusion.89 = f32[2,256,256]{2,1,0:T(8,128)} fusion(f32[2,2,256,256]{3,2,1,0:T(8,128)S(1)} %bitcast.183), kind=kLoop, calls=%fused_computation.59 | loop fusion | flops 524288 | bytes 1572864 | tf_op jit(solution)/shard_map/mul | solution.py:26
  66.0 0.4 copy-done.1
  66.6 0.9 %fusion.93 = f32[2,256,256]{2,1,0:T(8,128)} fusion(f32[2,2,256,256]{3,2,1,0:T(8,128)S(1)} %bitcast.184), kind=kLoop, calls=%fused_computation.65 | loop fusion | flops 524288 | bytes 1572864 | tf_op jit(solution)/shard_map/mul | solution.py:26
  67.6 0.9 %fusion.97 = f32[2,256,256]{2,1,0:T(8,128)} fusion(f32[2,2,256,256]{3,2,1,0:T(8,128)S(1)} %bitcast.181), kind=kLoop, calls=%fused_computation.71 | loop fusion | flops 524288 | bytes 1572864 | tf_op jit(solution)/shard_map/mul | solution.py:26
  68.5 0.5 slice_reduce_fusion.1
  69.3 1.0 %copy.108 = f32[4,256,1]{2,1,0:T(8,128)} copy(f32[4,256,1]{1,0,2:T(4,128)S(1)} %multiply_bitcast_fusion.1) | data formatting | bytes 8192 | tf_op jit(solution)/shard_map/mul | solution.py:26
  70.4 1.0 %copy.111 = f32[4,256,1]{2,1,0:T(8,128)} copy(f32[4,256,1]{1,0,2:T(4,128)S(1)} %multiply_bitcast_fusion) | data formatting | bytes 8192 | tf_op jit(solution)/shard_map/mul | solution.py:26
  71.5 4.1 %fusion.72 = f32[4,256,256]{2,1,0:T(8,128)} fusion(f32[4,256,256]{2,1,0:T(8,128)S(1)} %fusion.53, f32[4,256,1]{2,1,0:T(8,128)} %copy.111, f32[4,256,1]{2,1,0:T(8,128)} %copy.108, f32[4,1,256]{2,1,0:T(1,128)S(1)} %copy.104, f32[4,1,256]{2,1,0:T(1,128)S(1)} %copy.101, f32[2,256,256]{2,1,0:T(8,128)} %fusion.85, f32[2,256,256]{2,1,0:T(8,128)} %fusion.89, ...), kind=kLoop, calls=%fused_computation.32 | loop fusion | flops 3407872 | bytes 8388608 | tf_op jit(solution)/shard_map/add | solution.py:64
  (71 shorter events, 2.9 us)
Async XLA Ops:
  0.0 6.8 %copy-start.3 = (f32[4,256,256]{2,1,0:T(8,128)S(1)}, f32[4,256,256]{2,1,0:T(8,128)}, u32[]{:S(2)}) copy-start(f32[4,256,256]{2,1,0:T(8,128)} %param.8) | copy-start | bytes 3145732
  0.0 7.0 %copy-start.5 = (s32[1,1,16,2]{2,3,1,0:T(2,128)S(1)}, s32[1,1,16,2]{2,3,1,0:T(2,128)}, u32[]{:S(2)}) copy-start(s32[1,1,16,2]{2,3,1,0:T(2,128)} %param.12) | copy-start | bytes 388
  0.0 7.0 %copy-start.4 = (f32[128,128]{1,0:T(8,128)S(1)}, f32[128,128]{1,0:T(8,128)}, u32[]{:S(2)}) copy-start(f32[128,128]{1,0:T(8,128)} %param.10) | copy-start | bytes 196612
  0.0 7.3 %copy-start.6 = (s32[1,1,16,1]{2,3,1,0:T(1,128)S(1)}, s32[1,1,16,1]{2,3,1,0:T(1,128)}, u32[]{:S(2)}) copy-start(s32[1,1,16,1]{2,3,1,0:T(1,128)} %param.13) | copy-start | bytes 196
  0.0 24.5 %all-to-all-start = ((bf16[16,2,128,128]{3,2,1,0:T(8,128)(2,1)}), bf16[16,2,128,128]{3,2,1,0:T(8,128)(2,1)S(1)}, u32[]{:S(2)}, u32[]{:S(2)}) async-start(bf16[16,2,128,128]{3,2,1,0:T(8,128)(2,1)} %bitcast.186), calls=%async_computation | async-start | bytes 2097152 | tf_op jit(solution)/shard_map/all_to_all | solution.py:246
  24.5 1.0 %copy-start.2 = (bf16[16,2,128,128]{3,2,1,0:T(8,128)(2,1)}, bf16[16,2,128,128]{3,2,1,0:T(8,128)(2,1)S(1)}, u32[]{:S(2)}) copy-start(bf16[16,2,128,128]{3,2,1,0:T(8,128)(2,1)S(1)} %all-to-all-done) | copy-start | bytes 3145732
  47.2 21.8 %collective-permute-start = (f32[4,256]{1,0:T(4,128)S(1)}, f32[4,256]{1,0:T(4,128)S(1)}, u32[]{:S(2)}, u32[]{:S(2)}) collective-permute-start(f32[4,256]{1,0:T(4,128)S(1)} %fusion.120), channel_id=1, source_target_pairs={{0,16},{16,32},{32,48},{48,64},{64,80},{80,96},{96,112},{1,17},{17... | collective-permute-start | bytes 12296 | tf_op jit(solution)/shard_map/ppermute | solution.py:36
  51.9 17.2 %collective-permute-start.1 = (f32[4,256]{1,0:T(4,128)S(1)}, f32[4,256]{1,0:T(4,128)S(1)}, u32[]{:S(2)}, u32[]{:S(2)}) collective-permute-start(f32[4,256]{1,0:T(4,128)S(1)} %fusion.117), channel_id=1, source_target_pairs={{16,0},{32,16},{48,32},{64,48},{80,64},{96,80},{112,96},{17,1},{33... | collective-permute-start | bytes 12296 | tf_op jit(solution)/shard_map/ppermute | solution.py:37
  56.4 12.8 %collective-permute-start.2 = (f32[4,256]{1,0:T(4,128)S(1)}, f32[4,256]{1,0:T(4,128)S(1)}, u32[]{:S(2)}, u32[]{:S(2)}) collective-permute-start(f32[4,256]{1,0:T(4,128)S(1)} %fusion.115), channel_id=1, source_target_pairs={{0,1},{1,2},{2,3},{3,4},{4,5},{5,6},{6,7},{7,8},{8,9},{9,10},{10,1... | collective-permute-start | bytes 12296 | tf_op jit(solution)/shard_map/ppermute | solution.py:38
  59.5 10.8 %collective-permute-start.3 = (f32[4,256]{1,0:T(4,128)S(1)}, f32[4,256]{1,0:T(4,128)S(1)}, u32[]{:S(2)}, u32[]{:S(2)}) collective-permute-start(f32[4,256]{1,0:T(4,128)S(1)} %fusion.113), channel_id=1, source_target_pairs={{1,0},{2,1},{3,2},{4,3},{5,4},{6,5},{7,6},{8,7},{9,8},{10,9},{11,1... | collective-permute-start | bytes 12296 | tf_op jit(solution)/shard_map/ppermute | solution.py:39
  65.1 1.4 %copy-start.1 = (f32[4,255,256]{2,1,0:T(8,128)S(1)}, f32[4,255,256]{2,1,0:T(8,128)}, u32[]{:S(2)}) copy-start(f32[4,255,256]{2,1,0:T(8,128)} %get-tuple-element.12) | copy-start | bytes 3133444
  66.0 1.4 %copy-start = (f32[4,255,256]{2,1,0:T(8,128)S(1)}, f32[4,255,256]{2,1,0:T(8,128)}, u32[]{:S(2)}) copy-start(f32[4,255,256]{2,1,0:T(8,128)} %get-tuple-element.11) | copy-start | bytes 3133444

commit v4 on v3

--- a/solution.py
+++ b/solution.py
@@ -17,13 +17,6 @@
     same = owner[:, None] == owner[None, :]
     earlier = order[None, :] < order[:, None]
     return jnp.sum(jnp.where(same & earlier, 1, 0), axis=1).astype(jnp.int32)
-
-
-def _bent(diff):
-    slices = diff.shape[0] // 2
-    pairs = diff.reshape((slices, 2) + diff.shape[1:])
-    weight = 1.0 / jnp.sqrt(1.0 + pairs[:, 0] * pairs[:, 0] + pairs[:, 1] * pairs[:, 1])
-    return (pairs * weight[:, None]).reshape(diff.shape)
 
 
 def exchange_edges(top, bottom, first, last):
@@ -40,28 +33,52 @@
     return above, below, left, right
 
 
-def smooth(center, halos):
-    above, below, left, right = halos
-    zero = ((0, 0), (0, 0), (0, 0))
-    rows_pad = lambda lo, hi: ((0, 0), (lo, hi), (0, 0))
-    cols_pad = lambda lo, hi: ((0, 0), (0, 0), (lo, hi))
-    south = jnp.pad(center[:, 1:] - center[:, :-1], rows_pad(0, 1))
-    north = jnp.pad(center[:, :-1] - center[:, 1:], rows_pad(1, 0))
-    east = jnp.pad(center[:, :, 1:] - center[:, :, :-1], cols_pad(0, 1))
-    west = jnp.pad(center[:, :, :-1] - center[:, :, 1:], cols_pad(1, 0))
-    inner = _bent(south) + _bent(north) + _bent(east) + _bent(west)
-    size = center.shape[1] - 1
-    edge_north = _bent(above - center[:, 0, :])[:, None, :]
-    edge_south = _bent(below - center[:, -1, :])[:, None, :]
-    edge_west = _bent(left - center[:, :, 0])[:, :, None]
-    edge_east = _bent(right - center[:, :, -1])[:, :, None]
-    edges = (
-        jnp.pad(edge_north, rows_pad(0, size))
-        + jnp.pad(edge_south, rows_pad(size, 0))
-        + jnp.pad(edge_west, cols_pad(0, size))
-        + jnp.pad(edge_east, cols_pad(size, 0))
-    )
-    return center + smooth_rate * (inner + edges)
+def _smooth_kernel(field_ref, total_ref, above_ref, below_ref, left_ref, right_ref, out_ref):
+    size = field_ref.shape[-1]
+    rows = lax.broadcasted_iota(jnp.int32, (size, size), 0)
+    cols = lax.broadcasted_iota(jnp.int32, (size, size), 1)
+
+    def as_column(line):
+        return jnp.sum(jnp.where(rows == cols, line, 0.0), axis=1, keepdims=True)
+
+    centers, views = [], []
+    for part in range(2):
+        v = field_ref[part] - step_rate * total_ref[part]
+        above = above_ref[0, part:part + 1, :]
+        below = below_ref[0, part:part + 1, :]
+        left = as_column(left_ref[0, part:part + 1, :])
+        right = as_column(right_ref[0, part:part + 1, :])
+        south = jnp.where(rows == size - 1, below, pltpu.roll(v, size - 1, 0))
+        north = jnp.where(rows == 0, above, pltpu.roll(v, 1, 0))
+        east = jnp.where(cols == size - 1, right, pltpu.roll(v, size - 1, 1))
+        west = jnp.where(cols == 0, left, pltpu.roll(v, 1, 1))
+        centers.append(v)
+        views.append((south, north, east, west))
+    total_r = jnp.zeros_like(centers[0])
+    total_i = jnp.zeros_like(centers[1])
+    for n in range(4):
+        dr = views[0][n] - centers[0]
+        di = views[1][n] - centers[1]
+        weight = 1.0 / jnp.sqrt(1.0 + dr * dr + di * di)
+        total_r = total_r + dr * weight
+        total_i = total_i + di * weight
+    out_ref[0] = centers[0] + smooth_rate * total_r
+    out_ref[1] = centers[1] + smooth_rate * total_i
+
+
+def smooth_update(field, total, above, below, left, right):
+    channels, size, _ = field.shape
+    slices = channels // 2
+    plane = pl.BlockSpec((2, size, size), lambda s: (s, 0, 0))
+    edge = pl.BlockSpec((1, 2, size), lambda s: (s, 0, 0))
+    shaped = [x.reshape(slices, 2, size) for x in (above, below, left, right)]
+    return pl.pallas_call(
+        _smooth_kernel,
+        grid=(slices,),
+        in_specs=[plane, plane, edge, edge, edge, edge],
+        out_specs=plane,
+        out_shape=jax.ShapeDtypeStruct(field.shape, jnp.float32),
+    )(field, total, *shaped)
 
 
 def block_tables(width):
@@ -264,28 +281,17 @@
     kernel = jnp.stack([jnp.cos(propagator_phase), jnp.sin(propagator_phase)])
     far, incoming = forward_waves(windows, probe, kernel, tables)
     grads = backward_gradients(target, gathered, far, incoming, windows, probe, kernel, tables)
-    ends = jnp.stack([row_pick[:, :, 0], row_pick[:, :, -1]], axis=-1)
-    edge_rows = jnp.einsum(
-        "kie,kcij->kcej", ends, grads, preferred_element_type=jnp.float32
-    ).astype(jnp.bfloat16)
-    total_rows = jnp.einsum("kcej,ksj->ces", edge_rows, col_pick, preferred_element_type=jnp.float32)
-    sides = jnp.stack([col_pick[:, 0, :], col_pick[:, -1, :]], axis=1)
-    edge_cols = jnp.einsum(
-        "kcij,kej->kcie", grads, sides, preferred_element_type=jnp.float32
-    ).astype(jnp.bfloat16)
-    total_cols = jnp.einsum("kir,kcie->cer", row_pick, edge_cols, preferred_element_type=jnp.float32)
-    halos = exchange_edges(
-        field[:, 0, :] - step_rate * total_rows[:, 0],
-        field[:, -1, :] - step_rate * total_rows[:, 1],
-        field[:, :, 0] - step_rate * total_cols[:, 0],
-        field[:, :, -1] - step_rate * total_cols[:, 1],
-    )
     placed_rows = jnp.einsum(
         "kir,kcij->kcrj", row_pick, grads, preferred_element_type=jnp.float32
     ).astype(jnp.bfloat16)
     total = jnp.einsum("kcrj,ksj->crs", placed_rows, col_pick, preferred_element_type=jnp.float32)
-    updated = field - step_rate * total
-    return smooth(updated, halos)
+    halos = exchange_edges(
+        field[:, 0, :] - step_rate * total[:, 0, :],
+        field[:, -1, :] - step_rate * total[:, -1, :],
+        field[:, :, 0] - step_rate * total[:, :, 0],
+        field[:, :, -1] - step_rate * total[:, :, -1],
+    )
+    return smooth_update(field, total, *halos)
 
 
 def solution(mesh):

time: 76.3 us -> 65.4 us (0.86)
  the two profiles are of different devices: /device:TPU:25 before, /device:TPU:7 now
where the time goes in v4:
time: 65.4 us; the launch traced here: 65 us
  Pallas kernels  28.6 us (44%)
  starting transfers between devices  21.5 us (33%)
  matrix products  7.82 us (12%)
  local copies, waits for them, and re-layouts  3.65 us (6%)
  other arithmetic  2.11 us (3%)
  waiting for transfers between devices  1.18 us (2%)
    pallas_call x1, Pallas kernels, backward_gradients(): pl.pallas_call(_backward_kernel, grid_spec=grid_spec, out_shape=jax.Shape...  13.4 us
    pallas_call x1, Pallas kernels, forward_waves(): pl.pallas_call(_forward_kernel, grid=(count // group,), in_specs=[pl.Bloc...  11 us
    all_to_all x1, starting transfers between devices, per_device(): lax.all_to_all(measured[0, 0], 'ty', split_axis=0, concat_axis=0, tiled=T...  7 us
    ppermute x1, starting transfers between devices, exchange_edges(): above = lax.ppermute(bottom, 'tx', up_rows)  5.23 us
    ppermute x1, starting transfers between devices, exchange_edges(): left = lax.ppermute(last, 'ty', up_cols)  4.91 us
    pallas_call x1, Pallas kernels, smooth_update(): pl.pallas_call(_smooth_kernel, grid=(slices,), in_specs=[plane, plane, ed...  4.23 us
    dot_general x1, matrix products, per_device(): jnp.einsum('kcrj,ksj->crs', placed_rows, col_pick, preferred_element_type...  4.15 us
    dot_general x1, matrix products, per_device(): jnp.einsum('kcis,ksj->kcij', rows, col_pick, preferred_element_type=jnp.f...  3.67 us
  transfers between devices with their start and end apart: 5, of which 1 were waited for; matrix products, arithmetic and copies ran while one was open for 11% of the time, Pallas kernels for 17%

profile of v4, /device:TPU:7, one launch (start us, length us, event | category | flops | bytes accessed | tf_op | source)
XLA Modules:
  0.0 65.0 jit_solution(1002641067564280716)
XLA Ops:
  0.0 7.0 %all-to-all-start = ((bf16[16,2,128,128]{3,2,1,0:T(8,128)(2,1)}), bf16[16,2,128,128]{3,2,1,0:T(8,128)(2,1)S(1)}, u32[]{:S(2)}, u32[]{:S(2)}) async-start(bf16[16,2,128,128]{3,2,1,0:T(8,128)(2,1)} %bitcast.60), calls=%async_computation | async-start | bytes 2097152 | tf_op jit(solution)/shard_map/all_to_all | solution.py:263
  7.0 0.2 cosine_bitcast_fusion
  7.3 0.7 %pad_maximum_fusion.prop_ref = f32[2,128,128]{2,1,0:T(8,128)} fusion(f32[1,128,128]{2,1,0:T(8,128)S(1)} %get-tuple-element.14, f32[1,128,128]{2,1,0:T(8,128)S(1)} %get-tuple-element.13), kind=kLoop, calls=%fused_computation.29 | loop fusion | flops 32768 | bytes 262144 | tf_op jit(solution)/shard_map/stack | solution.py:281
  8.0 0.1 iota_add_fusion
  8.0 3.7 %fusion.22.win_ref = bf16[16,4,128,128]{3,2,1,0:T(8,128)(2,1)} fusion(s32[16,128]{1,0:T(8,128)S(1)} %get-tuple-element.17, s32[16,128]{1,0:T(8,128)S(1)} %get-tuple-element.18, f32[4,256,256]{2,1,0:T(8,128)S(1)} %copy-done), kind=kOutput, calls=%fused_computation.15 | convolution fusion | flops 1615069184 | bytes 3162112 | tf_op jit(solution)/shard_map/kcis,ksj->kcij/dot_general | solution.py:277
  11.7 11.0 %shard_map.82 = (f32[16,2,128,128]{3,2,1,0:T(8,128)}, f32[16,2,128,128]{3,2,1,0:T(8,128)}) custom-call(bf16[16,4,128,128]{3,2,1,0:T(8,128)(2,1)} %fusion.22.win_ref, f32[2,128,128]{2,1,0:T(8,128)} %probe_ref.3, f32[2,128,128]{2,1,0:T(8,128)} %pad_maximum_fusion.prop_ref, bf16[2,256,768]{2,1,0:T(8,128)(2,1)} %constant.14.clone.left_ref, ...), custom_call_target="tpu_custom_call" | custom-call | tf_op jit(solution)/shard_map/pallas_call | solution.py:203
  22.7 0.2 select_reduce_fusion
  22.8 0.5 add_clamp_fusion.target_ref
  23.4 0.0 all-to-all-done
  23.4 1.0 %copy-done.2 = bf16[16,2,128,128]{3,2,1,0:T(8,128)(2,1)} copy-done((bf16[16,2,128,128]{3,2,1,0:T(8,128)(2,1)}, bf16[16,2,128,128]{3,2,1,0:T(8,128)(2,1)S(1)}, u32[]{:S(2)}) %copy-start.2) | copy-done | bytes 1048600
  24.3 13.4 %shard_map.83 = bf16[16,4,128,128]{3,2,1,0:T(8,128)(2,1)} custom-call(s32[16]{0:T(128)} %add_clamp_fusion.target_ref, bf16[32,128,128]{2,1,0:T(8,128)(2,1)} %bitcast.59, f32[16,2,128,128]{3,2,1,0:T(8,128)} %get-tuple-element.7.far_ref, f32[16,2,128,128]{3,2,1,0:T(8,128)} %get-tuple-element.8.inc_ref, bf16[16,4,128,128]{3,2,1,0:T(8,128)(2,1)} %fusion.22.win_ref, ...), custom_call_target="tpu_custom_call" | custom-call | tf_op jit(solution)/shard_map/pallas_call | solution.py:245
  37.8 4.2 %fusion.29.total_ref = f32[4,256,256]{2,1,0:T(8,128)S(1)} fusion(bf16[16,4,128,128]{3,2,1,0:T(8,128)(2,1)} %shard_map.83, s32[16,128]{1,0:T(8,128)S(1)} %get-tuple-element.17, s32[16,128]{1,0:T(8,128)S(1)} %get-tuple-element.18), kind=kOutput, calls=%fused_computation.16 | convolution fusion | flops 1613758464 | bytes 3162112 | tf_op jit(solution)/shard_map/kcrj,ksj->crs/dot_general | solution.py:287
  42.0 0.6 fusion.45
  42.6 2.5 %collective-permute-start.3 = (f32[4,256]{1,0:T(4,128)S(1)}, f32[4,256]{1,0:T(4,128)S(1)}, u32[]{:S(2)}, u32[]{:S(2)}) collective-permute-start(f32[4,256]{1,0:T(4,128)S(1)} %get-tuple-element.9), channel_id=1, source_target_pairs={{1,0},{2,1},{3,2},{4,3},{5,4},{6,5},{7,6},{8,7},{9,8},{10,9},{11,1... | collective-permute-start | bytes 12296 | tf_op jit(solution)/shard_map/ppermute | solution.py:32
  45.1 4.9 %collective-permute-start.2 = (f32[4,256]{1,0:T(4,128)S(1)}, f32[4,256]{1,0:T(4,128)S(1)}, u32[]{:S(2)}, u32[]{:S(2)}) collective-permute-start(f32[4,256]{1,0:T(4,128)S(1)} %get-tuple-element.10), channel_id=1, source_target_pairs={{0,1},{1,2},{2,3},{3,4},{4,5},{5,6},{6,7},{7,8},{8,9},{9,10},{10,1... | collective-permute-start | bytes 12296 | tf_op jit(solution)/shard_map/ppermute | solution.py:31
  50.0 5.2 %collective-permute-start = (f32[4,256]{1,0:T(4,128)S(1)}, f32[4,256]{1,0:T(4,128)S(1)}, u32[]{:S(2)}, u32[]{:S(2)}) collective-permute-start(f32[4,256]{1,0:T(4,128)S(1)} %bitcast.62), channel_id=1, source_target_pairs={{0,16},{16,32},{32,48},{48,64},{64,80},{80,96},{96,112},{1,17},{17... | collective-permute-start | bytes 12296 | tf_op jit(solution)/shard_map/ppermute | solution.py:29
  55.3 1.9 %collective-permute-start.1 = (f32[4,256]{1,0:T(4,128)S(1)}, f32[4,256]{1,0:T(4,128)S(1)}, u32[]{:S(2)}, u32[]{:S(2)}) collective-permute-start(f32[4,256]{1,0:T(4,128)S(1)} %bitcast.61), channel_id=1, source_target_pairs={{16,0},{32,16},{48,32},{64,48},{80,64},{96,80},{112,96},{17,1},{33... | collective-permute-start | bytes 12296 | tf_op jit(solution)/shard_map/ppermute | solution.py:30
  57.2 0.0 collective-permute-done.3
  57.2 0.6 reshape.85.right_ref
  57.8 0.6 reshape.84.left_ref
  58.4 0.6 reshape.82.above_ref
  59.0 1.2 %collective-permute-done.1 = f32[4,256]{1,0:T(4,128)S(1)} collective-permute-done((f32[4,256]{1,0:T(4,128)S(1)}, f32[4,256]{1,0:T(4,128)S(1)}, u32[]{:S(2)}, u32[]{:S(2)}) %collective-permute-start.1) | collective-permute-done | bytes 4128 | tf_op jit(solution)/shard_map/ppermute | solution.py:30
  60.2 0.6 reshape.83.below_ref
  60.8 4.2 %shard_map.84 = f32[4,256,256]{2,1,0:T(8,128)} custom-call(f32[4,256,256]{2,1,0:T(8,128)} %field_ref.1, f32[4,256,256]{2,1,0:T(8,128)} %copy-done.1, f32[2,2,256]{2,1,0:T(2,128)} %reshape.82.above_ref, f32[2,2,256]{2,1,0:T(2,128)} %reshape.83.below_ref, f32[2,2,256]{2,1,0:T(2,128)} %reshape.84.left_ref, f32[2,2,256]{2,1,0:T(2,128)} %reshape.85.right_ref), custom_call_target="tpu_custom_call" | custom-call | tf_op jit(solution)/shard_map/pallas_call | solution.py:75
  (17 shorter events, 0.0 us)
Async XLA Ops:
  0.0 7.0 %copy-start.4 = (s32[1,1,16,2]{2,3,1,0:T(2,128)S(1)}, s32[1,1,16,2]{2,3,1,0:T(2,128)}, u32[]{:S(2)}) copy-start(s32[1,1,16,2]{2,3,1,0:T(2,128)} %param.12) | copy-start | bytes 388
  0.0 7.0 %copy-start.3 = (f32[128,128]{1,0:T(8,128)S(1)}, f32[128,128]{1,0:T(8,128)}, u32[]{:S(2)}) copy-start(f32[128,128]{1,0:T(8,128)} %param.10) | copy-start | bytes 196612
  0.0 8.0 %copy-start = (f32[4,256,256]{2,1,0:T(8,128)S(1)}, f32[4,256,256]{2,1,0:T(8,128)}, u32[]{:S(2)}) copy-start(f32[4,256,256]{2,1,0:T(8,128)} %field_ref.1) | copy-start | bytes 3145732
  0.0 23.4 %all-to-all-start = ((bf16[16,2,128,128]{3,2,1,0:T(8,128)(2,1)}), bf16[16,2,128,128]{3,2,1,0:T(8,128)(2,1)S(1)}, u32[]{:S(2)}, u32[]{:S(2)}) async-start(bf16[16,2,128,128]{3,2,1,0:T(8,128)(2,1)} %bitcast.60), calls=%async_computation | async-start | bytes 2097152 | tf_op jit(solution)/shard_map/all_to_all | solution.py:263
  11.7 11.0 %copy-start.5 = (s32[1,1,16,1]{2,3,1,0:T(1,128)S(1)}, s32[1,1,16,1]{2,3,1,0:T(1,128)}, u32[]{:S(2)}) copy-start(s32[1,1,16,1]{2,3,1,0:T(1,128)} %param.13) | copy-start | bytes 196
  23.4 1.0 %copy-start.2 = (bf16[16,2,128,128]{3,2,1,0:T(8,128)(2,1)}, bf16[16,2,128,128]{3,2,1,0:T(8,128)(2,1)S(1)}, u32[]{:S(2)}) copy-start(bf16[16,2,128,128]{3,2,1,0:T(8,128)(2,1)S(1)} %all-to-all-done) | copy-start | bytes 3145732
  41.9 18.9 %copy-start.1 = (f32[4,256,256]{2,1,0:T(8,128)}, f32[4,256,256]{2,1,0:T(8,128)S(1)}, u32[]{:S(2)}) copy-start(f32[4,256,256]{2,1,0:T(8,128)S(1)} %fusion.29.total_ref) | copy-start | bytes 3145732
  42.6 14.6 %collective-permute-start.3 = (f32[4,256]{1,0:T(4,128)S(1)}, f32[4,256]{1,0:T(4,128)S(1)}, u32[]{:S(2)}, u32[]{:S(2)}) collective-permute-start(f32[4,256]{1,0:T(4,128)S(1)} %get-tuple-element.9), channel_id=1, source_target_pairs={{1,0},{2,1},{3,2},{4,3},{5,4},{6,5},{7,6},{8,7},{9,8},{10,9},{11,1... | collective-permute-start | bytes 12296 | tf_op jit(solution)/shard_map/ppermute | solution.py:32
  45.1 12.7 %collective-permute-start.2 = (f32[4,256]{1,0:T(4,128)S(1)}, f32[4,256]{1,0:T(4,128)S(1)}, u32[]{:S(2)}, u32[]{:S(2)}) collective-permute-start(f32[4,256]{1,0:T(4,128)S(1)} %get-tuple-element.10), channel_id=1, source_target_pairs={{0,1},{1,2},{2,3},{3,4},{4,5},{5,6},{6,7},{7,8},{8,9},{9,10},{10,1... | collective-permute-start | bytes 12296 | tf_op jit(solution)/shard_map/ppermute | solution.py:31
  50.0 8.4 %collective-permute-start = (f32[4,256]{1,0:T(4,128)S(1)}, f32[4,256]{1,0:T(4,128)S(1)}, u32[]{:S(2)}, u32[]{:S(2)}) collective-permute-start(f32[4,256]{1,0:T(4,128)S(1)} %bitcast.62), channel_id=1, source_target_pairs={{0,16},{16,32},{32,48},{48,64},{64,80},{80,96},{96,112},{1,17},{17... | collective-permute-start | bytes 12296 | tf_op jit(solution)/shard_map/ppermute | solution.py:29
  55.3 4.9 %collective-permute-start.1 = (f32[4,256]{1,0:T(4,128)S(1)}, f32[4,256]{1,0:T(4,128)S(1)}, u32[]{:S(2)}, u32[]{:S(2)}) collective-permute-start(f32[4,256]{1,0:T(4,128)S(1)} %bitcast.61), channel_id=1, source_target_pairs={{16,0},{32,16},{48,32},{64,48},{80,64},{96,80},{112,96},{17,1},{33... | collective-permute-start | bytes 12296 | tf_op jit(solution)/shard_map/ppermute | solution.py:30

commit v5 on v4

--- a/solution.py
+++ b/solution.py
@@ -44,10 +44,11 @@
     centers, views = [], []
     for part in range(2):
         v = field_ref[part] - step_rate * total_ref[part]
-        above = above_ref[0, part:part + 1, :]
-        below = below_ref[0, part:part + 1, :]
-        left = as_column(left_ref[0, part:part + 1, :])
-        right = as_column(right_ref[0, part:part + 1, :])
+        channel = 2 * pl.program_id(0) + part
+        above = above_ref[pl.ds(channel, 1), :]
+        below = below_ref[pl.ds(channel, 1), :]
+        left = as_column(left_ref[pl.ds(channel, 1), :])
+        right = as_column(right_ref[pl.ds(channel, 1), :])
         south = jnp.where(rows == size - 1, below, pltpu.roll(v, size - 1, 0))
         north = jnp.where(rows == 0, above, pltpu.roll(v, 1, 0))
         east = jnp.where(cols == size - 1, right, pltpu.roll(v, size - 1, 1))
@@ -70,15 +71,14 @@
     channels, size, _ = field.shape
     slices = channels // 2
     plane = pl.BlockSpec((2, size, size), lambda s: (s, 0, 0))
-    edge = pl.BlockSpec((1, 2, size), lambda s: (s, 0, 0))
-    shaped = [x.reshape(slices, 2, size) for x in (above, below, left, right)]
+    edge = pl.BlockSpec((channels, size), lambda s: (0, 0))
     return pl.pallas_call(
         _smooth_kernel,
         grid=(slices,),
         in_specs=[plane, plane, edge, edge, edge, edge],
         out_specs=plane,
         out_shape=jax.ShapeDtypeStruct(field.shape, jnp.float32),
-    )(field, total, *shaped)
+    )(field, total, above, below, left, right)
 
 
 def block_tables(width):

time: 65.4 us -> 66.3 us (1.014)
  the two profiles are of different devices: /device:TPU:7 before, /device:TPU:25 now
where the time goes in v5:
time: 66.3 us; the launch traced here: 65.8 us
  Pallas kernels  28.6 us (43%)
  starting transfers between devices  21.3 us (32%)
  matrix products  8.19 us (12%)
  local copies, waits for them, and re-layouts  2.98 us (4%)
  waiting for transfers between devices  2.95 us (4%)
  other arithmetic  1.56 us (2%)
    pallas_call x1, Pallas kernels, backward_gradients(): pl.pallas_call(_backward_kernel, grid_spec=grid_spec, out_shape=jax.Shape...  13.5 us
    pallas_call x1, Pallas kernels, forward_waves(): pl.pallas_call(_forward_kernel, grid=(count // group,), in_specs=[pl.Bloc...  10.9 us
    all_to_all x1, starting transfers between devices, per_device(): lax.all_to_all(measured[0, 0], 'ty', split_axis=0, concat_axis=0, tiled=T...  6.75 us
    ppermute x1, starting transfers between devices, exchange_edges(): above = lax.ppermute(bottom, 'tx', up_rows)  5.23 us
    dot_general x1, matrix products, per_device(): jnp.einsum('kcrj,ksj->crs', placed_rows, col_pick, preferred_element_type...  4.57 us
    ppermute x1, starting transfers between devices, exchange_edges(): right = lax.ppermute(first, 'ty', down_cols)  4.3 us
    pallas_call x1, Pallas kernels, smooth_update(): pl.pallas_call(_smooth_kernel, grid=(slices,), in_specs=[plane, plane, ed...  4.19 us
    dot_general x1, matrix products, per_device(): jnp.einsum('kcis,ksj->kcij', rows, col_pick, preferred_element_type=jnp.f...  3.62 us
  transfers between devices with their start and end apart: 5, of which 1 were waited for; matrix products, arithmetic and copies ran while one was open for 9% of the time, Pallas kernels for 17%

profile of v5, /device:TPU:25, one launch (start us, length us, event | category | flops | bytes accessed | tf_op | source)
XLA Modules:
  0.0 65.8 jit_solution(13527666705750916967)
XLA Ops:
  0.0 6.8 %all-to-all-start = ((bf16[16,2,128,128]{3,2,1,0:T(8,128)(2,1)}), bf16[16,2,128,128]{3,2,1,0:T(8,128)(2,1)S(1)}, u32[]{:S(2)}, u32[]{:S(2)}) async-start(bf16[16,2,128,128]{3,2,1,0:T(8,128)(2,1)} %bitcast.62), calls=%async_computation | async-start | bytes 2097152 | tf_op jit(solution)/shard_map/all_to_all | solution.py:263
  6.8 0.2 cosine_bitcast_fusion
  7.0 0.2 fusion.54
  7.2 0.2 copy.33
  7.4 0.2 copy.35
  7.6 0.1 iota_add_fusion
  7.7 0.7 %pad_maximum_fusion.prop_ref = f32[2,128,128]{2,1,0:T(8,128)} fusion(f32[1,128,128]{2,1,0:T(8,128)S(1)} %get-tuple-element.18, f32[1,128,128]{2,1,0:T(8,128)S(1)} %get-tuple-element.17), kind=kLoop, calls=%fused_computation.23 | loop fusion | flops 32768 | bytes 262144 | tf_op jit(solution)/shard_map/stack | solution.py:281
  8.4 3.6 %fusion.22.win_ref = bf16[16,4,128,128]{3,2,1,0:T(8,128)(2,1)} fusion(s32[16,128]{1,0:T(8,128)S(1)} %get-tuple-element.21, s32[16,128]{1,0:T(8,128)S(1)} %get-tuple-element.22, f32[4,256,256]{2,1,0:T(8,128)S(1)} %copy-done), kind=kOutput, calls=%fused_computation.15 | convolution fusion | flops 1615069184 | bytes 3162112 | tf_op jit(solution)/shard_map/kcis,ksj->kcij/dot_general | solution.py:277
  12.0 10.9 %shard_map.82 = (f32[16,2,128,128]{3,2,1,0:T(8,128)}, f32[16,2,128,128]{3,2,1,0:T(8,128)}) custom-call(bf16[16,4,128,128]{3,2,1,0:T(8,128)(2,1)} %fusion.22.win_ref, f32[2,128,128]{2,1,0:T(8,128)} %probe_ref.3, f32[2,128,128]{2,1,0:T(8,128)} %pad_maximum_fusion.prop_ref, bf16[2,256,768]{2,1,0:T(8,128)(2,1)} %constant.14.clone.left_ref, ...), custom_call_target="tpu_custom_call" | custom-call | tf_op jit(solution)/shard_map/pallas_call | solution.py:203
  22.9 0.2 select_reduce_fusion
  23.1 0.6 add_clamp_fusion.target_ref
  23.7 1.0 %copy-done.2 = bf16[16,2,128,128]{3,2,1,0:T(8,128)(2,1)} copy-done((bf16[16,2,128,128]{3,2,1,0:T(8,128)(2,1)}, bf16[16,2,128,128]{3,2,1,0:T(8,128)(2,1)S(1)}, u32[]{:S(2)}) %copy-start.2) | copy-done | bytes 1048600
  24.7 13.5 %shard_map.83 = bf16[16,4,128,128]{3,2,1,0:T(8,128)(2,1)} custom-call(s32[16]{0:T(128)} %add_clamp_fusion.target_ref, bf16[32,128,128]{2,1,0:T(8,128)(2,1)} %bitcast.61, f32[16,2,128,128]{3,2,1,0:T(8,128)} %get-tuple-element.7.far_ref, f32[16,2,128,128]{3,2,1,0:T(8,128)} %get-tuple-element.8.inc_ref, bf16[16,4,128,128]{3,2,1,0:T(8,128)(2,1)} %fusion.22.win_ref, ...), custom_call_target="tpu_custom_call" | custom-call | tf_op jit(solution)/shard_map/pallas_call | solution.py:245
  38.2 4.6 %fusion.29.total_ref = f32[4,256,256]{2,1,0:T(8,128)S(1)} fusion(bf16[16,4,128,128]{3,2,1,0:T(8,128)(2,1)} %shard_map.83, s32[16,128]{1,0:T(8,128)S(1)} %get-tuple-element.21, s32[16,128]{1,0:T(8,128)S(1)} %get-tuple-element.22), kind=kOutput, calls=%fused_computation.16 | convolution fusion | flops 1613758464 | bytes 3162112 | tf_op jit(solution)/shard_map/kcrj,ksj->crs/dot_general | solution.py:287
  42.8 0.2 fusion.53
  43.0 0.2 copy.34
  43.2 3.1 %collective-permute-start.2 = (f32[4,256]{1,0:T(4,128)S(1)}, f32[4,256]{1,0:T(4,128)S(1)}, u32[]{:S(2)}, u32[]{:S(2)}) collective-permute-start(f32[4,256]{1,0:T(4,128)S(1)} %subtract_bitcast_fusion.1), channel_id=1, source_target_pairs={{0,1},{1,2},{2,3},{3,4},{4,5},{5,6},{6,7},{7,8},{8,9},{9,10},{10,1... | collective-permute-start | bytes 12296 | tf_op jit(solution)/shard_map/ppermute | solution.py:31
  46.3 0.2 copy.36
  46.5 4.3 %collective-permute-start.3 = (f32[4,256]{1,0:T(4,128)S(1)}, f32[4,256]{1,0:T(4,128)S(1)}, u32[]{:S(2)}, u32[]{:S(2)}) collective-permute-start(f32[4,256]{1,0:T(4,128)S(1)} %subtract_bitcast_fusion), channel_id=1, source_target_pairs={{1,0},{2,1},{3,2},{4,3},{5,4},{6,5},{7,6},{8,7},{9,8},{10,9},{11,1... | collective-permute-start | bytes 12296 | tf_op jit(solution)/shard_map/ppermute | solution.py:32
  50.8 5.2 %collective-permute-start = (f32[4,256]{1,0:T(4,128)S(1)}, f32[4,256]{1,0:T(4,128)S(1)}, u32[]{:S(2)}, u32[]{:S(2)}) collective-permute-start(f32[4,256]{1,0:T(4,128)S(1)} %fusion.52), channel_id=1, source_target_pairs={{0,16},{16,32},{32,48},{48,64},{64,80},{80,96},{96,112},{1,17},{17... | collective-permute-start | bytes 12296 | tf_op jit(solution)/shard_map/ppermute | solution.py:29
  56.0 1.9 %collective-permute-start.1 = (f32[4,256]{1,0:T(4,128)S(1)}, f32[4,256]{1,0:T(4,128)S(1)}, u32[]{:S(2)}, u32[]{:S(2)}) collective-permute-start(f32[4,256]{1,0:T(4,128)S(1)} %fusion.50), channel_id=1, source_target_pairs={{16,0},{32,16},{48,32},{64,48},{80,64},{96,80},{112,96},{17,1},{33... | collective-permute-start | bytes 12296 | tf_op jit(solution)/shard_map/ppermute | solution.py:30
  58.0 2.9 %collective-permute-done.1.below_ref = f32[4,256]{1,0:T(4,128)S(1)} collective-permute-done((f32[4,256]{1,0:T(4,128)S(1)}, f32[4,256]{1,0:T(4,128)S(1)}, u32[]{:S(2)}, u32[]{:S(2)}) %collective-permute-start.1) | collective-permute-done | bytes 4128 | tf_op jit(solution)/shard_map/ppermute | solution.py:30
  61.0 0.6 copy-done.7
  61.6 4.2 %shard_map.84 = f32[4,256,256]{2,1,0:T(8,128)} custom-call(f32[4,256,256]{2,1,0:T(8,128)} %field_ref.1, f32[4,256,256]{2,1,0:T(8,128)} %copy-done.1, f32[4,256]{1,0:T(4,128)} %copy-done.6, f32[4,256]{1,0:T(4,128)} %copy-done.7, f32[4,256]{1,0:T(4,128)} %copy-done.4, f32[4,256]{1,0:T(4,128)} %copy-done.5), custom_call_target="tpu_custom_call" | custom-call | tf_op jit(solution)/shard_map/pallas_call | solution.py:75
  (29 shorter events, 0.1 us)
Async XLA Ops:
  0.0 6.8 %copy-start.8 = (s32[1,1,16,2]{2,3,1,0:T(2,128)S(1)}, s32[1,1,16,2]{2,3,1,0:T(2,128)}, u32[]{:S(2)}) copy-start(s32[1,1,16,2]{2,3,1,0:T(2,128)} %param.12) | copy-start | bytes 388
  0.0 6.8 %copy-start.3 = (f32[128,128]{1,0:T(8,128)S(1)}, f32[128,128]{1,0:T(8,128)}, u32[]{:S(2)}) copy-start(f32[128,128]{1,0:T(8,128)} %param.10) | copy-start | bytes 196612
  0.0 7.0 %copy-start = (f32[4,256,256]{2,1,0:T(8,128)S(1)}, f32[4,256,256]{2,1,0:T(8,128)}, u32[]{:S(2)}) copy-start(f32[4,256,256]{2,1,0:T(8,128)} %field_ref.1) | copy-start | bytes 3145732
  0.0 23.7 %all-to-all-start = ((bf16[16,2,128,128]{3,2,1,0:T(8,128)(2,1)}), bf16[16,2,128,128]{3,2,1,0:T(8,128)(2,1)S(1)}, u32[]{:S(2)}, u32[]{:S(2)}) async-start(bf16[16,2,128,128]{3,2,1,0:T(8,128)(2,1)} %bitcast.62), calls=%async_computation | async-start | bytes 2097152 | tf_op jit(solution)/shard_map/all_to_all | solution.py:263
  12.0 10.9 %copy-start.9 = (s32[1,1,16,1]{2,3,1,0:T(1,128)S(1)}, s32[1,1,16,1]{2,3,1,0:T(1,128)}, u32[]{:S(2)}) copy-start(s32[1,1,16,1]{2,3,1,0:T(1,128)} %param.13) | copy-start | bytes 196
  23.7 1.0 %copy-start.2 = (bf16[16,2,128,128]{3,2,1,0:T(8,128)(2,1)}, bf16[16,2,128,128]{3,2,1,0:T(8,128)(2,1)S(1)}, u32[]{:S(2)}) copy-start(bf16[16,2,128,128]{3,2,1,0:T(8,128)(2,1)S(1)} %all-to-all-done) | copy-start | bytes 3145732
  42.7 18.2 %copy-start.1 = (f32[4,256,256]{2,1,0:T(8,128)}, f32[4,256,256]{2,1,0:T(8,128)S(1)}, u32[]{:S(2)}) copy-start(f32[4,256,256]{2,1,0:T(8,128)S(1)} %fusion.29.total_ref) | copy-start | bytes 3145732
  43.2 14.8 %collective-permute-start.2 = (f32[4,256]{1,0:T(4,128)S(1)}, f32[4,256]{1,0:T(4,128)S(1)}, u32[]{:S(2)}, u32[]{:S(2)}) collective-permute-start(f32[4,256]{1,0:T(4,128)S(1)} %subtract_bitcast_fusion.1), channel_id=1, source_target_pairs={{0,1},{1,2},{2,3},{3,4},{4,5},{5,6},{6,7},{7,8},{8,9},{9,10},{10,1... | collective-permute-start | bytes 12296 | tf_op jit(solution)/shard_map/ppermute | solution.py:31
  46.5 11.5 %collective-permute-start.3 = (f32[4,256]{1,0:T(4,128)S(1)}, f32[4,256]{1,0:T(4,128)S(1)}, u32[]{:S(2)}, u32[]{:S(2)}) collective-permute-start(f32[4,256]{1,0:T(4,128)S(1)} %subtract_bitcast_fusion), channel_id=1, source_target_pairs={{1,0},{2,1},{3,2},{4,3},{5,4},{6,5},{7,6},{8,7},{9,8},{10,9},{11,1... | collective-permute-start | bytes 12296 | tf_op jit(solution)/shard_map/ppermute | solution.py:32
  50.8 7.2 %collective-permute-start = (f32[4,256]{1,0:T(4,128)S(1)}, f32[4,256]{1,0:T(4,128)S(1)}, u32[]{:S(2)}, u32[]{:S(2)}) collective-permute-start(f32[4,256]{1,0:T(4,128)S(1)} %fusion.52), channel_id=1, source_target_pairs={{0,16},{16,32},{32,48},{48,64},{64,80},{80,96},{96,112},{1,17},{17... | collective-permute-start | bytes 12296 | tf_op jit(solution)/shard_map/ppermute | solution.py:29
  56.0 4.9 %collective-permute-start.1 = (f32[4,256]{1,0:T(4,128)S(1)}, f32[4,256]{1,0:T(4,128)S(1)}, u32[]{:S(2)}, u32[]{:S(2)}) collective-permute-start(f32[4,256]{1,0:T(4,128)S(1)} %fusion.50), channel_id=1, source_target_pairs={{16,0},{32,16},{48,32},{64,48},{80,64},{96,80},{112,96},{17,1},{33... | collective-permute-start | bytes 12296 | tf_op jit(solution)/shard_map/ppermute | solution.py:30
  58.0 3.0 %copy-start.4 = (f32[4,256]{1,0:T(4,128)}, f32[4,256]{1,0:T(4,128)S(1)}, u32[]{:S(2)}) copy-start(f32[4,256]{1,0:T(4,128)S(1)} %collective-permute-done.2.left_ref) | copy-start | bytes 12292
  58.0 3.0 %copy-start.5 = (f32[4,256]{1,0:T(4,128)}, f32[4,256]{1,0:T(4,128)S(1)}, u32[]{:S(2)}) copy-start(f32[4,256]{1,0:T(4,128)S(1)} %collective-permute-done.3.right_ref) | copy-start | bytes 12292
  58.0 3.0 %copy-start.6 = (f32[4,256]{1,0:T(4,128)}, f32[4,256]{1,0:T(4,128)S(1)}, u32[]{:S(2)}) copy-start(f32[4,256]{1,0:T(4,128)S(1)} %collective-permute-done.above_ref) | copy-start | bytes 12292
  61.0 0.6 copy-start.7

commit v6 on v5

--- a/solution.py
+++ b/solution.py
@@ -33,52 +33,86 @@
     return above, below, left, right
 
 
-def _smooth_kernel(field_ref, total_ref, above_ref, below_ref, left_ref, right_ref, out_ref):
+def _bend(real, imag):
+    weight = 1.0 / jnp.sqrt(1.0 + real * real + imag * imag)
+    return real * weight, imag * weight
+
+
+def _inner_kernel(field_ref, total_ref, out_ref):
     size = field_ref.shape[-1]
     rows = lax.broadcasted_iota(jnp.int32, (size, size), 0)
     cols = lax.broadcasted_iota(jnp.int32, (size, size), 1)
-
-    def as_column(line):
-        return jnp.sum(jnp.where(rows == cols, line, 0.0), axis=1, keepdims=True)
-
-    centers, views = [], []
-    for part in range(2):
-        v = field_ref[part] - step_rate * total_ref[part]
-        channel = 2 * pl.program_id(0) + part
-        above = above_ref[pl.ds(channel, 1), :]
-        below = below_ref[pl.ds(channel, 1), :]
-        left = as_column(left_ref[pl.ds(channel, 1), :])
-        right = as_column(right_ref[pl.ds(channel, 1), :])
-        south = jnp.where(rows == size - 1, below, pltpu.roll(v, size - 1, 0))
-        north = jnp.where(rows == 0, above, pltpu.roll(v, 1, 0))
-        east = jnp.where(cols == size - 1, right, pltpu.roll(v, size - 1, 1))
-        west = jnp.where(cols == 0, left, pltpu.roll(v, 1, 1))
-        centers.append(v)
-        views.append((south, north, east, west))
+    centers = [field_ref[p] - step_rate * total_ref[p] for p in range(2)]
+    views = []
+    for v in centers:
+        views.append((
+            jnp.where(rows == size - 1, v, pltpu.roll(v, size - 1, 0)),
+            jnp.where(rows == 0, v, pltpu.roll(v, 1, 0)),
+            jnp.where(cols == size - 1, v, pltpu.roll(v, size - 1, 1)),
+            jnp.where(cols == 0, v, pltpu.roll(v, 1, 1)),
+        ))
     total_r = jnp.zeros_like(centers[0])
     total_i = jnp.zeros_like(centers[1])
     for n in range(4):
-        dr = views[0][n] - centers[0]
-        di = views[1][n] - centers[1]
-        weight = 1.0 / jnp.sqrt(1.0 + dr * dr + di * di)
-        total_r = total_r + dr * weight
-        total_i = total_i + di * weight
+        bent = _bend(views[0][n] - centers[0], views[1][n] - centers[1])
+        total_r = total_r + bent[0]
+        total_i = total_i + bent[1]
     out_ref[0] = centers[0] + smooth_rate * total_r
     out_ref[1] = centers[1] + smooth_rate * total_i
 
 
-def smooth_update(field, total, above, below, left, right):
+def _edge_kernel(inner_ref, top_ref, bottom_ref, first_ref, last_ref,
+                 above_ref, below_ref, left_ref, right_ref, out_ref):
+    size, lanes = inner_ref.shape[1], inner_ref.shape[2]
+    block = pl.program_id(0)
+    rows = lax.broadcasted_iota(jnp.int32, (size, lanes), 0)
+    cols = lax.broadcasted_iota(jnp.int32, (size, lanes), 1)
+    square = lax.broadcasted_iota(jnp.int32, (size, size), 0) == lax.broadcasted_iota(
+        jnp.int32, (size, size), 1)
+
+    def as_column(line):
+        return jnp.sum(jnp.where(square, line, 0.0), axis=1, keepdims=True)
+
+    edge_col = jnp.where(block == 0, 0, lanes - 1)
+    for s in range(inner_ref.shape[0] // 2):
+        c0, c1 = 2 * s, 2 * s + 1
+        north = _bend(above_ref[c0:c0 + 1] - top_ref[c0:c0 + 1], above_ref[c1:c1 + 1] - top_ref[c1:c1 + 1])
+        south = _bend(below_ref[c0:c0 + 1] - bottom_ref[c0:c0 + 1],
+                      below_ref[c1:c1 + 1] - bottom_ref[c1:c1 + 1])
+        west = _bend(left_ref[c0:c0 + 1] - first_ref[c0:c0 + 1], left_ref[c1:c1 + 1] - first_ref[c1:c1 + 1])
+        east = _bend(right_ref[c0:c0 + 1] - last_ref[c0:c0 + 1], right_ref[c1:c1 + 1] - last_ref[c1:c1 + 1])
+        for part, c in ((0, c0), (1, c1)):
+            side = as_column(jnp.where(block == 0, west[part], east[part]))
+            extra = (
+                jnp.where(rows == 0, north[part], 0.0)
+                + jnp.where(rows == size - 1, south[part], 0.0)
+                + jnp.where(cols == edge_col, side, 0.0)
+            )
+            out_ref[c] = inner_ref[c] + smooth_rate * extra
+
+
+def smooth_update(field, total, edges, halos):
     channels, size, _ = field.shape
-    slices = channels // 2
     plane = pl.BlockSpec((2, size, size), lambda s: (s, 0, 0))
-    edge = pl.BlockSpec((channels, size), lambda s: (0, 0))
-    return pl.pallas_call(
-        _smooth_kernel,
-        grid=(slices,),
-        in_specs=[plane, plane, edge, edge, edge, edge],
+    inner = pl.pallas_call(
+        _inner_kernel,
+        grid=(channels // 2,),
+        in_specs=[plane, plane],
         out_specs=plane,
         out_shape=jax.ShapeDtypeStruct(field.shape, jnp.float32),
-    )(field, total, above, below, left, right)
+    )(field, total)
+    lanes = 128
+    half = pl.BlockSpec((channels, size, lanes), lambda b: (0, 0, b))
+    row_part = pl.BlockSpec((channels, lanes), lambda b: (0, b))
+    whole = pl.BlockSpec((channels, size), lambda b: (0, 0))
+    return pl.pallas_call(
+        _edge_kernel,
+        grid=(size // lanes,),
+        in_specs=[half, row_part, row_part, whole, whole, row_part, row_part, whole, whole],
+        out_specs=half,
+        out_shape=jax.ShapeDtypeStruct(field.shape, jnp.float32),
+        input_output_aliases={0: 0},
+    )(inner, *edges, *halos)
 
 
 def block_tables(width):
@@ -285,13 +319,14 @@
         "kir,kcij->kcrj", row_pick, grads, preferred_element_type=jnp.float32
     ).astype(jnp.bfloat16)
     total = jnp.einsum("kcrj,ksj->crs", placed_rows, col_pick, preferred_element_type=jnp.float32)
-    halos = exchange_edges(
+    edges = (
         field[:, 0, :] - step_rate * total[:, 0, :],
         field[:, -1, :] - step_rate * total[:, -1, :],
         field[:, :, 0] - step_rate * total[:, :, 0],
         field[:, :, -1] - step_rate * total[:, :, -1],
     )
-    return smooth_update(field, total, *halos)
+    halos = exchange_edges(*edges)
+    return smooth_update(field, total, edges, halos)
 
 
 def solution(mesh):

time: 66.3 us -> 66 us (level)
  waiting for transfers between devices: 2.95 us -> 0.01 us
  Pallas kernels: 28.6 us -> 30.7 us
    ppermute x1, waiting for transfers between devices: 2.94 us -> 0.01 us  [exchange_edges(): below = lax.ppermute(top, 'tx', down_rows)]
    pallas_call x1 -> x2, Pallas kernels: 4.19 us -> 6.3 us  [the longest x1 3.93 us: smooth_update(): pl.pallas_call(_inner_kernel, grid=(channels // 2,), in_specs=[plane, pla...]
    unnamed x24 -> x32, local copies, waits for them, and re-layouts: 2.32 us -> 2.87 us
  transfers between devices with their start and end apart: 5 -> 5, of which waited for: 1 -> 0; matrix products, arithmetic and copies ran while one was open for 9% -> 9% of each run, Pallas kernels for 17% -> 23%
where the time goes in v6:
time: 66 us; the launch traced here: 65.4 us
  Pallas kernels  30.7 us (47%)
  starting transfers between devices  21.3 us (32%)
  matrix products  8.18 us (12%)
  local copies, waits for them, and re-layouts  3.54 us (5%)
  other arithmetic  1.47 us (2%)
    pallas_call x1, Pallas kernels, backward_gradients(): pl.pallas_call(_backward_kernel, grid_spec=grid_spec, out_shape=jax.Shape...  13.5 us
    pallas_call x1, Pallas kernels, forward_waves(): pl.pallas_call(_forward_kernel, grid=(count // group,), in_specs=[pl.Bloc...  10.9 us
    all_to_all x1, starting transfers between devices, per_device(): lax.all_to_all(measured[0, 0], 'ty', split_axis=0, concat_axis=0, tiled=T...  6.75 us
    ppermute x1, starting transfers between devices, exchange_edges(): above = lax.ppermute(bottom, 'tx', up_rows)  5.23 us
    dot_general x1, matrix products, per_device(): jnp.einsum('kcrj,ksj->crs', placed_rows, col_pick, preferred_element_type...  4.57 us
    ppermute x1, starting transfers between devices, exchange_edges(): right = lax.ppermute(first, 'ty', down_cols)  4.31 us
    pallas_call x1, Pallas kernels, smooth_update(): pl.pallas_call(_inner_kernel, grid=(channels // 2,), in_specs=[plane, pla...  3.93 us
    dot_general x1, matrix products, per_device(): jnp.einsum('kcis,ksj->kcij', rows, col_pick, preferred_element_type=jnp.f...  3.61 us
  transfers between devices with their start and end apart: 5, of which 0 were waited for; matrix products, arithmetic and copies ran while one was open for 9% of the time, Pallas kernels for 23%

profile of v6, /device:TPU:25, one launch (start us, length us, event | category | flops | bytes accessed | tf_op | source)
XLA Modules:
  0.0 65.4 jit_solution(7782134579969496061)
XLA Ops:
  0.0 6.8 %all-to-all-start = ((bf16[16,2,128,128]{3,2,1,0:T(8,128)(2,1)}), bf16[16,2,128,128]{3,2,1,0:T(8,128)(2,1)S(1)}, u32[]{:S(2)}, u32[]{:S(2)}) async-start(bf16[16,2,128,128]{3,2,1,0:T(8,128)(2,1)} %bitcast.62), calls=%async_computation | async-start | bytes 2097152 | tf_op jit(solution)/shard_map/all_to_all | solution.py:297
  6.8 0.2 cosine_bitcast_fusion
  7.0 0.2 fusion.54
  7.2 0.2 copy.36
  7.4 0.2 copy.34
  7.7 0.7 %pad_maximum_fusion.prop_ref = f32[2,128,128]{2,1,0:T(8,128)} fusion(f32[1,128,128]{2,1,0:T(8,128)S(1)} %get-tuple-element.18, f32[1,128,128]{2,1,0:T(8,128)S(1)} %get-tuple-element.17), kind=kLoop, calls=%fused_computation.23 | loop fusion | flops 32768 | bytes 262144 | tf_op jit(solution)/shard_map/stack | solution.py:315
  8.4 3.6 %fusion.22.win_ref = bf16[16,4,128,128]{3,2,1,0:T(8,128)(2,1)} fusion(s32[16,128]{1,0:T(8,128)S(1)} %get-tuple-element.21, s32[16,128]{1,0:T(8,128)S(1)} %get-tuple-element.22, f32[4,256,256]{2,1,0:T(8,128)S(1)} %copy-done), kind=kOutput, calls=%fused_computation.15 | convolution fusion | flops 1615069184 | bytes 3162112 | tf_op jit(solution)/shard_map/kcis,ksj->kcij/dot_general | solution.py:311
  12.0 10.9 %shard_map.82 = (f32[16,2,128,128]{3,2,1,0:T(8,128)}, f32[16,2,128,128]{3,2,1,0:T(8,128)}) custom-call(bf16[16,4,128,128]{3,2,1,0:T(8,128)(2,1)} %fusion.22.win_ref, f32[2,128,128]{2,1,0:T(8,128)} %probe_ref.3, f32[2,128,128]{2,1,0:T(8,128)} %pad_maximum_fusion.prop_ref, bf16[2,256,768]{2,1,0:T(8,128)(2,1)} %constant.14.clone.left_ref, ...), custom_call_target="tpu_custom_call" | custom-call | tf_op jit(solution)/shard_map/pallas_call | solution.py:237
  22.9 0.2 select_reduce_fusion
  23.1 0.5 add_clamp_fusion.target_ref
  23.6 1.0 %copy-done.2 = bf16[16,2,128,128]{3,2,1,0:T(8,128)(2,1)} copy-done((bf16[16,2,128,128]{3,2,1,0:T(8,128)(2,1)}, bf16[16,2,128,128]{3,2,1,0:T(8,128)(2,1)S(1)}, u32[]{:S(2)}) %copy-start.2) | copy-done | bytes 1048600
  24.6 13.5 %shard_map.83 = bf16[16,4,128,128]{3,2,1,0:T(8,128)(2,1)} custom-call(s32[16]{0:T(128)} %add_clamp_fusion.target_ref, bf16[32,128,128]{2,1,0:T(8,128)(2,1)} %bitcast.61, f32[16,2,128,128]{3,2,1,0:T(8,128)} %get-tuple-element.7.far_ref, f32[16,2,128,128]{3,2,1,0:T(8,128)} %get-tuple-element.8.inc_ref, bf16[16,4,128,128]{3,2,1,0:T(8,128)(2,1)} %fusion.22.win_ref, ...), custom_call_target="tpu_custom_call" | custom-call | tf_op jit(solution)/shard_map/pallas_call | solution.py:279
  38.1 4.6 %fusion.29.total_ref = f32[4,256,256]{2,1,0:T(8,128)S(1)} fusion(bf16[16,4,128,128]{3,2,1,0:T(8,128)(2,1)} %shard_map.83, s32[16,128]{1,0:T(8,128)S(1)} %get-tuple-element.21, s32[16,128]{1,0:T(8,128)S(1)} %get-tuple-element.22), kind=kOutput, calls=%fused_computation.16 | convolution fusion | flops 1613758464 | bytes 3162112 | tf_op jit(solution)/shard_map/kcrj,ksj->crs/dot_general | solution.py:321
  42.7 0.2 fusion.53
  42.9 0.2 copy.37
  43.1 3.1 %collective-permute-start.2 = (f32[4,256]{1,0:T(4,128)S(1)}, f32[4,256]{1,0:T(4,128)S(1)}, u32[]{:S(2)}, u32[]{:S(2)}) collective-permute-start(f32[4,256]{1,0:T(4,128)S(1)} %subtract_bitcast_fusion.last_ref), channel_id=1, source_target_pairs={{0,1},{1,2},{2,3},{3,4},{4,5},{5,6},{6,7},{7,8},{8,9},{9,10},{10,1... | collective-permute-start | bytes 12296 | tf_op jit(solution)/shard_map/ppermute | solution.py:31
  46.2 0.2 copy.35
  46.4 4.3 %collective-permute-start.3 = (f32[4,256]{1,0:T(4,128)S(1)}, f32[4,256]{1,0:T(4,128)S(1)}, u32[]{:S(2)}, u32[]{:S(2)}) collective-permute-start(f32[4,256]{1,0:T(4,128)S(1)} %subtract_bitcast_fusion.1.first_ref), channel_id=1, source_target_pairs={{1,0},{2,1},{3,2},{4,3},{5,4},{6,5},{7,6},{8,7},{9,8},{10,9},{11,1... | collective-permute-start | bytes 12296 | tf_op jit(solution)/shard_map/ppermute | solution.py:32
  50.7 5.2 %collective-permute-start = (f32[4,256]{1,0:T(4,128)S(1)}, f32[4,256]{1,0:T(4,128)S(1)}, u32[]{:S(2)}, u32[]{:S(2)}) collective-permute-start(f32[4,256]{1,0:T(4,128)S(1)} %fusion.50.bottom_ref), channel_id=1, source_target_pairs={{0,16},{16,32},{32,48},{48,64},{64,80},{80,96},{96,112},{1,17},{17... | collective-permute-start | bytes 12296 | tf_op jit(solution)/shard_map/ppermute | solution.py:29
  56.0 1.9 %collective-permute-start.1 = (f32[4,256]{1,0:T(4,128)S(1)}, f32[4,256]{1,0:T(4,128)S(1)}, u32[]{:S(2)}, u32[]{:S(2)}) collective-permute-start(f32[4,256]{1,0:T(4,128)S(1)} %fusion.52.top_ref), channel_id=1, source_target_pairs={{16,0},{32,16},{48,32},{64,48},{80,64},{96,80},{112,96},{17,1},{33... | collective-permute-start | bytes 12296 | tf_op jit(solution)/shard_map/ppermute | solution.py:30
  57.9 3.9 %shard_map.84.inner_ref = f32[4,256,256]{2,1,0:T(8,128)} custom-call(f32[4,256,256]{2,1,0:T(8,128)} %field_ref.1, f32[4,256,256]{2,1,0:T(8,128)} %copy-done.1), custom_call_target="tpu_custom_call" | custom-call | tf_op jit(solution)/shard_map/pallas_call | solution.py:97
  61.9 0.5 copy-done.8
  62.5 0.6 copy-done.11
  63.1 2.4 %shard_map.85 = f32[4,256,256]{2,1,0:T(8,128)} custom-call(f32[4,256,256]{2,1,0:T(8,128)} %shard_map.84.inner_ref, f32[4,256]{1,0:T(4,128)} %copy-done.7, f32[4,256]{1,0:T(4,128)} %copy-done.6, f32[4,256]{1,0:T(4,128)} %copy-done.5, f32[4,256]{1,0:T(4,128)} %copy-done.4, f32[4,256]{1,0:T(4,128)} %copy-done.10, ...), custom_call_target="tpu_custom_call", output_to_operand_aliasing={{}: (0, {})} | custom-call | tf_op jit(solution)/shard_map/pallas_call | solution.py:108
  (38 shorter events, 0.2 us)
Async XLA Ops:
  0.0 6.8 %copy-start.12 = (s32[1,1,16,2]{2,3,1,0:T(2,128)S(1)}, s32[1,1,16,2]{2,3,1,0:T(2,128)}, u32[]{:S(2)}) copy-start(s32[1,1,16,2]{2,3,1,0:T(2,128)} %param.12) | copy-start | bytes 388
  0.0 6.8 %copy-start.3 = (f32[128,128]{1,0:T(8,128)S(1)}, f32[128,128]{1,0:T(8,128)}, u32[]{:S(2)}) copy-start(f32[128,128]{1,0:T(8,128)} %param.10) | copy-start | bytes 196612
  0.0 7.0 %copy-start = (f32[4,256,256]{2,1,0:T(8,128)S(1)}, f32[4,256,256]{2,1,0:T(8,128)}, u32[]{:S(2)}) copy-start(f32[4,256,256]{2,1,0:T(8,128)} %field_ref.1) | copy-start | bytes 3145732
  0.0 23.6 %all-to-all-start = ((bf16[16,2,128,128]{3,2,1,0:T(8,128)(2,1)}), bf16[16,2,128,128]{3,2,1,0:T(8,128)(2,1)S(1)}, u32[]{:S(2)}, u32[]{:S(2)}) async-start(bf16[16,2,128,128]{3,2,1,0:T(8,128)(2,1)} %bitcast.62), calls=%async_computation | async-start | bytes 2097152 | tf_op jit(solution)/shard_map/all_to_all | solution.py:297
  12.0 10.9 %copy-start.13 = (s32[1,1,16,1]{2,3,1,0:T(1,128)S(1)}, s32[1,1,16,1]{2,3,1,0:T(1,128)}, u32[]{:S(2)}) copy-start(s32[1,1,16,1]{2,3,1,0:T(1,128)} %param.13) | copy-start | bytes 196
  23.6 1.0 %copy-start.2 = (bf16[16,2,128,128]{3,2,1,0:T(8,128)(2,1)}, bf16[16,2,128,128]{3,2,1,0:T(8,128)(2,1)S(1)}, u32[]{:S(2)}) copy-start(bf16[16,2,128,128]{3,2,1,0:T(8,128)(2,1)S(1)} %all-to-all-done) | copy-start | bytes 3145732
  42.7 15.2 %copy-start.1 = (f32[4,256,256]{2,1,0:T(8,128)}, f32[4,256,256]{2,1,0:T(8,128)S(1)}, u32[]{:S(2)}) copy-start(f32[4,256,256]{2,1,0:T(8,128)S(1)} %fusion.29.total_ref) | copy-start | bytes 3145732
  43.1 18.8 %copy-start.4 = (f32[4,256]{1,0:T(4,128)}, f32[4,256]{1,0:T(4,128)S(1)}, u32[]{:S(2)}) copy-start(f32[4,256]{1,0:T(4,128)S(1)} %subtract_bitcast_fusion.last_ref) | copy-start | bytes 12292
  43.1 18.8 %collective-permute-start.2 = (f32[4,256]{1,0:T(4,128)S(1)}, f32[4,256]{1,0:T(4,128)S(1)}, u32[]{:S(2)}, u32[]{:S(2)}) collective-permute-start(f32[4,256]{1,0:T(4,128)S(1)} %subtract_bitcast_fusion.last_ref), channel_id=1, source_target_pairs={{0,1},{1,2},{2,3},{3,4},{4,5},{5,6},{6,7},{7,8},{8,9},{9,10},{10,1... | collective-permute-start | bytes 12296 | tf_op jit(solution)/shard_map/ppermute | solution.py:31
  46.4 15.5 %copy-start.5 = (f32[4,256]{1,0:T(4,128)}, f32[4,256]{1,0:T(4,128)S(1)}, u32[]{:S(2)}) copy-start(f32[4,256]{1,0:T(4,128)S(1)} %subtract_bitcast_fusion.1.first_ref) | copy-start | bytes 12292
  46.4 15.5 %collective-permute-start.3 = (f32[4,256]{1,0:T(4,128)S(1)}, f32[4,256]{1,0:T(4,128)S(1)}, u32[]{:S(2)}, u32[]{:S(2)}) collective-permute-start(f32[4,256]{1,0:T(4,128)S(1)} %subtract_bitcast_fusion.1.first_ref), channel_id=1, source_target_pairs={{1,0},{2,1},{3,2},{4,3},{5,4},{6,5},{7,6},{8,7},{9,8},{10,9},{11,1... | collective-permute-start | bytes 12296 | tf_op jit(solution)/shard_map/ppermute | solution.py:32
  50.7 11.2 %copy-start.6 = (f32[4,256]{1,0:T(4,128)}, f32[4,256]{1,0:T(4,128)S(1)}, u32[]{:S(2)}) copy-start(f32[4,256]{1,0:T(4,128)S(1)} %fusion.50.bottom_ref) | copy-start | bytes 12292
  50.7 11.2 %collective-permute-start = (f32[4,256]{1,0:T(4,128)S(1)}, f32[4,256]{1,0:T(4,128)S(1)}, u32[]{:S(2)}, u32[]{:S(2)}) collective-permute-start(f32[4,256]{1,0:T(4,128)S(1)} %fusion.50.bottom_ref), channel_id=1, source_target_pairs={{0,16},{16,32},{32,48},{48,64},{64,80},{80,96},{96,112},{1,17},{17... | collective-permute-start | bytes 12296 | tf_op jit(solution)/shard_map/ppermute | solution.py:29
  56.0 6.0 %copy-start.7 = (f32[4,256]{1,0:T(4,128)}, f32[4,256]{1,0:T(4,128)S(1)}, u32[]{:S(2)}) copy-start(f32[4,256]{1,0:T(4,128)S(1)} %fusion.52.top_ref) | copy-start | bytes 12292
  56.0 5.9 %collective-permute-start.1 = (f32[4,256]{1,0:T(4,128)S(1)}, f32[4,256]{1,0:T(4,128)S(1)}, u32[]{:S(2)}, u32[]{:S(2)}) collective-permute-start(f32[4,256]{1,0:T(4,128)S(1)} %fusion.52.top_ref), channel_id=1, source_target_pairs={{16,0},{32,16},{48,32},{64,48},{80,64},{96,80},{112,96},{17,1},{33... | collective-permute-start | bytes 12296 | tf_op jit(solution)/shard_map/ppermute | solution.py:30
  61.8 0.6 copy-start.8
  61.8 0.6 copy-start.9
  61.9 0.6 copy-start.10
  62.5 0.6 copy-start.11

commit v7 on v6

--- a/solution.py
+++ b/solution.py
@@ -203,7 +203,8 @@
 
 
 def _backward_kernel(
-    target_ref, amp_ref, far_ref, inc_ref, win_ref, probe_ref, prop_ref, left_ref, right_ref, out_ref
+    target_ref, tops_ref, lefts_ref, amp_ref, far_ref, inc_ref, win_ref, probe_ref, prop_ref,
+    left_ref, right_ref, out_ref
 ):
     group, width = win_ref.shape[0], probe_ref.shape[-1]
     step = pl.program_id(0)
@@ -224,9 +225,34 @@
         grads[s] = _conj_times((inc_ref[:, 2 * (s - 1)], inc_ref[:, 2 * (s - 1) + 1]), back)
         back = transform(_times(kernel_conj, transform(_conj_times(layers[s], back), -1)), 1)
     grads[0] = _conj_times(probe, back)
-    for s in range(slices):
-        out_ref[:, 2 * s] = grads[s][0].astype(out_ref.dtype)
-        out_ref[:, 2 * s + 1] = grads[s][1].astype(out_ref.dtype)
+    planes = [part.astype(jnp.bfloat16) for pair in grads for part in pair]
+    channels, tile = out_ref.shape[0], out_ref.shape[-1]
+    down = lax.broadcasted_iota(jnp.int32, (tile, width), 0) - lax.broadcasted_iota(
+        jnp.int32, (tile, width), 1)
+    across = lax.broadcasted_iota(jnp.int32, (width, tile), 1) - lax.broadcasted_iota(
+        jnp.int32, (width, tile), 0)
+    placed, col_picks = [], []
+    for g in range(group):
+        top = tops_ref[step * group + g]
+        left = lefts_ref[step * group + g]
+        row_pick = (down == top).astype(jnp.bfloat16)
+        col_picks.append((across == left).astype(jnp.bfloat16))
+        stacked = jnp.concatenate([plane[g] for plane in planes], axis=1)
+        placed.append(_dot(row_pick, stacked).astype(jnp.bfloat16))
+    spread = jnp.concatenate(
+        [
+            jnp.concatenate([rows[:, c * width:(c + 1) * width] for rows in placed], axis=1)
+            for c in range(channels)
+        ],
+        axis=0,
+    )
+    contribution = _dot(spread, jnp.concatenate(col_picks, axis=0)).reshape(channels, tile, tile)
+
+    @pl.when(step == 0)
+    def _():
+        out_ref[...] = jnp.zeros_like(out_ref)
+
+    out_ref[...] += contribution
 
 
 def forward_waves(windows, probe, kernel, tables, group=8):
@@ -255,14 +281,15 @@
     )(windows, probe, kernel, left_tables, right_tables)
 
 
-def backward_gradients(target, amplitudes, far, incoming, windows, probe, kernel, tables, group=8):
+def backward_gradients(target, tops, lefts, amplitudes, far, incoming, windows, probe, kernel,
+                       tables, tile, group=8):
     count, channels, width, _ = windows.shape
     group = math.gcd(count, group)
     left_tables, right_tables = tables
-    fixed = lambda k, t: (0, 0, 0)
-    batch = lambda k, t: (k, 0, 0, 0)
+    fixed = lambda k, *_: (0, 0, 0)
+    batch = lambda k, *_: (k, 0, 0, 0)
     grid_spec = pltpu.PrefetchScalarGridSpec(
-        num_scalar_prefetch=1,
+        num_scalar_prefetch=3,
         grid=(count // group,),
         in_specs=[
             pl.BlockSpec(amplitudes.shape, fixed),
@@ -274,13 +301,14 @@
             pl.BlockSpec(left_tables.shape, fixed),
             pl.BlockSpec(right_tables.shape, fixed),
         ],
-        out_specs=pl.BlockSpec((group, channels, width, width), batch),
+        out_specs=pl.BlockSpec((channels, tile, tile), fixed),
     )
     return pl.pallas_call(
         _backward_kernel,
         grid_spec=grid_spec,
-        out_shape=jax.ShapeDtypeStruct((count, channels, width, width), jnp.bfloat16),
-    )(target, amplitudes, far, incoming, windows, probe, kernel, left_tables, right_tables)
+        out_shape=jax.ShapeDtypeStruct((channels, tile, tile), jnp.float32),
+    )(target, tops, lefts, amplitudes, far, incoming, windows, probe, kernel, left_tables,
+      right_tables)
 
 
 def per_device(object_init, probe, propagator_phase, measured, corners, owner_column):
@@ -314,11 +342,9 @@
     tables = block_tables(width)
     kernel = jnp.stack([jnp.cos(propagator_phase), jnp.sin(propagator_phase)])
     far, incoming = forward_waves(windows, probe, kernel, tables)
-    grads = backward_gradients(target, gathered, far, incoming, windows, probe, kernel, tables)
-    placed_rows = jnp.einsum(
-        "kir,kcij->kcrj", row_pick, grads, preferred_element_type=jnp.float32
-    ).astype(jnp.bfloat16)
-    total = jnp.einsum("kcrj,ksj->crs", placed_rows, col_pick, preferred_element_type=jnp.float32)
+    total = backward_gradients(
+        target, tops, lefts, gathered, far, incoming, windows, probe, kernel, tables, tile
+    )
     edges = (
         field[:, 0, :] - step_rate * total[:, 0, :],
         field[:, -1, :] - step_rate * total[:, -1, :],

time: 66 us -> 66.5 us (level)
  matrix products: 8.18 us -> 3.61 us
  Pallas kernels: 30.7 us -> 33.6 us
  local copies, waits for them, and re-layouts: 3.54 us -> 5.51 us
    dot_general x1 -> x0, matrix products: 4.57 us -> none  [per_device(): jnp.einsum('kcrj,ksj->crs', placed_rows, col_pick, preferred_element_type...]
    pallas_call x1, Pallas kernels: 13.5 us -> 16.4 us  [backward_gradients(): pl.pallas_call(_backward_kernel, grid_spec=grid_spec, out_shape=jax.Shape...]
    slice x1, local copies, waits for them, and re-layouts: 0.2 us -> 1.4 us  [per_device(): total[:, :, -1]]
    slice x1, local copies, waits for them, and re-layouts: 0.01 us -> 0.79 us  [per_device(): total[:, -1, :]]
    unnamed x32 -> x34, local copies, waits for them, and re-layouts: 2.87 us -> 2.87 us
where the time goes in v7:
time: 66.5 us; the launch traced here: 65.8 us
  Pallas kernels  33.6 us (51%)
  starting transfers between devices  21.3 us (32%)
  local copies, waits for them, and re-layouts  5.51 us (8%)
  matrix products  3.61 us (5%)
  other arithmetic  1.54 us (2%)
    pallas_call x1, Pallas kernels, backward_gradients(): pl.pallas_call(_backward_kernel, grid_spec=grid_spec, out_shape=jax.Shape...  16.4 us
    pallas_call x1, Pallas kernels, forward_waves(): pl.pallas_call(_forward_kernel, grid=(count // group,), in_specs=[pl.Bloc...  10.9 us
    all_to_all x1, starting transfers between devices, per_device(): lax.all_to_all(measured[0, 0], 'ty', split_axis=0, concat_axis=0, tiled=T...  6.75 us
    ppermute x1, starting transfers between devices, exchange_edges(): above = lax.ppermute(bottom, 'tx', up_rows)  5.23 us
    ppermute x1, starting transfers between devices, exchange_edges(): right = lax.ppermute(first, 'ty', down_cols)  4.3 us
    pallas_call x1, Pallas kernels, smooth_update(): pl.pallas_call(_inner_kernel, grid=(channels // 2,), in_specs=[plane, pla...  3.93 us
    dot_general x1, matrix products, per_device(): jnp.einsum('kcis,ksj->kcij', rows, col_pick, preferred_element_type=jnp.f...  3.61 us
    ppermute x1, starting transfers between devices, exchange_edges(): left = lax.ppermute(last, 'ty', up_cols)  3.09 us
  transfers between devices with their start and end apart: 5, of which 0 were waited for; matrix products, arithmetic and copies ran while one was open for 9% of the time, Pallas kernels for 23%

profile of v7, /device:TPU:25, one launch (start us, length us, event | category | flops | bytes accessed | tf_op | source)
XLA Modules:
  0.0 65.8 jit_solution(5662010970085176931)
XLA Ops:
  0.0 6.8 %all-to-all-start = ((bf16[16,2,128,128]{3,2,1,0:T(8,128)(2,1)}), bf16[16,2,128,128]{3,2,1,0:T(8,128)(2,1)S(1)}, u32[]{:S(2)}, u32[]{:S(2)}) async-start(bf16[16,2,128,128]{3,2,1,0:T(8,128)(2,1)} %bitcast.45), calls=%async_computation | async-start | bytes 2097152 | tf_op jit(solution)/shard_map/all_to_all | solution.py:325
  6.8 0.2 cosine_bitcast_fusion
  7.1 0.2 fusion.30
  7.3 0.2 copy.34
  7.5 0.2 copy.32
  7.7 0.7 %pad_maximum_fusion.prop_ref = f32[2,128,128]{2,1,0:T(8,128)} fusion(f32[1,128,128]{2,1,0:T(8,128)S(1)} %get-tuple-element.18, f32[1,128,128]{2,1,0:T(8,128)S(1)} %get-tuple-element.17), kind=kLoop, calls=%fused_computation.13 | loop fusion | flops 32768 | bytes 262144 | tf_op jit(solution)/shard_map/stack | solution.py:343
  8.4 3.6 %fusion.10.win_ref = bf16[16,4,128,128]{3,2,1,0:T(8,128)(2,1)} fusion(s32[16,128]{1,0:T(8,128)S(1)} %get-tuple-element.21, s32[16,128]{1,0:T(8,128)S(1)} %get-tuple-element.22, f32[4,256,256]{2,1,0:T(8,128)S(1)} %copy-done), kind=kOutput, calls=%fused_computation.8 | convolution fusion | flops 1615069184 | bytes 3162112 | tf_op jit(solution)/shard_map/kcis,ksj->kcij/dot_general | solution.py:339
  12.0 10.9 %shard_map.82 = (f32[16,2,128,128]{3,2,1,0:T(8,128)}, f32[16,2,128,128]{3,2,1,0:T(8,128)}) custom-call(bf16[16,4,128,128]{3,2,1,0:T(8,128)(2,1)} %fusion.10.win_ref, f32[2,128,128]{2,1,0:T(8,128)} %probe_ref.3, f32[2,128,128]{2,1,0:T(8,128)} %pad_maximum_fusion.prop_ref, bf16[2,256,768]{2,1,0:T(8,128)(2,1)} %constant.14.clone.left_ref, ...), custom_call_target="tpu_custom_call" | custom-call | tf_op jit(solution)/shard_map/pallas_call | solution.py:263
  22.9 0.2 select_reduce_fusion
  23.1 0.6 add_clamp_fusion.target_ref
  23.7 1.0 %copy-done.1 = bf16[16,2,128,128]{3,2,1,0:T(8,128)(2,1)} copy-done((bf16[16,2,128,128]{3,2,1,0:T(8,128)(2,1)}, bf16[16,2,128,128]{3,2,1,0:T(8,128)(2,1)S(1)}, u32[]{:S(2)}) %copy-start.1) | copy-done | bytes 1048600
  24.7 16.4 %shard_map.83.total_ref = f32[4,256,256]{2,1,0:T(8,128)} custom-call(s32[16]{0:T(128)} %add_clamp_fusion.target_ref, s32[16]{0:T(128)} %copy-done.8, s32[16]{0:T(128)} %copy-done.7, bf16[32,128,128]{2,1,0:T(8,128)(2,1)} %bitcast.44, f32[16,2,128,128]{3,2,1,0:T(8,128)} %get-tuple-element.7.far_ref, f32[16,2,128,128]{3,2,1,0:T(8,128)} %get-tuple-element.8.inc_ref, ...), custom_call_target="tpu_custom_call" | custom-call | tf_op jit(solution)/shard_map/pallas_call | solution.py:306
  41.1 1.4 %fusion.29 = (f32[4,256,1]{2,1,0:T(8,128)S(1)}, f32[4,256,1]{2,1,0:T(8,128)S(1)}) fusion(f32[4,256,256]{2,1,0:T(8,128)} %shard_map.83.total_ref), kind=kLoop, calls=%fused_computation.32 | loop fusion | bytes 16384 | tf_op jit(solution)/shard_map/slice | solution.py:352
  42.5 0.8 %fusion.32 = (f32[4,1,256]{2,1,0:T(1,128)S(1)}, f32[4,1,256]{2,1,0:T(1,128)S(1)}) fusion(f32[4,256,256]{2,1,0:T(8,128)} %shard_map.83.total_ref), kind=kLoop, calls=%fused_computation.35 | loop fusion | bytes 16384 | tf_op jit(solution)/shard_map/slice | solution.py:350
  43.3 0.2 copy.35
  43.5 3.1 %collective-permute-start.2 = (f32[4,256]{1,0:T(4,128)S(1)}, f32[4,256]{1,0:T(4,128)S(1)}, u32[]{:S(2)}, u32[]{:S(2)}) collective-permute-start(f32[4,256]{1,0:T(4,128)S(1)} %subtract_bitcast_fusion.last_ref), channel_id=1, source_target_pairs={{0,1},{1,2},{2,3},{3,4},{4,5},{5,6},{6,7},{7,8},{8,9},{9,10},{10,1... | collective-permute-start | bytes 12296 | tf_op jit(solution)/shard_map/ppermute | solution.py:31
  46.6 0.2 copy.33
  46.8 4.3 %collective-permute-start.3 = (f32[4,256]{1,0:T(4,128)S(1)}, f32[4,256]{1,0:T(4,128)S(1)}, u32[]{:S(2)}, u32[]{:S(2)}) collective-permute-start(f32[4,256]{1,0:T(4,128)S(1)} %subtract_bitcast_fusion.1.first_ref), channel_id=1, source_target_pairs={{1,0},{2,1},{3,2},{4,3},{5,4},{6,5},{7,6},{8,7},{9,8},{10,9},{11,1... | collective-permute-start | bytes 12296 | tf_op jit(solution)/shard_map/ppermute | solution.py:32
  51.1 5.2 %collective-permute-start = (f32[4,256]{1,0:T(4,128)S(1)}, f32[4,256]{1,0:T(4,128)S(1)}, u32[]{:S(2)}, u32[]{:S(2)}) collective-permute-start(f32[4,256]{1,0:T(4,128)S(1)} %fusion.26.bottom_ref), channel_id=1, source_target_pairs={{0,16},{16,32},{32,48},{48,64},{64,80},{80,96},{96,112},{1,17},{17... | collective-permute-start | bytes 12296 | tf_op jit(solution)/shard_map/ppermute | solution.py:29
  56.4 1.9 %collective-permute-start.1 = (f32[4,256]{1,0:T(4,128)S(1)}, f32[4,256]{1,0:T(4,128)S(1)}, u32[]{:S(2)}, u32[]{:S(2)}) collective-permute-start(f32[4,256]{1,0:T(4,128)S(1)} %fusion.28.top_ref), channel_id=1, source_target_pairs={{16,0},{32,16},{48,32},{64,48},{80,64},{96,80},{112,96},{17,1},{33... | collective-permute-start | bytes 12296 | tf_op jit(solution)/shard_map/ppermute | solution.py:30
  58.3 3.9 %shard_map.84.inner_ref = f32[4,256,256]{2,1,0:T(8,128)} custom-call(f32[4,256,256]{2,1,0:T(8,128)} %field_ref.1, f32[4,256,256]{2,1,0:T(8,128)} %shard_map.83.total_ref), custom_call_target="tpu_custom_call" | custom-call | tf_op jit(solution)/shard_map/pallas_call | solution.py:97
  62.3 0.5 copy-done.9
  62.9 0.6 copy-done.12
  63.4 2.4 %shard_map.85 = f32[4,256,256]{2,1,0:T(8,128)} custom-call(f32[4,256,256]{2,1,0:T(8,128)} %shard_map.84.inner_ref, f32[4,256]{1,0:T(4,128)} %copy-done.6, f32[4,256]{1,0:T(4,128)} %copy-done.5, f32[4,256]{1,0:T(4,128)} %copy-done.4, f32[4,256]{1,0:T(4,128)} %copy-done.3, f32[4,256]{1,0:T(4,128)} %copy-done.11, ...), custom_call_target="tpu_custom_call", output_to_operand_aliasing={{}: (0, {})} | custom-call | tf_op jit(solution)/shard_map/pallas_call | solution.py:108
  (39 shorter events, 0.2 us)
Async XLA Ops:
  0.0 6.8 %copy-start.13 = (s32[1,1,16,2]{2,3,1,0:T(2,128)S(1)}, s32[1,1,16,2]{2,3,1,0:T(2,128)}, u32[]{:S(2)}) copy-start(s32[1,1,16,2]{2,3,1,0:T(2,128)} %param.12) | copy-start | bytes 388
  0.0 6.8 %copy-start.2 = (f32[128,128]{1,0:T(8,128)S(1)}, f32[128,128]{1,0:T(8,128)}, u32[]{:S(2)}) copy-start(f32[128,128]{1,0:T(8,128)} %param.10) | copy-start | bytes 196612
  0.0 7.1 %copy-start = (f32[4,256,256]{2,1,0:T(8,128)S(1)}, f32[4,256,256]{2,1,0:T(8,128)}, u32[]{:S(2)}) copy-start(f32[4,256,256]{2,1,0:T(8,128)} %field_ref.1) | copy-start | bytes 3145732
  0.0 23.7 %all-to-all-start = ((bf16[16,2,128,128]{3,2,1,0:T(8,128)(2,1)}), bf16[16,2,128,128]{3,2,1,0:T(8,128)(2,1)S(1)}, u32[]{:S(2)}, u32[]{:S(2)}) async-start(bf16[16,2,128,128]{3,2,1,0:T(8,128)(2,1)} %bitcast.45), calls=%async_computation | async-start | bytes 2097152 | tf_op jit(solution)/shard_map/all_to_all | solution.py:325
  6.8 5.2 %copy-start.7 = (s32[16]{0:T(128)}, s32[16]{0:T(128)S(1)}, u32[]{:S(2)}) copy-start(s32[16]{0:T(128)S(1)} %get-tuple-element.19.lefts_ref) | copy-start | bytes 196
  6.8 5.2 %copy-start.8 = (s32[16]{0:T(128)}, s32[16]{0:T(128)S(1)}, u32[]{:S(2)}) copy-start(s32[16]{0:T(128)S(1)} %get-tuple-element.20.tops_ref) | copy-start | bytes 196
  12.0 10.9 %copy-start.14 = (s32[1,1,16,1]{2,3,1,0:T(1,128)S(1)}, s32[1,1,16,1]{2,3,1,0:T(1,128)}, u32[]{:S(2)}) copy-start(s32[1,1,16,1]{2,3,1,0:T(1,128)} %param.13) | copy-start | bytes 196
  23.7 1.0 %copy-start.1 = (bf16[16,2,128,128]{3,2,1,0:T(8,128)(2,1)}, bf16[16,2,128,128]{3,2,1,0:T(8,128)(2,1)S(1)}, u32[]{:S(2)}) copy-start(bf16[16,2,128,128]{3,2,1,0:T(8,128)(2,1)S(1)} %all-to-all-done) | copy-start | bytes 3145732
  43.5 18.8 %copy-start.3 = (f32[4,256]{1,0:T(4,128)}, f32[4,256]{1,0:T(4,128)S(1)}, u32[]{:S(2)}) copy-start(f32[4,256]{1,0:T(4,128)S(1)} %subtract_bitcast_fusion.last_ref) | copy-start | bytes 12292
  43.5 18.7 %collective-permute-start.2 = (f32[4,256]{1,0:T(4,128)S(1)}, f32[4,256]{1,0:T(4,128)S(1)}, u32[]{:S(2)}, u32[]{:S(2)}) collective-permute-start(f32[4,256]{1,0:T(4,128)S(1)} %subtract_bitcast_fusion.last_ref), channel_id=1, source_target_pairs={{0,1},{1,2},{2,3},{3,4},{4,5},{5,6},{6,7},{7,8},{8,9},{9,10},{10,1... | collective-permute-start | bytes 12296 | tf_op jit(solution)/shard_map/ppermute | solution.py:31
  46.8 15.5 %copy-start.4 = (f32[4,256]{1,0:T(4,128)}, f32[4,256]{1,0:T(4,128)S(1)}, u32[]{:S(2)}) copy-start(f32[4,256]{1,0:T(4,128)S(1)} %subtract_bitcast_fusion.1.first_ref) | copy-start | bytes 12292
  46.8 15.5 %collective-permute-start.3 = (f32[4,256]{1,0:T(4,128)S(1)}, f32[4,256]{1,0:T(4,128)S(1)}, u32[]{:S(2)}, u32[]{:S(2)}) collective-permute-start(f32[4,256]{1,0:T(4,128)S(1)} %subtract_bitcast_fusion.1.first_ref), channel_id=1, source_target_pairs={{1,0},{2,1},{3,2},{4,3},{5,4},{6,5},{7,6},{8,7},{9,8},{10,9},{11,1... | collective-permute-start | bytes 12296 | tf_op jit(solution)/shard_map/ppermute | solution.py:32
  51.1 11.2 %copy-start.5 = (f32[4,256]{1,0:T(4,128)}, f32[4,256]{1,0:T(4,128)S(1)}, u32[]{:S(2)}) copy-start(f32[4,256]{1,0:T(4,128)S(1)} %fusion.26.bottom_ref) | copy-start | bytes 12292
  51.1 11.1 %collective-permute-start = (f32[4,256]{1,0:T(4,128)S(1)}, f32[4,256]{1,0:T(4,128)S(1)}, u32[]{:S(2)}, u32[]{:S(2)}) collective-permute-start(f32[4,256]{1,0:T(4,128)S(1)} %fusion.26.bottom_ref), channel_id=1, source_target_pairs={{0,16},{16,32},{32,48},{48,64},{64,80},{80,96},{96,112},{1,17},{17... | collective-permute-start | bytes 12296 | tf_op jit(solution)/shard_map/ppermute | solution.py:29
  56.4 6.0 %copy-start.6 = (f32[4,256]{1,0:T(4,128)}, f32[4,256]{1,0:T(4,128)S(1)}, u32[]{:S(2)}) copy-start(f32[4,256]{1,0:T(4,128)S(1)} %fusion.28.top_ref) | copy-start | bytes 12292
  56.4 5.9 %collective-permute-start.1 = (f32[4,256]{1,0:T(4,128)S(1)}, f32[4,256]{1,0:T(4,128)S(1)}, u32[]{:S(2)}, u32[]{:S(2)}) collective-permute-start(f32[4,256]{1,0:T(4,128)S(1)} %fusion.28.top_ref), channel_id=1, source_target_pairs={{16,0},{32,16},{48,32},{64,48},{80,64},{96,80},{112,96},{17,1},{33... | collective-permute-start | bytes 12296 | tf_op jit(solution)/shard_map/ppermute | solution.py:30
  62.2 0.6 copy-start.9
  62.2 0.6 copy-start.10
  62.3 0.6 copy-start.11
  62.9 0.6 copy-start.12

commit v8 on v7

--- a/solution.py
+++ b/solution.py
@@ -67,11 +67,18 @@
     block = pl.program_id(0)
     rows = lax.broadcasted_iota(jnp.int32, (size, lanes), 0)
     cols = lax.broadcasted_iota(jnp.int32, (size, lanes), 1)
-    square = lax.broadcasted_iota(jnp.int32, (size, size), 0) == lax.broadcasted_iota(
-        jnp.int32, (size, size), 1)
+    square = lax.broadcasted_iota(jnp.int32, (lanes, lanes), 0) == lax.broadcasted_iota(
+        jnp.int32, (lanes, lanes), 1)
 
     def as_column(line):
-        return jnp.sum(jnp.where(square, line, 0.0), axis=1, keepdims=True)
+        return jnp.concatenate(
+            [
+                jnp.sum(jnp.where(square, line[:, h * lanes:(h + 1) * lanes], 0.0), axis=1,
+                        keepdims=True)
+                for h in range(size // lanes)
+            ],
+            axis=0,
+        )
 
     edge_col = jnp.where(block == 0, 0, lanes - 1)
     for s in range(inner_ref.shape[0] // 2):
@@ -204,7 +211,7 @@
 
 def _backward_kernel(
     target_ref, tops_ref, lefts_ref, amp_ref, far_ref, inc_ref, win_ref, probe_ref, prop_ref,
-    left_ref, right_ref, out_ref
+    left_ref, right_ref, out_ref, edges_ref
 ):
     group, width = win_ref.shape[0], probe_ref.shape[-1]
     step = pl.program_id(0)
@@ -254,6 +261,28 @@
 
     out_ref[...] += contribution
 
+    @pl.when(step == pl.num_programs(0) - 1)
+    def _():
+        lanes = lax.broadcasted_iota(jnp.int32, (8, tile), 1)
+        which = jnp.where(lax.broadcasted_iota(jnp.int32, (8, tile), 0) == 0, 0, tile - 1)
+        pick = (lanes == which).astype(jnp.bfloat16)
+        for c in range(channels):
+            plane = out_ref[c]
+            edges_ref[0, c:c + 1, :] = plane[0:1, :]
+            edges_ref[1, c:c + 1, :] = plane[tile - 1:tile, :]
+            high = plane.astype(jnp.bfloat16)
+            rest = plane - high.astype(jnp.float32)
+            middle = rest.astype(jnp.bfloat16)
+            low = (rest - middle.astype(jnp.float32)).astype(jnp.bfloat16)
+            cols = None
+            for part in (high, middle, low):
+                term = lax.dot_general(
+                    pick, part, (((1,), (1,)), ((), ())), preferred_element_type=jnp.float32
+                )
+                cols = term if cols is None else cols + term
+            edges_ref[2, c:c + 1, :] = cols[0:1]
+            edges_ref[3, c:c + 1, :] = cols[1:2]
+
 
 def forward_waves(windows, probe, kernel, tables, group=8):
     count, channels, width, _ = windows.shape
@@ -301,12 +330,18 @@
             pl.BlockSpec(left_tables.shape, fixed),
             pl.BlockSpec(right_tables.shape, fixed),
         ],
-        out_specs=pl.BlockSpec((channels, tile, tile), fixed),
+        out_specs=[
+            pl.BlockSpec((channels, tile, tile), fixed),
+            pl.BlockSpec((4, channels, tile), fixed),
+        ],
     )
     return pl.pallas_call(
         _backward_kernel,
         grid_spec=grid_spec,
-        out_shape=jax.ShapeDtypeStruct((channels, tile, tile), jnp.float32),
+        out_shape=[
+            jax.ShapeDtypeStruct((channels, tile, tile), jnp.float32),
+            jax.ShapeDtypeStruct((4, channels, tile), jnp.float32),
+        ],
     )(target, tops, lefts, amplitudes, far, incoming, windows, probe, kernel, left_tables,
       right_tables)
 
@@ -342,14 +377,14 @@
     tables = block_tables(width)
     kernel = jnp.stack([jnp.cos(propagator_phase), jnp.sin(propagator_phase)])
     far, incoming = forward_waves(windows, probe, kernel, tables)
-    total = backward_gradients(
+    total, total_edges = backward_gradients(
         target, tops, lefts, gathered, far, incoming, windows, probe, kernel, tables, tile
     )
     edges = (
-        field[:, 0, :] - step_rate * total[:, 0, :],
-        field[:, -1, :] - step_rate * total[:, -1, :],
-        field[:, :, 0] - step_rate * total[:, :, 0],
-        field[:, :, -1] - step_rate * total[:, :, -1],
+        field[:, 0, :] - step_rate * total_edges[0],
+        field[:, -1, :] - step_rate * total_edges[1],
+        field[:, :, 0] - step_rate * total_edges[2],
+        field[:, :, -1] - step_rate * total_edges[3],
     )
     halos = exchange_edges(*edges)
     return smooth_update(field, total, edges, halos)

time: 66.5 us -> 65 us (0.977)
  local copies, waits for them, and re-layouts: 5.51 us -> 2.96 us
  Pallas kernels: 33.6 us -> 34.6 us
  other arithmetic: 1.54 us -> 2.21 us
    slice x4 -> x2, local copies, waits for them, and re-layouts: 2.39 us -> 0.21 us  [the longest x1 0.2 us: per_device(): field[:, :, -1] - step_rate * total_edges[3]]
    sub x4 -> x1, other arithmetic: 0.03 us -> 0.7 us  [per_device(): field[:, :, -1] - step_rate * total_edges[3]]
    unnamed x34 -> x32, local copies, waits for them, and re-layouts: 2.87 us -> 2.5 us
where the time goes in v8:
time: 65 us; the launch traced here: 64.3 us
  Pallas kernels  34.6 us (53%)
  starting transfers between devices  20.7 us (32%)
  matrix products  3.61 us (6%)
  local copies, waits for them, and re-layouts  2.96 us (5%)
  other arithmetic  2.21 us (3%)
    pallas_call x1, Pallas kernels, backward_gradients(): pl.pallas_call(_backward_kernel, grid_spec=grid_spec, out_shape=[jax.Shap...  17 us
    pallas_call x1, Pallas kernels, forward_waves(): pl.pallas_call(_forward_kernel, grid=(count // group,), in_specs=[pl.Bloc...  10.9 us
    all_to_all x1, starting transfers between devices, per_device(): lax.all_to_all(measured[0, 0], 'ty', split_axis=0, concat_axis=0, tiled=T...  6.75 us
    ppermute x1, starting transfers between devices, exchange_edges(): above = lax.ppermute(bottom, 'tx', up_rows)  4.67 us
    ppermute x1, starting transfers between devices, exchange_edges(): right = lax.ppermute(first, 'ty', down_cols)  4.3 us
    pallas_call x1, Pallas kernels, smooth_update(): pl.pallas_call(_inner_kernel, grid=(channels // 2,), in_specs=[plane, pla...  3.93 us
    dot_general x1, matrix products, per_device(): jnp.einsum('kcis,ksj->kcij', rows, col_pick, preferred_element_type=jnp.f...  3.61 us
    ppermute x1, starting transfers between devices, exchange_edges(): left = lax.ppermute(last, 'ty', up_cols)  3.09 us
  transfers between devices with their start and end apart: 5, of which 0 were waited for; matrix products, arithmetic and copies ran while one was open for 9% of the time, Pallas kernels for 23%

profile of v8, /device:TPU:25, one launch (start us, length us, event | category | flops | bytes accessed | tf_op | source)
XLA Modules:
  0.0 64.3 jit_solution(13687494129161927040)
XLA Ops:
  0.0 6.8 %all-to-all-start = ((bf16[16,2,128,128]{3,2,1,0:T(8,128)(2,1)}), bf16[16,2,128,128]{3,2,1,0:T(8,128)(2,1)S(1)}, u32[]{:S(2)}, u32[]{:S(2)}) async-start(bf16[16,2,128,128]{3,2,1,0:T(8,128)(2,1)} %bitcast.57), calls=%async_computation | async-start | bytes 2097152 | tf_op jit(solution)/shard_map/all_to_all | solution.py:360
  6.8 0.2 cosine_bitcast_fusion
  7.1 0.2 fusion.27
  7.3 0.2 copy.22
  7.5 0.2 copy.23
  7.6 0.1 iota_add_fusion
  7.7 0.7 %pad_maximum_fusion.prop_ref = f32[2,128,128]{2,1,0:T(8,128)} fusion(f32[1,128,128]{2,1,0:T(8,128)S(1)} %get-tuple-element.18, f32[1,128,128]{2,1,0:T(8,128)S(1)} %get-tuple-element.17), kind=kLoop, calls=%fused_computation.13 | loop fusion | flops 32768 | bytes 262144 | tf_op jit(solution)/shard_map/stack | solution.py:378
  8.4 3.6 %fusion.10.win_ref = bf16[16,4,128,128]{3,2,1,0:T(8,128)(2,1)} fusion(s32[16,128]{1,0:T(8,128)S(1)} %get-tuple-element.25, s32[16,128]{1,0:T(8,128)S(1)} %get-tuple-element.26, f32[4,256,256]{2,1,0:T(8,128)S(1)} %copy-done), kind=kOutput, calls=%fused_computation.8 | convolution fusion | flops 1615069184 | bytes 3162112 | tf_op jit(solution)/shard_map/kcis,ksj->kcij/dot_general | solution.py:374
  12.0 10.9 %shard_map.82 = (f32[16,2,128,128]{3,2,1,0:T(8,128)}, f32[16,2,128,128]{3,2,1,0:T(8,128)}) custom-call(bf16[16,4,128,128]{3,2,1,0:T(8,128)(2,1)} %fusion.10.win_ref, f32[2,128,128]{2,1,0:T(8,128)} %probe_ref.3, f32[2,128,128]{2,1,0:T(8,128)} %pad_maximum_fusion.prop_ref, bf16[2,256,768]{2,1,0:T(8,128)(2,1)} %constant.14.clone.left_ref, ...), custom_call_target="tpu_custom_call" | custom-call | tf_op jit(solution)/shard_map/pallas_call | solution.py:292
  22.9 0.2 select_reduce_fusion
  23.1 0.6 add_clamp_fusion.target_ref
  23.7 1.0 %copy-done.1 = bf16[16,2,128,128]{3,2,1,0:T(8,128)(2,1)} copy-done((bf16[16,2,128,128]{3,2,1,0:T(8,128)(2,1)}, bf16[16,2,128,128]{3,2,1,0:T(8,128)(2,1)S(1)}, u32[]{:S(2)}) %copy-start.1) | copy-done | bytes 1048600
  24.7 17.0 %shard_map.83 = (f32[4,256,256]{2,1,0:T(8,128)}, f32[4,4,256]{2,1,0:T(4,128)}) custom-call(s32[16]{0:T(128)} %add_clamp_fusion.target_ref, s32[16]{0:T(128)} %copy-done.8, s32[16]{0:T(128)} %copy-done.7, bf16[32,128,128]{2,1,0:T(8,128)(2,1)} %bitcast.56, f32[16,2,128,128]{3,2,1,0:T(8,128)} %get-tuple-element.9.far_ref, ...), custom_call_target="tpu_custom_call" | custom-call | tf_op jit(solution)/shard_map/pallas_call | solution.py:338
  41.7 0.7 %bitcast_subtract_fusion = (f32[4,256]{1,0:T(4,128)S(1)}, f32[4,256]{1,0:T(4,128)S(1)}, f32[4,256]{1,0:T(4,128)S(1)}, f32[4,256]{1,0:T(4,128)S(1)}) fusion(f32[4,256,1]{1,0,2:T(4,128)S(1)} %copy.23, f32[4,4,256]{2,1,0:T(4,128)} %get-tuple-element.12, f32[4,256,1]{1,0,2:T(4,128)S(1)} %copy.22, f32[4,1,256]{2,1,0:T(1,128)S(1)} %get-tuple-element.15, ...), kind=kLoop, calls=%fused_computation.25 | loop fusion | flops 8192 | bytes 49152 | tf_op jit(solution)/shard_map/sub | solution.py:387
  42.4 4.7 %collective-permute-start = (f32[4,256]{1,0:T(4,128)S(1)}, f32[4,256]{1,0:T(4,128)S(1)}, u32[]{:S(2)}, u32[]{:S(2)}) collective-permute-start(f32[4,256]{1,0:T(4,128)S(1)} %get-tuple-element.21.bottom_ref), channel_id=1, source_target_pairs={{0,16},{16,32},{32,48},{48,64},{64,80},{80,96},{96,112},{1,17},{17... | collective-permute-start | bytes 12296 | tf_op jit(solution)/shard_map/ppermute | solution.py:29
  47.1 1.9 %collective-permute-start.1 = (f32[4,256]{1,0:T(4,128)S(1)}, f32[4,256]{1,0:T(4,128)S(1)}, u32[]{:S(2)}, u32[]{:S(2)}) collective-permute-start(f32[4,256]{1,0:T(4,128)S(1)} %get-tuple-element.22.top_ref), channel_id=1, source_target_pairs={{16,0},{32,16},{48,32},{64,48},{80,64},{96,80},{112,96},{17,1},{33... | collective-permute-start | bytes 12296 | tf_op jit(solution)/shard_map/ppermute | solution.py:30
  49.0 3.1 %collective-permute-start.2 = (f32[4,256]{1,0:T(4,128)S(1)}, f32[4,256]{1,0:T(4,128)S(1)}, u32[]{:S(2)}, u32[]{:S(2)}) collective-permute-start(f32[4,256]{1,0:T(4,128)S(1)} %get-tuple-element.19.last_ref), channel_id=1, source_target_pairs={{0,1},{1,2},{2,3},{3,4},{4,5},{5,6},{6,7},{7,8},{8,9},{9,10},{10,1... | collective-permute-start | bytes 12296 | tf_op jit(solution)/shard_map/ppermute | solution.py:31
  52.1 4.3 %collective-permute-start.3 = (f32[4,256]{1,0:T(4,128)S(1)}, f32[4,256]{1,0:T(4,128)S(1)}, u32[]{:S(2)}, u32[]{:S(2)}) collective-permute-start(f32[4,256]{1,0:T(4,128)S(1)} %get-tuple-element.20.first_ref), channel_id=1, source_target_pairs={{1,0},{2,1},{3,2},{4,3},{5,4},{6,5},{7,6},{8,7},{9,8},{10,9},{11,1... | collective-permute-start | bytes 12296 | tf_op jit(solution)/shard_map/ppermute | solution.py:32
  56.4 3.9 %shard_map.84.inner_ref = f32[4,256,256]{2,1,0:T(8,128)} custom-call(f32[4,256,256]{2,1,0:T(8,128)} %field_ref.1, f32[4,256,256]{2,1,0:T(8,128)} %get-tuple-element.11.total_ref), custom_call_target="tpu_custom_call" | custom-call | tf_op jit(solution)/shard_map/pallas_call | solution.py:104
  60.5 0.5 copy-done.9
  61.0 0.0 copy-done.10
  61.0 0.0 copy-done.11
  61.0 0.6 copy-done.12
  61.6 2.7 %shard_map.85 = f32[4,256,256]{2,1,0:T(8,128)} custom-call(f32[4,256,256]{2,1,0:T(8,128)} %shard_map.84.inner_ref, f32[4,256]{1,0:T(4,128)} %copy-done.6, f32[4,256]{1,0:T(4,128)} %copy-done.5, f32[4,256]{1,0:T(4,128)} %copy-done.4, f32[4,256]{1,0:T(4,128)} %copy-done.3, f32[4,256]{1,0:T(4,128)} %copy-done.9, ...), custom_call_target="tpu_custom_call", output_to_operand_aliasing={{}: (0, {})} | custom-call | tf_op jit(solution)/shard_map/pallas_call | solution.py:115
  (32 shorter events, 0.1 us)
Async XLA Ops:
  0.0 6.8 %copy-start.13 = (s32[1,1,16,2]{2,3,1,0:T(2,128)S(1)}, s32[1,1,16,2]{2,3,1,0:T(2,128)}, u32[]{:S(2)}) copy-start(s32[1,1,16,2]{2,3,1,0:T(2,128)} %param.12) | copy-start | bytes 388
  0.0 6.8 %copy-start.2 = (f32[128,128]{1,0:T(8,128)S(1)}, f32[128,128]{1,0:T(8,128)}, u32[]{:S(2)}) copy-start(f32[128,128]{1,0:T(8,128)} %param.10) | copy-start | bytes 196612
  0.0 7.1 %copy-start = (f32[4,256,256]{2,1,0:T(8,128)S(1)}, f32[4,256,256]{2,1,0:T(8,128)}, u32[]{:S(2)}) copy-start(f32[4,256,256]{2,1,0:T(8,128)} %field_ref.1) | copy-start | bytes 3145732
  0.0 23.7 %all-to-all-start = ((bf16[16,2,128,128]{3,2,1,0:T(8,128)(2,1)}), bf16[16,2,128,128]{3,2,1,0:T(8,128)(2,1)S(1)}, u32[]{:S(2)}, u32[]{:S(2)}) async-start(bf16[16,2,128,128]{3,2,1,0:T(8,128)(2,1)} %bitcast.57), calls=%async_computation | async-start | bytes 2097152 | tf_op jit(solution)/shard_map/all_to_all | solution.py:360
  6.8 5.2 %copy-start.7 = (s32[16]{0:T(128)}, s32[16]{0:T(128)S(1)}, u32[]{:S(2)}) copy-start(s32[16]{0:T(128)S(1)} %get-tuple-element.23.lefts_ref) | copy-start | bytes 196
  6.8 5.2 %copy-start.8 = (s32[16]{0:T(128)}, s32[16]{0:T(128)S(1)}, u32[]{:S(2)}) copy-start(s32[16]{0:T(128)S(1)} %get-tuple-element.24.tops_ref) | copy-start | bytes 196
  12.0 10.9 %copy-start.14 = (s32[1,1,16,1]{2,3,1,0:T(1,128)S(1)}, s32[1,1,16,1]{2,3,1,0:T(1,128)}, u32[]{:S(2)}) copy-start(s32[1,1,16,1]{2,3,1,0:T(1,128)} %param.13) | copy-start | bytes 196
  23.7 1.0 %copy-start.1 = (bf16[16,2,128,128]{3,2,1,0:T(8,128)(2,1)}, bf16[16,2,128,128]{3,2,1,0:T(8,128)(2,1)S(1)}, u32[]{:S(2)}) copy-start(bf16[16,2,128,128]{3,2,1,0:T(8,128)(2,1)S(1)} %all-to-all-done) | copy-start | bytes 3145732
  42.4 18.0 %copy-start.3 = (f32[4,256]{1,0:T(4,128)}, f32[4,256]{1,0:T(4,128)S(1)}, u32[]{:S(2)}) copy-start(f32[4,256]{1,0:T(4,128)S(1)} %get-tuple-element.19.last_ref) | copy-start | bytes 12292
  42.4 18.0 %copy-start.4 = (f32[4,256]{1,0:T(4,128)}, f32[4,256]{1,0:T(4,128)S(1)}, u32[]{:S(2)}) copy-start(f32[4,256]{1,0:T(4,128)S(1)} %get-tuple-element.20.first_ref) | copy-start | bytes 12292
  42.4 18.0 %copy-start.5 = (f32[4,256]{1,0:T(4,128)}, f32[4,256]{1,0:T(4,128)S(1)}, u32[]{:S(2)}) copy-start(f32[4,256]{1,0:T(4,128)S(1)} %get-tuple-element.21.bottom_ref) | copy-start | bytes 12292
  42.4 18.0 %copy-start.6 = (f32[4,256]{1,0:T(4,128)}, f32[4,256]{1,0:T(4,128)S(1)}, u32[]{:S(2)}) copy-start(f32[4,256]{1,0:T(4,128)S(1)} %get-tuple-element.22.top_ref) | copy-start | bytes 12292
  42.4 17.9 %collective-permute-start = (f32[4,256]{1,0:T(4,128)S(1)}, f32[4,256]{1,0:T(4,128)S(1)}, u32[]{:S(2)}, u32[]{:S(2)}) collective-permute-start(f32[4,256]{1,0:T(4,128)S(1)} %get-tuple-element.21.bottom_ref), channel_id=1, source_target_pairs={{0,16},{16,32},{32,48},{48,64},{64,80},{80,96},{96,112},{1,17},{17... | collective-permute-start | bytes 12296 | tf_op jit(solution)/shard_map/ppermute | solution.py:29
  47.1 13.3 %collective-permute-start.1 = (f32[4,256]{1,0:T(4,128)S(1)}, f32[4,256]{1,0:T(4,128)S(1)}, u32[]{:S(2)}, u32[]{:S(2)}) collective-permute-start(f32[4,256]{1,0:T(4,128)S(1)} %get-tuple-element.22.top_ref), channel_id=1, source_target_pairs={{16,0},{32,16},{48,32},{64,48},{80,64},{96,80},{112,96},{17,1},{33... | collective-permute-start | bytes 12296 | tf_op jit(solution)/shard_map/ppermute | solution.py:30
  49.0 11.4 %collective-permute-start.2 = (f32[4,256]{1,0:T(4,128)S(1)}, f32[4,256]{1,0:T(4,128)S(1)}, u32[]{:S(2)}, u32[]{:S(2)}) collective-permute-start(f32[4,256]{1,0:T(4,128)S(1)} %get-tuple-element.19.last_ref), channel_id=1, source_target_pairs={{0,1},{1,2},{2,3},{3,4},{4,5},{5,6},{6,7},{7,8},{8,9},{9,10},{10,1... | collective-permute-start | bytes 12296 | tf_op jit(solution)/shard_map/ppermute | solution.py:31
  52.1 8.3 %collective-permute-start.3 = (f32[4,256]{1,0:T(4,128)S(1)}, f32[4,256]{1,0:T(4,128)S(1)}, u32[]{:S(2)}, u32[]{:S(2)}) collective-permute-start(f32[4,256]{1,0:T(4,128)S(1)} %get-tuple-element.20.first_ref), channel_id=1, source_target_pairs={{1,0},{2,1},{3,2},{4,3},{5,4},{6,5},{7,6},{8,7},{9,8},{10,9},{11,1... | collective-permute-start | bytes 12296 | tf_op jit(solution)/shard_map/ppermute | solution.py:32
  60.4 0.6 copy-start.9
  60.4 0.6 copy-start.10
  60.4 0.6 copy-start.11
  61.0 0.6 copy-start.12

commit v9 on v8

--- a/solution.py
+++ b/solution.py
@@ -211,7 +211,7 @@
 
 def _backward_kernel(
     target_ref, tops_ref, lefts_ref, amp_ref, far_ref, inc_ref, win_ref, probe_ref, prop_ref,
-    left_ref, right_ref, out_ref, edges_ref
+    left_ref, right_ref, border_ref, out_ref, edges_ref
 ):
     group, width = win_ref.shape[0], probe_ref.shape[-1]
     step = pl.program_id(0)
@@ -268,8 +268,8 @@
         pick = (lanes == which).astype(jnp.bfloat16)
         for c in range(channels):
             plane = out_ref[c]
-            edges_ref[0, c:c + 1, :] = plane[0:1, :]
-            edges_ref[1, c:c + 1, :] = plane[tile - 1:tile, :]
+            edges_ref[0, c:c + 1, :] = border_ref[0, c:c + 1, :] - step_rate * plane[0:1, :]
+            edges_ref[1, c:c + 1, :] = border_ref[1, c:c + 1, :] - step_rate * plane[tile - 1:tile, :]
             high = plane.astype(jnp.bfloat16)
             rest = plane - high.astype(jnp.float32)
             middle = rest.astype(jnp.bfloat16)
@@ -280,8 +280,8 @@
                     pick, part, (((1,), (1,)), ((), ())), preferred_element_type=jnp.float32
                 )
                 cols = term if cols is None else cols + term
-            edges_ref[2, c:c + 1, :] = cols[0:1]
-            edges_ref[3, c:c + 1, :] = cols[1:2]
+            edges_ref[2, c:c + 1, :] = border_ref[2, c:c + 1, :] - step_rate * cols[0:1]
+            edges_ref[3, c:c + 1, :] = border_ref[3, c:c + 1, :] - step_rate * cols[1:2]
 
 
 def forward_waves(windows, probe, kernel, tables, group=8):
@@ -311,7 +311,8 @@
 
 
 def backward_gradients(target, tops, lefts, amplitudes, far, incoming, windows, probe, kernel,
-                       tables, tile, group=8):
+                       tables, border, group=8):
+    tile = border.shape[-1]
     count, channels, width, _ = windows.shape
     group = math.gcd(count, group)
     left_tables, right_tables = tables
@@ -321,7 +322,7 @@
         num_scalar_prefetch=3,
         grid=(count // group,),
         in_specs=[
-            pl.BlockSpec(amplitudes.shape, fixed),
+            pl.BlockSpec(memory_space=pltpu.VMEM),
             pl.BlockSpec((group, 2, width, width), batch),
             pl.BlockSpec((group, channels - 2, width, width), batch),
             pl.BlockSpec((group, channels, width, width), batch),
@@ -329,6 +330,7 @@
             pl.BlockSpec((2, width, width), fixed),
             pl.BlockSpec(left_tables.shape, fixed),
             pl.BlockSpec(right_tables.shape, fixed),
+            pl.BlockSpec(border.shape, fixed),
         ],
         out_specs=[
             pl.BlockSpec((channels, tile, tile), fixed),
@@ -343,7 +345,7 @@
             jax.ShapeDtypeStruct((4, channels, tile), jnp.float32),
         ],
     )(target, tops, lefts, amplitudes, far, incoming, windows, probe, kernel, left_tables,
-      right_tables)
+      right_tables, border)
 
 
 def per_device(object_init, probe, propagator_phase, measured, corners, owner_column):
@@ -377,15 +379,11 @@
     tables = block_tables(width)
     kernel = jnp.stack([jnp.cos(propagator_phase), jnp.sin(propagator_phase)])
     far, incoming = forward_waves(windows, probe, kernel, tables)
-    total, total_edges = backward_gradients(
-        target, tops, lefts, gathered, far, incoming, windows, probe, kernel, tables, tile
-    )
-    edges = (
-        field[:, 0, :] - step_rate * total_edges[0],
-        field[:, -1, :] - step_rate * total_edges[1],
-        field[:, :, 0] - step_rate * total_edges[2],
-        field[:, :, -1] - step_rate * total_edges[3],
-    )
+    border = jnp.stack([field[:, 0, :], field[:, -1, :], field[:, :, 0], field[:, :, -1]])
+    total, updated_edges = backward_gradients(
+        target, tops, lefts, gathered, far, incoming, windows, probe, kernel, tables, border
+    )
+    edges = tuple(updated_edges[k] for k in range(4))
     halos = exchange_edges(*edges)
     return smooth_update(field, total, edges, halos)
 

time: 65 us -> 66 us (1.015)
  local copies, waits for them, and re-layouts: 2.96 us -> 3.66 us
    sub x1 -> x0, other arithmetic: 0.7 us -> none  [per_device(): field[:, :, -1] - step_rate * total_edges[3]]
    squeeze x0 -> x1, local copies, waits for them, and re-layouts: none -> 0.69 us  [per_device(): edges = tuple((updated_edges[k] for k in range(4)))]
  transfers between devices with their start and end apart: 5 -> 5, of which waited for: 0 -> 0; matrix products, arithmetic and copies ran while one was open for 9% -> 10% of each run, Pallas kernels for 23% -> 23%
where the time goes in v9:
time: 66 us; the launch traced here: 65.4 us
  Pallas kernels  34.5 us (52%)
  starting transfers between devices  21.3 us (32%)
  local copies, waits for them, and re-layouts  3.66 us (6%)
  matrix products  3.6 us (5%)
  other arithmetic  2.11 us (3%)
    pallas_call x1, Pallas kernels, backward_gradients(): pl.pallas_call(_backward_kernel, grid_spec=grid_spec, out_shape=[jax.Shap...  17 us
    pallas_call x1, Pallas kernels, forward_waves(): pl.pallas_call(_forward_kernel, grid=(count // group,), in_specs=[pl.Bloc...  10.9 us
    all_to_all x1, starting transfers between devices, per_device(): lax.all_to_all(measured[0, 0], 'ty', split_axis=0, concat_axis=0, tiled=T...  6.75 us
    ppermute x1, starting transfers between devices, exchange_edges(): above = lax.ppermute(bottom, 'tx', up_rows)  5.23 us
    ppermute x1, starting transfers between devices, exchange_edges(): right = lax.ppermute(first, 'ty', down_cols)  4.3 us
    pallas_call x1, Pallas kernels, smooth_update(): pl.pallas_call(_inner_kernel, grid=(channels // 2,), in_specs=[plane, pla...  3.93 us
    dot_general x1, matrix products, per_device(): jnp.einsum('kcis,ksj->kcij', rows, col_pick, preferred_element_type=jnp.f...  3.6 us
    ppermute x1, starting transfers between devices, exchange_edges(): left = lax.ppermute(last, 'ty', up_cols)  3.09 us
  transfers between devices with their start and end apart: 5, of which 0 were waited for; matrix products, arithmetic and copies ran while one was open for 10% of the time, Pallas kernels for 23%

profile of v9, /device:TPU:25, one launch (start us, length us, event | category | flops | bytes accessed | tf_op | source)
XLA Modules:
  0.0 65.4 jit_solution(5680998846494897451)
XLA Ops:
  0.0 6.8 %all-to-all-start = ((bf16[16,2,128,128]{3,2,1,0:T(8,128)(2,1)}), bf16[16,2,128,128]{3,2,1,0:T(8,128)(2,1)S(1)}, u32[]{:S(2)}, u32[]{:S(2)}) async-start(bf16[16,2,128,128]{3,2,1,0:T(8,128)(2,1)} %bitcast.51), calls=%async_computation | async-start | bytes 2097152 | tf_op jit(solution)/shard_map/all_to_all | solution.py:362
  6.8 0.2 cosine_bitcast_fusion
  7.1 0.2 fusion.26
  7.3 0.2 copy.22
  7.5 0.2 copy.23
  7.6 0.1 iota_add_fusion
  7.7 3.6 %fusion.10.win_ref = bf16[16,4,128,128]{3,2,1,0:T(8,128)(2,1)} fusion(s32[16,128]{1,0:T(8,128)S(1)} %get-tuple-element.25, s32[16,128]{1,0:T(8,128)S(1)} %get-tuple-element.26, f32[4,256,256]{2,1,0:T(8,128)S(1)} %copy-done), kind=kOutput, calls=%fused_computation.8 | convolution fusion | flops 1615069184 | bytes 3162112 | tf_op jit(solution)/shard_map/kcis,ksj->kcij/dot_general | solution.py:376
  11.3 0.7 %pad_maximum_fusion.prop_ref = f32[2,128,128]{2,1,0:T(8,128)} fusion(f32[1,128,128]{2,1,0:T(8,128)S(1)} %get-tuple-element.18, f32[1,128,128]{2,1,0:T(8,128)S(1)} %get-tuple-element.17), kind=kLoop, calls=%fused_computation.13 | loop fusion | flops 32768 | bytes 262144 | tf_op jit(solution)/shard_map/stack | solution.py:380
  12.0 10.9 %shard_map.82 = (f32[16,2,128,128]{3,2,1,0:T(8,128)}, f32[16,2,128,128]{3,2,1,0:T(8,128)}) custom-call(bf16[16,4,128,128]{3,2,1,0:T(8,128)(2,1)} %fusion.10.win_ref, f32[2,128,128]{2,1,0:T(8,128)} %probe_ref.3, f32[2,128,128]{2,1,0:T(8,128)} %pad_maximum_fusion.prop_ref, bf16[2,256,768]{2,1,0:T(8,128)(2,1)} %constant.12.clone.left_ref, ...), custom_call_target="tpu_custom_call" | custom-call | tf_op jit(solution)/shard_map/pallas_call | solution.py:292
  22.9 0.6 pad_maximum_fusion.1.border_ref
  23.5 0.2 select_reduce_fusion
  23.7 0.6 add_clamp_fusion.target_ref
  24.3 1.0 %copy-done.1 = bf16[16,2,128,128]{3,2,1,0:T(8,128)(2,1)} copy-done((bf16[16,2,128,128]{3,2,1,0:T(8,128)(2,1)}, bf16[16,2,128,128]{3,2,1,0:T(8,128)(2,1)S(1)}, u32[]{:S(2)}) %copy-start.1) | copy-done | bytes 1048600
  25.3 17.0 %shard_map.83 = (f32[4,256,256]{2,1,0:T(8,128)}, f32[4,4,256]{2,1,0:T(4,128)}) custom-call(s32[16]{0:T(128)} %add_clamp_fusion.target_ref, s32[16]{0:T(128)} %copy-done.8, s32[16]{0:T(128)} %copy-done.7, bf16[32,128,128]{2,1,0:T(8,128)(2,1)} %bitcast.50, f32[16,2,128,128]{3,2,1,0:T(8,128)} %get-tuple-element.9.far_ref, ...), custom_call_target="tpu_custom_call" | custom-call | tf_op jit(solution)/shard_map/pallas_call | solution.py:340
  42.3 0.7 %slice_bitcast_fusion = (f32[4,256]{1,0:T(4,128)S(1)}, f32[4,256]{1,0:T(4,128)S(1)}, f32[4,256]{1,0:T(4,128)S(1)}, f32[4,256]{1,0:T(4,128)S(1)}) fusion(f32[4,4,256]{2,1,0:T(4,128)} %get-tuple-element.12), kind=kLoop, calls=%fused_computation.24 | loop fusion | bytes 32768 | tf_op jit(solution)/shard_map/squeeze | solution.py:386
  43.0 3.1 %collective-permute-start.2 = (f32[4,256]{1,0:T(4,128)S(1)}, f32[4,256]{1,0:T(4,128)S(1)}, u32[]{:S(2)}, u32[]{:S(2)}) collective-permute-start(f32[4,256]{1,0:T(4,128)S(1)} %get-tuple-element.19.last_ref), channel_id=1, source_target_pairs={{0,1},{1,2},{2,3},{3,4},{4,5},{5,6},{6,7},{7,8},{8,9},{9,10},{10,1... | collective-permute-start | bytes 12296 | tf_op jit(solution)/shard_map/ppermute | solution.py:31
  46.1 4.3 %collective-permute-start.3 = (f32[4,256]{1,0:T(4,128)S(1)}, f32[4,256]{1,0:T(4,128)S(1)}, u32[]{:S(2)}, u32[]{:S(2)}) collective-permute-start(f32[4,256]{1,0:T(4,128)S(1)} %get-tuple-element.20.first_ref), channel_id=1, source_target_pairs={{1,0},{2,1},{3,2},{4,3},{5,4},{6,5},{7,6},{8,7},{9,8},{10,9},{11,1... | collective-permute-start | bytes 12296 | tf_op jit(solution)/shard_map/ppermute | solution.py:32
  50.4 5.2 %collective-permute-start = (f32[4,256]{1,0:T(4,128)S(1)}, f32[4,256]{1,0:T(4,128)S(1)}, u32[]{:S(2)}, u32[]{:S(2)}) collective-permute-start(f32[4,256]{1,0:T(4,128)S(1)} %get-tuple-element.21.bottom_ref), channel_id=1, source_target_pairs={{0,16},{16,32},{32,48},{48,64},{64,80},{80,96},{96,112},{1,17},{17... | collective-permute-start | bytes 12296 | tf_op jit(solution)/shard_map/ppermute | solution.py:29
  55.6 1.9 %collective-permute-start.1 = (f32[4,256]{1,0:T(4,128)S(1)}, f32[4,256]{1,0:T(4,128)S(1)}, u32[]{:S(2)}, u32[]{:S(2)}) collective-permute-start(f32[4,256]{1,0:T(4,128)S(1)} %get-tuple-element.22.top_ref), channel_id=1, source_target_pairs={{16,0},{32,16},{48,32},{64,48},{80,64},{96,80},{112,96},{17,1},{33... | collective-permute-start | bytes 12296 | tf_op jit(solution)/shard_map/ppermute | solution.py:30
  57.6 3.9 %shard_map.84.inner_ref = f32[4,256,256]{2,1,0:T(8,128)} custom-call(f32[4,256,256]{2,1,0:T(8,128)} %field_ref.1, f32[4,256,256]{2,1,0:T(8,128)} %get-tuple-element.11.total_ref), custom_call_target="tpu_custom_call" | custom-call | tf_op jit(solution)/shard_map/pallas_call | solution.py:104
  61.6 0.5 copy-done.9
  62.1 0.0 copy-done.11
  62.1 0.6 copy-done.12
  62.7 2.7 %shard_map.85 = f32[4,256,256]{2,1,0:T(8,128)} custom-call(f32[4,256,256]{2,1,0:T(8,128)} %shard_map.84.inner_ref, f32[4,256]{1,0:T(4,128)} %copy-done.6, f32[4,256]{1,0:T(4,128)} %copy-done.5, f32[4,256]{1,0:T(4,128)} %copy-done.4, f32[4,256]{1,0:T(4,128)} %copy-done.3, f32[4,256]{1,0:T(4,128)} %copy-done.11, ...), custom_call_target="tpu_custom_call", output_to_operand_aliasing={{}: (0, {})} | custom-call | tf_op jit(solution)/shard_map/pallas_call | solution.py:115
  (34 shorter events, 0.1 us)
Async XLA Ops:
  0.0 6.8 %copy-start.13 = (s32[1,1,16,2]{2,3,1,0:T(2,128)S(1)}, s32[1,1,16,2]{2,3,1,0:T(2,128)}, u32[]{:S(2)}) copy-start(s32[1,1,16,2]{2,3,1,0:T(2,128)} %param.12) | copy-start | bytes 388
  0.0 6.8 %copy-start.2 = (f32[128,128]{1,0:T(8,128)S(1)}, f32[128,128]{1,0:T(8,128)}, u32[]{:S(2)}) copy-start(f32[128,128]{1,0:T(8,128)} %param.10) | copy-start | bytes 196612
  0.0 7.1 %copy-start = (f32[4,256,256]{2,1,0:T(8,128)S(1)}, f32[4,256,256]{2,1,0:T(8,128)}, u32[]{:S(2)}) copy-start(f32[4,256,256]{2,1,0:T(8,128)} %field_ref.1) | copy-start | bytes 3145732
  0.0 24.3 %all-to-all-start = ((bf16[16,2,128,128]{3,2,1,0:T(8,128)(2,1)}), bf16[16,2,128,128]{3,2,1,0:T(8,128)(2,1)S(1)}, u32[]{:S(2)}, u32[]{:S(2)}) async-start(bf16[16,2,128,128]{3,2,1,0:T(8,128)(2,1)} %bitcast.51), calls=%async_computation | async-start | bytes 2097152 | tf_op jit(solution)/shard_map/all_to_all | solution.py:362
  6.8 4.5 %copy-start.7 = (s32[16]{0:T(128)}, s32[16]{0:T(128)S(1)}, u32[]{:S(2)}) copy-start(s32[16]{0:T(128)S(1)} %get-tuple-element.23.lefts_ref) | copy-start | bytes 196
  6.8 4.5 %copy-start.8 = (s32[16]{0:T(128)}, s32[16]{0:T(128)S(1)}, u32[]{:S(2)}) copy-start(s32[16]{0:T(128)S(1)} %get-tuple-element.24.tops_ref) | copy-start | bytes 196
  11.3 12.2 %copy-start.14 = (s32[1,1,16,1]{2,3,1,0:T(1,128)S(1)}, s32[1,1,16,1]{2,3,1,0:T(1,128)}, u32[]{:S(2)}) copy-start(s32[1,1,16,1]{2,3,1,0:T(1,128)} %param.13) | copy-start | bytes 196
  24.3 1.0 %copy-start.1 = (bf16[16,2,128,128]{3,2,1,0:T(8,128)(2,1)}, bf16[16,2,128,128]{3,2,1,0:T(8,128)(2,1)S(1)}, u32[]{:S(2)}) copy-start(bf16[16,2,128,128]{3,2,1,0:T(8,128)(2,1)S(1)} %all-to-all-done) | copy-start | bytes 3145732
  43.0 18.6 %copy-start.3 = (f32[4,256]{1,0:T(4,128)}, f32[4,256]{1,0:T(4,128)S(1)}, u32[]{:S(2)}) copy-start(f32[4,256]{1,0:T(4,128)S(1)} %get-tuple-element.19.last_ref) | copy-start | bytes 12292
  43.0 18.6 %copy-start.4 = (f32[4,256]{1,0:T(4,128)}, f32[4,256]{1,0:T(4,128)S(1)}, u32[]{:S(2)}) copy-start(f32[4,256]{1,0:T(4,128)S(1)} %get-tuple-element.20.first_ref) | copy-start | bytes 12292
  43.0 18.6 %copy-start.5 = (f32[4,256]{1,0:T(4,128)}, f32[4,256]{1,0:T(4,128)S(1)}, u32[]{:S(2)}) copy-start(f32[4,256]{1,0:T(4,128)S(1)} %get-tuple-element.21.bottom_ref) | copy-start | bytes 12292
  43.0 18.6 %copy-start.6 = (f32[4,256]{1,0:T(4,128)}, f32[4,256]{1,0:T(4,128)S(1)}, u32[]{:S(2)}) copy-start(f32[4,256]{1,0:T(4,128)S(1)} %get-tuple-element.22.top_ref) | copy-start | bytes 12292
  43.0 18.5 %collective-permute-start.2 = (f32[4,256]{1,0:T(4,128)S(1)}, f32[4,256]{1,0:T(4,128)S(1)}, u32[]{:S(2)}, u32[]{:S(2)}) collective-permute-start(f32[4,256]{1,0:T(4,128)S(1)} %get-tuple-element.19.last_ref), channel_id=1, source_target_pairs={{0,1},{1,2},{2,3},{3,4},{4,5},{5,6},{6,7},{7,8},{8,9},{9,10},{10,1... | collective-permute-start | bytes 12296 | tf_op jit(solution)/shard_map/ppermute | solution.py:31
  46.1 15.4 %collective-permute-start.3 = (f32[4,256]{1,0:T(4,128)S(1)}, f32[4,256]{1,0:T(4,128)S(1)}, u32[]{:S(2)}, u32[]{:S(2)}) collective-permute-start(f32[4,256]{1,0:T(4,128)S(1)} %get-tuple-element.20.first_ref), channel_id=1, source_target_pairs={{1,0},{2,1},{3,2},{4,3},{5,4},{6,5},{7,6},{8,7},{9,8},{10,9},{11,1... | collective-permute-start | bytes 12296 | tf_op jit(solution)/shard_map/ppermute | solution.py:32
  50.4 11.1 %collective-permute-start = (f32[4,256]{1,0:T(4,128)S(1)}, f32[4,256]{1,0:T(4,128)S(1)}, u32[]{:S(2)}, u32[]{:S(2)}) collective-permute-start(f32[4,256]{1,0:T(4,128)S(1)} %get-tuple-element.21.bottom_ref), channel_id=1, source_target_pairs={{0,16},{16,32},{32,48},{48,64},{64,80},{80,96},{96,112},{1,17},{17... | collective-permute-start | bytes 12296 | tf_op jit(solution)/shard_map/ppermute | solution.py:29
  55.6 5.9 %collective-permute-start.1 = (f32[4,256]{1,0:T(4,128)S(1)}, f32[4,256]{1,0:T(4,128)S(1)}, u32[]{:S(2)}, u32[]{:S(2)}) collective-permute-start(f32[4,256]{1,0:T(4,128)S(1)} %get-tuple-element.22.top_ref), channel_id=1, source_target_pairs={{16,0},{32,16},{48,32},{64,48},{80,64},{96,80},{112,96},{17,1},{33... | collective-permute-start | bytes 12296 | tf_op jit(solution)/shard_map/ppermute | solution.py:30
  61.5 0.6 copy-start.9
  61.5 0.6 copy-start.10
  61.5 0.6 copy-start.11
  62.1 0.6 copy-start.12

commit v10 on v8

--- a/solution.py
+++ b/solution.py
@@ -19,17 +19,21 @@
     return jnp.sum(jnp.where(same & earlier, 1, 0), axis=1).astype(jnp.int32)
 
 
+def _swap_pairs(axis, first, last):
+    size = lax.axis_size(axis)
+    parity = lax.axis_index(axis) % 2
+    even = [(i, i + 1) for i in range(0, size - 1, 2)] + [(i + 1, i) for i in range(0, size - 1, 2)]
+    odd = [(i, i + 1) for i in range(1, size - 1, 2)] + [(i + 1, i) for i in range(1, size - 1, 2)]
+    from_even = lax.ppermute(jnp.where(parity == 0, last, first), axis, even)
+    from_odd = lax.ppermute(jnp.where(parity == 1, last, first), axis, odd)
+    before = jnp.where(parity == 1, from_even, from_odd)
+    after = jnp.where(parity == 0, from_even, from_odd)
+    return before, after
+
+
 def exchange_edges(top, bottom, first, last):
-    n_rows = lax.axis_size("tx")
-    n_cols = lax.axis_size("ty")
-    up_rows = [(i, i + 1) for i in range(n_rows - 1)]
-    down_rows = [(i + 1, i) for i in range(n_rows - 1)]
-    up_cols = [(i, i + 1) for i in range(n_cols - 1)]
-    down_cols = [(i + 1, i) for i in range(n_cols - 1)]
-    above = lax.ppermute(bottom, "tx", up_rows)
-    below = lax.ppermute(top, "tx", down_rows)
-    left = lax.ppermute(last, "ty", up_cols)
-    right = lax.ppermute(first, "ty", down_cols)
+    above, below = _swap_pairs("tx", top, bottom)
+    left, right = _swap_pairs("ty", first, last)
     return above, below, left, right
 
 

time: 65 us -> 62.6 us (0.963)
  starting transfers between devices: 20.7 us -> 16.7 us
  waiting for transfers between devices: 0.01 us -> 1.84 us
  local copies, waits for them, and re-layouts: 2.96 us -> 1.84 us
  other arithmetic: 2.21 us -> 3.32 us
    ppermute x4, starting transfers between devices: 14 us -> 9.92 us  [the longest x2 7.42 us: _swap_pairs(): from_odd = lax.ppermute(jnp.where(parity == 1, last, first), axis, odd)]
    select_n x0 -> x5, other arithmetic: none -> 1.92 us  [the longest x2 1.2 us: _swap_pairs(): after = jnp.where(parity == 0, from_even, from_odd)]
    ppermute x4, waiting for transfers between devices: 0.01 us -> 1.84 us  [the longest x2 1.83 us: _swap_pairs(): from_odd = lax.ppermute(jnp.where(parity == 1, last, first), axis, odd)]
    unnamed x32 -> x24, local copies, waits for them, and re-layouts: 2.5 us -> 1.38 us
    sub x1 -> x0, other arithmetic: 0.7 us -> none  [per_device(): field[:, :, -1] - step_rate * total_edges[3]]
  transfers between devices with their start and end apart: 5 -> 5, of which waited for: 0 -> 1; matrix products, arithmetic and copies ran while one was open for 9% -> 10% of each run, Pallas kernels for 23% -> 24%
where the time goes in v10:
time: 62.6 us; the launch traced here: 62.1 us
  Pallas kernels  34.6 us (55%)
  starting transfers between devices  16.7 us (27%)
  matrix products  3.61 us (6%)
  other arithmetic  3.32 us (5%)
  local copies, waits for them, and re-layouts  1.84 us (3%)
  waiting for transfers between devices  1.84 us (3%)
    pallas_call x1, Pallas kernels, backward_gradients(): pl.pallas_call(_backward_kernel, grid_spec=grid_spec, out_shape=[jax.Shap...  17 us
    pallas_call x1, Pallas kernels, forward_waves(): pl.pallas_call(_forward_kernel, grid=(count // group,), in_specs=[pl.Bloc...  10.9 us
    ppermute x2, starting transfers between devices, _swap_pairs(): from_odd = lax.ppermute(jnp.where(parity == 1, last, first), axis, odd)  7.42 us
    all_to_all x1, starting transfers between devices, per_device(): lax.all_to_all(measured[0, 0], 'ty', split_axis=0, concat_axis=0, tiled=T...  6.75 us
    pallas_call x1, Pallas kernels, smooth_update(): pl.pallas_call(_inner_kernel, grid=(channels // 2,), in_specs=[plane, pla...  3.93 us
    dot_general x1, matrix products, per_device(): jnp.einsum('kcis,ksj->kcij', rows, col_pick, preferred_element_type=jnp.f...  3.61 us
    pallas_call x1, Pallas kernels, smooth_update(): pl.pallas_call(_edge_kernel, grid=(size // lanes,), in_specs=[half, row_p...  2.73 us
    ppermute x2, starting transfers between devices, _swap_pairs(): from_even = lax.ppermute(jnp.where(parity == 0, last, first), axis, even)  2.5 us
  transfers between devices with their start and end apart: 5, of which 1 were waited for; matrix products, arithmetic and copies ran while one was open for 10% of the time, Pallas kernels for 24%

profile of v10, /device:TPU:25, one launch (start us, length us, event | category | flops | bytes accessed | tf_op | source)
XLA Modules:
  0.0 62.1 jit_solution(6470686163590921165)
XLA Ops:
  0.0 6.8 %all-to-all-start = ((bf16[16,2,128,128]{3,2,1,0:T(8,128)(2,1)}), bf16[16,2,128,128]{3,2,1,0:T(8,128)(2,1)S(1)}, u32[]{:S(2)}, u32[]{:S(2)}) async-start(bf16[16,2,128,128]{3,2,1,0:T(8,128)(2,1)} %bitcast.65), calls=%async_computation | async-start | bytes 2097152 | tf_op jit(solution)/shard_map/all_to_all | solution.py:364
  6.8 0.2 cosine_bitcast_fusion
  7.1 0.2 fusion.29
  7.3 0.2 copy.23
  7.5 0.2 copy.22
  7.6 0.1 iota_add_fusion
  7.7 0.7 %pad_maximum_fusion.prop_ref = f32[2,128,128]{2,1,0:T(8,128)} fusion(f32[1,128,128]{2,1,0:T(8,128)S(1)} %get-tuple-element.24, f32[1,128,128]{2,1,0:T(8,128)S(1)} %get-tuple-element.23), kind=kLoop, calls=%fused_computation.13 | loop fusion | flops 32768 | bytes 262144 | tf_op jit(solution)/shard_map/stack | solution.py:382
  8.4 3.6 %fusion.10.win_ref = bf16[16,4,128,128]{3,2,1,0:T(8,128)(2,1)} fusion(s32[16,128]{1,0:T(8,128)S(1)} %get-tuple-element.34, s32[16,128]{1,0:T(8,128)S(1)} %get-tuple-element.35, f32[4,256,256]{2,1,0:T(8,128)S(1)} %copy-done), kind=kOutput, calls=%fused_computation.8 | convolution fusion | flops 1615069184 | bytes 3162112 | tf_op jit(solution)/shard_map/kcis,ksj->kcij/dot_general | solution.py:378
  12.0 10.9 %shard_map.82 = (f32[16,2,128,128]{3,2,1,0:T(8,128)}, f32[16,2,128,128]{3,2,1,0:T(8,128)}) custom-call(bf16[16,4,128,128]{3,2,1,0:T(8,128)(2,1)} %fusion.10.win_ref, f32[2,128,128]{2,1,0:T(8,128)} %probe_ref.3, f32[2,128,128]{2,1,0:T(8,128)} %pad_maximum_fusion.prop_ref, bf16[2,256,768]{2,1,0:T(8,128)(2,1)} %constant.37.clone.left_ref, ...), custom_call_target="tpu_custom_call" | custom-call | tf_op jit(solution)/shard_map/pallas_call | solution.py:296
  23.0 0.2 select_reduce_fusion
  23.1 0.5 add_clamp_fusion.target_ref
  23.6 0.0 copy-start.1
  23.7 1.0 %copy-done.1 = bf16[16,2,128,128]{3,2,1,0:T(8,128)(2,1)} copy-done((bf16[16,2,128,128]{3,2,1,0:T(8,128)(2,1)}, bf16[16,2,128,128]{3,2,1,0:T(8,128)(2,1)S(1)}, u32[]{:S(2)}) %copy-start.1) | copy-done | bytes 1048600
  24.6 17.0 %shard_map.83 = (f32[4,256,256]{2,1,0:T(8,128)}, f32[4,4,256]{2,1,0:T(4,128)}) custom-call(s32[16]{0:T(128)} %add_clamp_fusion.target_ref, s32[16]{0:T(128)} %copy-done.8, s32[16]{0:T(128)} %copy-done.7, bf16[32,128,128]{2,1,0:T(8,128)(2,1)} %bitcast.64, f32[16,2,128,128]{3,2,1,0:T(8,128)} %get-tuple-element.9.far_ref, ...), custom_call_target="tpu_custom_call" | custom-call | tf_op jit(solution)/shard_map/pallas_call | solution.py:342
  41.6 0.7 %broadcast_select_fusion.3 = (f32[4,256]{1,0:T(4,128)S(1)}, f32[4,256]{1,0:T(4,128)S(1)}, f32[4,256]{1,0:T(4,128)S(1)}, f32[4,256]{1,0:T(4,128)S(1)}, f32[4,256]{1,0:T(4,128)S(1)}, /*index=5*/f32[4,256]{1,0:T(4,128)S(1)}) fusion(pred[]{:T(512)S(6)} %eq.69, f32[4,4,256]{2,1,0:T(4,128)} %get-tuple-element.12, f32[4,256,1]{1,0,2:T(4,128)S(1)} %copy.23, ...), kind=kLoop, calls=%fused_computation.30 | loop fusion | flops 10240 | bytes 57346 | tf_op jit(solution)/shard_map/jit(_where)/select_n | solution.py:28
  42.4 1.3 %collective-permute-start = (f32[4,256]{1,0:T(4,128)S(1)}, f32[4,256]{1,0:T(4,128)S(1)}, u32[]{:S(2)}, u32[]{:S(2)}) collective-permute-start(f32[4,256]{1,0:T(4,128)S(1)} %broadcast_select_fusion.5), channel_id=1, source_target_pairs={{0,16},{32,48},{64,80},{96,112},{16,0},{48,32},{80,64},{112,96},{1... | collective-permute-start | bytes 12296 | tf_op jit(solution)/shard_map/ppermute | solution.py:27
  43.7 3.4 %collective-permute-start.1 = (f32[4,256]{1,0:T(4,128)S(1)}, f32[4,256]{1,0:T(4,128)S(1)}, u32[]{:S(2)}, u32[]{:S(2)}) collective-permute-start(f32[4,256]{1,0:T(4,128)S(1)} %get-tuple-element.25), channel_id=1, source_target_pairs={{16,32},{48,64},{80,96},{32,16},{64,48},{96,80},{17,33},{49,65},{8... | collective-permute-start | bytes 12296 | tf_op jit(solution)/shard_map/ppermute | solution.py:28
  47.1 3.9 %shard_map.84.inner_ref = f32[4,256,256]{2,1,0:T(8,128)} custom-call(f32[4,256,256]{2,1,0:T(8,128)} %field_ref.1, f32[4,256,256]{2,1,0:T(8,128)} %get-tuple-element.11.total_ref), custom_call_target="tpu_custom_call" | custom-call | tf_op jit(solution)/shard_map/pallas_call | solution.py:108
  51.1 1.2 %collective-permute-start.2 = (f32[4,256]{1,0:T(4,128)S(1)}, f32[4,256]{1,0:T(4,128)S(1)}, u32[]{:S(2)}, u32[]{:S(2)}) collective-permute-start(f32[4,256]{1,0:T(4,128)S(1)} %broadcast_select_fusion.1), channel_id=1, source_target_pairs={{0,1},{2,3},{4,5},{6,7},{8,9},{10,11},{12,13},{14,15},{1,0},{3,2},... | collective-permute-start | bytes 12296 | tf_op jit(solution)/shard_map/ppermute | solution.py:27
  52.3 4.0 %collective-permute-start.3 = (f32[4,256]{1,0:T(4,128)S(1)}, f32[4,256]{1,0:T(4,128)S(1)}, u32[]{:S(2)}, u32[]{:S(2)}) collective-permute-start(f32[4,256]{1,0:T(4,128)S(1)} %get-tuple-element.13), channel_id=1, source_target_pairs={{1,2},{3,4},{5,6},{7,8},{9,10},{11,12},{13,14},{2,1},{4,3},{6,5},{... | collective-permute-start | bytes 12296 | tf_op jit(solution)/shard_map/ppermute | solution.py:28
  56.3 0.6 broadcast_select_fusion.4
  56.9 1.8 %collective-permute-done.3 = f32[4,256]{1,0:T(4,128)S(1)} collective-permute-done((f32[4,256]{1,0:T(4,128)S(1)}, f32[4,256]{1,0:T(4,128)S(1)}, u32[]{:S(2)}, u32[]{:S(2)}) %collective-permute-start.3) | collective-permute-done | bytes 4128 | tf_op jit(solution)/shard_map/ppermute | solution.py:28
  58.7 0.6 broadcast_select_fusion
  59.3 2.7 %shard_map.85 = f32[4,256,256]{2,1,0:T(8,128)} custom-call(f32[4,256,256]{2,1,0:T(8,128)} %shard_map.84.inner_ref, f32[4,256]{1,0:T(4,128)} %copy-done.5, f32[4,256]{1,0:T(4,128)} %copy-done.6, f32[4,256]{1,0:T(4,128)} %copy-done.4, f32[4,256]{1,0:T(4,128)} %copy-done.3, f32[4,256]{1,0:T(4,128)} %get-tuple-element.31.above_ref, ...), custom_call_target="tpu_custom_call", output_to_operand_aliasing={{}: (0, {})} | custom-call | tf_op jit(solution)/shard_map/pallas_call | solution.py:119
  (28 shorter events, 0.1 us)
Async XLA Ops:
  0.0 6.8 %copy-start.9 = (s32[1,1,16,2]{2,3,1,0:T(2,128)S(1)}, s32[1,1,16,2]{2,3,1,0:T(2,128)}, u32[]{:S(2)}) copy-start(s32[1,1,16,2]{2,3,1,0:T(2,128)} %param.12) | copy-start | bytes 388
  0.0 6.8 %copy-start.2 = (f32[128,128]{1,0:T(8,128)S(1)}, f32[128,128]{1,0:T(8,128)}, u32[]{:S(2)}) copy-start(f32[128,128]{1,0:T(8,128)} %param.10) | copy-start | bytes 196612
  0.0 7.1 %copy-start = (f32[4,256,256]{2,1,0:T(8,128)S(1)}, f32[4,256,256]{2,1,0:T(8,128)}, u32[]{:S(2)}) copy-start(f32[4,256,256]{2,1,0:T(8,128)} %field_ref.1) | copy-start | bytes 3145732
  0.0 23.6 %all-to-all-start = ((bf16[16,2,128,128]{3,2,1,0:T(8,128)(2,1)}), bf16[16,2,128,128]{3,2,1,0:T(8,128)(2,1)S(1)}, u32[]{:S(2)}, u32[]{:S(2)}) async-start(bf16[16,2,128,128]{3,2,1,0:T(8,128)(2,1)} %bitcast.65), calls=%async_computation | async-start | bytes 2097152 | tf_op jit(solution)/shard_map/all_to_all | solution.py:364
  6.8 5.2 %copy-start.7 = (s32[16]{0:T(128)}, s32[16]{0:T(128)S(1)}, u32[]{:S(2)}) copy-start(s32[16]{0:T(128)S(1)} %get-tuple-element.32.lefts_ref) | copy-start | bytes 196
  6.8 5.2 %copy-start.8 = (s32[16]{0:T(128)}, s32[16]{0:T(128)S(1)}, u32[]{:S(2)}) copy-start(s32[16]{0:T(128)S(1)} %get-tuple-element.33.tops_ref) | copy-start | bytes 196
  12.0 10.9 %copy-start.10 = (s32[1,1,16,1]{2,3,1,0:T(1,128)S(1)}, s32[1,1,16,1]{2,3,1,0:T(1,128)}, u32[]{:S(2)}) copy-start(s32[1,1,16,1]{2,3,1,0:T(1,128)} %param.13) | copy-start | bytes 196
  23.6 1.0 %copy-start.1 = (bf16[16,2,128,128]{3,2,1,0:T(8,128)(2,1)}, bf16[16,2,128,128]{3,2,1,0:T(8,128)(2,1)S(1)}, u32[]{:S(2)}) copy-start(bf16[16,2,128,128]{3,2,1,0:T(8,128)(2,1)S(1)} %all-to-all-done) | copy-start | bytes 3145732
  42.3 17.0 %copy-start.3 = (f32[4,256]{1,0:T(4,128)}, f32[4,256]{1,0:T(4,128)S(1)}, u32[]{:S(2)}) copy-start(f32[4,256]{1,0:T(4,128)S(1)} %get-tuple-element.14.last_ref) | copy-start | bytes 12292
  42.3 17.0 %copy-start.4 = (f32[4,256]{1,0:T(4,128)}, f32[4,256]{1,0:T(4,128)S(1)}, u32[]{:S(2)}) copy-start(f32[4,256]{1,0:T(4,128)S(1)} %get-tuple-element.15.first_ref) | copy-start | bytes 12292
  42.3 17.0 %copy-start.5 = (f32[4,256]{1,0:T(4,128)}, f32[4,256]{1,0:T(4,128)S(1)}, u32[]{:S(2)}) copy-start(f32[4,256]{1,0:T(4,128)S(1)} %get-tuple-element.26.top_ref) | copy-start | bytes 12292
  42.3 17.0 %copy-start.6 = (f32[4,256]{1,0:T(4,128)}, f32[4,256]{1,0:T(4,128)S(1)}, u32[]{:S(2)}) copy-start(f32[4,256]{1,0:T(4,128)S(1)} %get-tuple-element.27.bottom_ref) | copy-start | bytes 12292
  42.4 13.9 %collective-permute-start = (f32[4,256]{1,0:T(4,128)S(1)}, f32[4,256]{1,0:T(4,128)S(1)}, u32[]{:S(2)}, u32[]{:S(2)}) collective-permute-start(f32[4,256]{1,0:T(4,128)S(1)} %broadcast_select_fusion.5), channel_id=1, source_target_pairs={{0,16},{32,48},{64,80},{96,112},{16,0},{48,32},{80,64},{112,96},{1... | collective-permute-start | bytes 12296 | tf_op jit(solution)/shard_map/ppermute | solution.py:27
  43.7 12.6 %collective-permute-start.1 = (f32[4,256]{1,0:T(4,128)S(1)}, f32[4,256]{1,0:T(4,128)S(1)}, u32[]{:S(2)}, u32[]{:S(2)}) collective-permute-start(f32[4,256]{1,0:T(4,128)S(1)} %get-tuple-element.25), channel_id=1, source_target_pairs={{16,32},{48,64},{80,96},{32,16},{64,48},{96,80},{17,33},{49,65},{8... | collective-permute-start | bytes 12296 | tf_op jit(solution)/shard_map/ppermute | solution.py:28
  51.1 5.8 %collective-permute-start.2 = (f32[4,256]{1,0:T(4,128)S(1)}, f32[4,256]{1,0:T(4,128)S(1)}, u32[]{:S(2)}, u32[]{:S(2)}) collective-permute-start(f32[4,256]{1,0:T(4,128)S(1)} %broadcast_select_fusion.1), channel_id=1, source_target_pairs={{0,1},{2,3},{4,5},{6,7},{8,9},{10,11},{12,13},{14,15},{1,0},{3,2},... | collective-permute-start | bytes 12296 | tf_op jit(solution)/shard_map/ppermute | solution.py:27
  52.3 6.4 %collective-permute-start.3 = (f32[4,256]{1,0:T(4,128)S(1)}, f32[4,256]{1,0:T(4,128)S(1)}, u32[]{:S(2)}, u32[]{:S(2)}) collective-permute-start(f32[4,256]{1,0:T(4,128)S(1)} %get-tuple-element.13), channel_id=1, source_target_pairs={{1,2},{3,4},{5,6},{7,8},{9,10},{11,12},{13,14},{2,1},{4,3},{6,5},{... | collective-permute-start | bytes 12296 | tf_op jit(solution)/shard_map/ppermute | solution.py:28

commit v11 on v9

--- a/solution.py
+++ b/solution.py
@@ -19,18 +19,11 @@
     return jnp.sum(jnp.where(same & earlier, 1, 0), axis=1).astype(jnp.int32)
 
 
-def exchange_edges(top, bottom, first, last):
-    n_rows = lax.axis_size("tx")
-    n_cols = lax.axis_size("ty")
-    up_rows = [(i, i + 1) for i in range(n_rows - 1)]
-    down_rows = [(i + 1, i) for i in range(n_rows - 1)]
-    up_cols = [(i, i + 1) for i in range(n_cols - 1)]
-    down_cols = [(i + 1, i) for i in range(n_cols - 1)]
-    above = lax.ppermute(bottom, "tx", up_rows)
-    below = lax.ppermute(top, "tx", down_rows)
-    left = lax.ppermute(last, "ty", up_cols)
-    right = lax.ppermute(first, "ty", down_cols)
-    return above, below, left, right
+def _swap(axis, even_payload, odd_payload):
+    size = lax.axis_size(axis)
+    even = [(i, i + 1) for i in range(0, size - 1, 2)] + [(i + 1, i) for i in range(0, size - 1, 2)]
+    odd = [(i, i + 1) for i in range(1, size - 1, 2)] + [(i + 1, i) for i in range(1, size - 1, 2)]
+    return lax.ppermute(even_payload, axis, even), lax.ppermute(odd_payload, axis, odd)
 
 
 def _bend(real, imag):
@@ -61,10 +54,24 @@
     out_ref[1] = centers[1] + smooth_rate * total_i
 
 
-def _edge_kernel(inner_ref, top_ref, bottom_ref, first_ref, last_ref,
-                 above_ref, below_ref, left_ref, right_ref, out_ref):
+def _edge_kernel(parity_ref, inner_ref, row_even_ref, row_odd_ref, col_even_ref, col_odd_ref,
+                 got_row_even_ref, got_row_odd_ref, got_col_even_ref, got_col_odd_ref, out_ref):
     size, lanes = inner_ref.shape[1], inner_ref.shape[2]
     block = pl.program_id(0)
+    row_parity = parity_ref[0]
+    col_parity = parity_ref[1]
+    row_even, row_odd = row_even_ref[...], row_odd_ref[...]
+    col_even, col_odd = col_even_ref[...], col_odd_ref[...]
+    got_row_even, got_row_odd = got_row_even_ref[...], got_row_odd_ref[...]
+    got_col_even, got_col_odd = got_col_even_ref[...], got_col_odd_ref[...]
+    top = jnp.where(row_parity == 0, row_odd, row_even)
+    bottom = jnp.where(row_parity == 0, row_even, row_odd)
+    first = jnp.where(col_parity == 0, col_odd, col_even)
+    last = jnp.where(col_parity == 0, col_even, col_odd)
+    above = jnp.where(row_parity == 1, got_row_even, got_row_odd)
+    below = jnp.where(row_parity == 0, got_row_even, got_row_odd)
+    left = jnp.where(col_parity == 1, got_col_even, got_col_odd)
+    right = jnp.where(col_parity == 0, got_col_even, got_col_odd)
     rows = lax.broadcasted_iota(jnp.int32, (size, lanes), 0)
     cols = lax.broadcasted_iota(jnp.int32, (size, lanes), 1)
     square = lax.broadcasted_iota(jnp.int32, (lanes, lanes), 0) == lax.broadcasted_iota(
@@ -83,11 +90,11 @@
     edge_col = jnp.where(block == 0, 0, lanes - 1)
     for s in range(inner_ref.shape[0] // 2):
         c0, c1 = 2 * s, 2 * s + 1
-        north = _bend(above_ref[c0:c0 + 1] - top_ref[c0:c0 + 1], above_ref[c1:c1 + 1] - top_ref[c1:c1 + 1])
-        south = _bend(below_ref[c0:c0 + 1] - bottom_ref[c0:c0 + 1],
-                      below_ref[c1:c1 + 1] - bottom_ref[c1:c1 + 1])
-        west = _bend(left_ref[c0:c0 + 1] - first_ref[c0:c0 + 1], left_ref[c1:c1 + 1] - first_ref[c1:c1 + 1])
-        east = _bend(right_ref[c0:c0 + 1] - last_ref[c0:c0 + 1], right_ref[c1:c1 + 1] - last_ref[c1:c1 + 1])
+        north = _bend(above[c0:c0 + 1] - top[c0:c0 + 1], above[c1:c1 + 1] - top[c1:c1 + 1])
+        south = _bend(below[c0:c0 + 1] - bottom[c0:c0 + 1],
+                      below[c1:c1 + 1] - bottom[c1:c1 + 1])
+        west = _bend(left[c0:c0 + 1] - first[c0:c0 + 1], left[c1:c1 + 1] - first[c1:c1 + 1])
+        east = _bend(right[c0:c0 + 1] - last[c0:c0 + 1], right[c1:c1 + 1] - last[c1:c1 + 1])
         for part, c in ((0, c0), (1, c1)):
             side = as_column(jnp.where(block == 0, west[part], east[part]))
             extra = (
@@ -98,7 +105,7 @@
             out_ref[c] = inner_ref[c] + smooth_rate * extra
 
 
-def smooth_update(field, total, edges, halos):
+def smooth_update(field, total, parity, payloads, received):
     channels, size, _ = field.shape
     plane = pl.BlockSpec((2, size, size), lambda s: (s, 0, 0))
     inner = pl.pallas_call(
@@ -112,14 +119,15 @@
     half = pl.BlockSpec((channels, size, lanes), lambda b: (0, 0, b))
     row_part = pl.BlockSpec((channels, lanes), lambda b: (0, b))
     whole = pl.BlockSpec((channels, size), lambda b: (0, 0))
+    scalars = pl.BlockSpec(memory_space=pltpu.SMEM)
     return pl.pallas_call(
         _edge_kernel,
         grid=(size // lanes,),
-        in_specs=[half, row_part, row_part, whole, whole, row_part, row_part, whole, whole],
+        in_specs=[scalars, half, row_part, row_part, whole, whole, row_part, row_part, whole, whole],
         out_specs=half,
         out_shape=jax.ShapeDtypeStruct(field.shape, jnp.float32),
-        input_output_aliases={0: 0},
-    )(inner, *edges, *halos)
+        input_output_aliases={1: 0},
+    )(parity, inner, *payloads, *received)
 
 
 def block_tables(width):
@@ -210,8 +218,9 @@
 
 
 def _backward_kernel(
-    target_ref, tops_ref, lefts_ref, amp_ref, far_ref, inc_ref, win_ref, probe_ref, prop_ref,
-    left_ref, right_ref, border_ref, out_ref, edges_ref
+    target_ref, tops_ref, lefts_ref, parity_ref, amp_ref, far_ref, inc_ref, win_ref, probe_ref,
+    prop_ref, left_ref, right_ref, border_ref, out_ref, row_even_ref, row_odd_ref, col_even_ref,
+    col_odd_ref
 ):
     group, width = win_ref.shape[0], probe_ref.shape[-1]
     step = pl.program_id(0)
@@ -266,10 +275,14 @@
         lanes = lax.broadcasted_iota(jnp.int32, (8, tile), 1)
         which = jnp.where(lax.broadcasted_iota(jnp.int32, (8, tile), 0) == 0, 0, tile - 1)
         pick = (lanes == which).astype(jnp.bfloat16)
+        row_parity = parity_ref[0]
+        col_parity = parity_ref[1]
         for c in range(channels):
             plane = out_ref[c]
-            edges_ref[0, c:c + 1, :] = border_ref[0, c:c + 1, :] - step_rate * plane[0:1, :]
-            edges_ref[1, c:c + 1, :] = border_ref[1, c:c + 1, :] - step_rate * plane[tile - 1:tile, :]
+            top = border_ref[0, c:c + 1, :] - step_rate * plane[0:1, :]
+            bottom = border_ref[1, c:c + 1, :] - step_rate * plane[tile - 1:tile, :]
+            row_even_ref[c:c + 1, :] = jnp.where(row_parity == 0, bottom, top)
+            row_odd_ref[c:c + 1, :] = jnp.where(row_parity == 1, bottom, top)
             high = plane.astype(jnp.bfloat16)
             rest = plane - high.astype(jnp.float32)
             middle = rest.astype(jnp.bfloat16)
@@ -280,8 +293,10 @@
                     pick, part, (((1,), (1,)), ((), ())), preferred_element_type=jnp.float32
                 )
                 cols = term if cols is None else cols + term
-            edges_ref[2, c:c + 1, :] = border_ref[2, c:c + 1, :] - step_rate * cols[0:1]
-            edges_ref[3, c:c + 1, :] = border_ref[3, c:c + 1, :] - step_rate * cols[1:2]
+            first = border_ref[2, c:c + 1, :] - step_rate * cols[0:1]
+            last = border_ref[3, c:c + 1, :] - step_rate * cols[1:2]
+            col_even_ref[c:c + 1, :] = jnp.where(col_parity == 0, last, first)
+            col_odd_ref[c:c + 1, :] = jnp.where(col_parity == 1, last, first)
 
 
 def forward_waves(windows, probe, kernel, tables, group=8):
@@ -310,19 +325,20 @@
     )(windows, probe, kernel, left_tables, right_tables)
 
 
-def backward_gradients(target, tops, lefts, amplitudes, far, incoming, windows, probe, kernel,
-                       tables, border, group=8):
+def backward_gradients(target, tops, lefts, parity, amplitudes, far, incoming, windows, probe,
+                       kernel, tables, border, group=8):
+    count, channels, width, _ = windows.shape
     tile = border.shape[-1]
-    count, channels, width, _ = windows.shape
     group = math.gcd(count, group)
     left_tables, right_tables = tables
     fixed = lambda k, *_: (0, 0, 0)
     batch = lambda k, *_: (k, 0, 0, 0)
+    line = pl.BlockSpec((channels, tile), lambda k, *_: (0, 0))
     grid_spec = pltpu.PrefetchScalarGridSpec(
-        num_scalar_prefetch=3,
+        num_scalar_prefetch=4,
         grid=(count // group,),
         in_specs=[
-            pl.BlockSpec(memory_space=pltpu.VMEM),
+            pl.BlockSpec(amplitudes.shape, fixed),
             pl.BlockSpec((group, 2, width, width), batch),
             pl.BlockSpec((group, channels - 2, width, width), batch),
             pl.BlockSpec((group, channels, width, width), batch),
@@ -332,19 +348,14 @@
             pl.BlockSpec(right_tables.shape, fixed),
             pl.BlockSpec(border.shape, fixed),
         ],
-        out_specs=[
-            pl.BlockSpec((channels, tile, tile), fixed),
-            pl.BlockSpec((4, channels, tile), fixed),
-        ],
-    )
+        out_specs=[pl.BlockSpec((channels, tile, tile), fixed), line, line, line, line],
+    )
+    edge = jax.ShapeDtypeStruct((channels, tile), jnp.float32)
     return pl.pallas_call(
         _backward_kernel,
         grid_spec=grid_spec,
-        out_shape=[
-            jax.ShapeDtypeStruct((channels, tile, tile), jnp.float32),
-            jax.ShapeDtypeStruct((4, channels, tile), jnp.float32),
-        ],
-    )(target, tops, lefts, amplitudes, far, incoming, windows, probe, kernel, left_tables,
+        out_shape=[jax.ShapeDtypeStruct((channels, tile, tile), jnp.float32), edge, edge, edge, edge],
+    )(target, tops, lefts, parity, amplitudes, far, incoming, windows, probe, kernel, left_tables,
       right_tables, border)
 
 
@@ -379,13 +390,13 @@
     tables = block_tables(width)
     kernel = jnp.stack([jnp.cos(propagator_phase), jnp.sin(propagator_phase)])
     far, incoming = forward_waves(windows, probe, kernel, tables)
+    parity = jnp.stack([lax.axis_index("tx") % 2, lax.axis_index("ty") % 2]).astype(jnp.int32)
     border = jnp.stack([field[:, 0, :], field[:, -1, :], field[:, :, 0], field[:, :, -1]])
-    total, updated_edges = backward_gradients(
-        target, tops, lefts, gathered, far, incoming, windows, probe, kernel, tables, border
-    )
-    edges = tuple(updated_edges[k] for k in range(4))
-    halos = exchange_edges(*edges)
-    return smooth_update(field, total, edges, halos)
+    total, *payloads = backward_gradients(
+        target, tops, lefts, parity, gathered, far, incoming, windows, probe, kernel, tables, border
+    )
+    received = _swap("tx", payloads[0], payloads[1]) + _swap("ty", payloads[2], payloads[3])
+    return smooth_update(field, total, parity, payloads, received)
 
 
 def solution(mesh):

time: 66 us -> 61.2 us (0.927)
  starting transfers between devices: 21.3 us -> 16.8 us
  local copies, waits for them, and re-layouts: 3.66 us -> 2.99 us
    ppermute x4, starting transfers between devices: 14.5 us -> 10 us  [the longest x2 7.43 us: _swap(): lax.ppermute(odd_payload, axis, odd)]
    squeeze x1 -> x0, local copies, waits for them, and re-layouts: 0.69 us -> none  [per_device(): edges = tuple((updated_edges[k] for k in range(4)))]
    unnamed x32 -> x24, local copies, waits for them, and re-layouts: 2.51 us -> 2.54 us
  transfers between devices with their start and end apart: 5 -> 5, of which waited for: 0 -> 0; matrix products, arithmetic and copies ran while one was open for 10% -> 12% of each run, Pallas kernels for 23% -> 24%
where the time goes in v11:
time: 61.2 us; the launch traced here: 60.9 us
  Pallas kernels  34.6 us (57%)
  starting transfers between devices  16.8 us (27%)
  matrix products  3.61 us (6%)
  local copies, waits for them, and re-layouts  2.99 us (5%)
  other arithmetic  2.76 us (5%)
    pallas_call x1, Pallas kernels, backward_gradients(): pl.pallas_call(_backward_kernel, grid_spec=grid_spec, out_shape=[jax.Shap...  17 us
    pallas_call x1, Pallas kernels, forward_waves(): pl.pallas_call(_forward_kernel, grid=(count // group,), in_specs=[pl.Bloc...  10.9 us
    ppermute x2, starting transfers between devices, _swap(): lax.ppermute(odd_payload, axis, odd)  7.43 us
    all_to_all x1, starting transfers between devices, per_device(): lax.all_to_all(measured[0, 0], 'ty', split_axis=0, concat_axis=0, tiled=T...  6.75 us
    pallas_call x1, Pallas kernels, smooth_update(): pl.pallas_call(_inner_kernel, grid=(channels // 2,), in_specs=[plane, pla...  3.93 us
    dot_general x1, matrix products, per_device(): jnp.einsum('kcis,ksj->kcij', rows, col_pick, preferred_element_type=jnp.f...  3.61 us
    pallas_call x1, Pallas kernels, smooth_update(): pl.pallas_call(_edge_kernel, grid=(size // lanes,), in_specs=[scalars, ha...  2.73 us
    ppermute x2, starting transfers between devices, _swap(): lax.ppermute(even_payload, axis, even)  2.57 us
  transfers between devices with their start and end apart: 5, of which 0 were waited for; matrix products, arithmetic and copies ran while one was open for 12% of the time, Pallas kernels for 24%

profile of v11, /device:TPU:25, one launch (start us, length us, event | category | flops | bytes accessed | tf_op | source)
XLA Modules:
  0.0 60.9 jit_solution(15643380364184561956)
XLA Ops:
  0.0 6.8 %all-to-all-start = ((bf16[16,2,128,128]{3,2,1,0:T(8,128)(2,1)}), bf16[16,2,128,128]{3,2,1,0:T(8,128)(2,1)S(1)}, u32[]{:S(2)}, u32[]{:S(2)}) async-start(bf16[16,2,128,128]{3,2,1,0:T(8,128)(2,1)} %bitcast.45), calls=%async_computation | async-start | bytes 2097152 | tf_op jit(solution)/shard_map/all_to_all | solution.py:373
  6.8 0.2 cosine_bitcast_fusion
  7.1 0.2 fusion.26
  7.3 0.2 copy.22
  7.5 0.2 copy.23
  7.6 0.1 iota_add_fusion
  7.7 0.7 %pad_maximum_fusion.prop_ref = f32[2,128,128]{2,1,0:T(8,128)} fusion(f32[1,128,128]{2,1,0:T(8,128)S(1)} %get-tuple-element.24, f32[1,128,128]{2,1,0:T(8,128)S(1)} %get-tuple-element.23), kind=kLoop, calls=%fused_computation.13 | loop fusion | flops 32768 | bytes 262144 | tf_op jit(solution)/shard_map/stack | solution.py:391
  8.4 3.6 %fusion.10.win_ref = bf16[16,4,128,128]{3,2,1,0:T(8,128)(2,1)} fusion(s32[16,128]{1,0:T(8,128)S(1)} %get-tuple-element.27, s32[16,128]{1,0:T(8,128)S(1)} %get-tuple-element.28, f32[4,256,256]{2,1,0:T(8,128)S(1)} %copy-done), kind=kOutput, calls=%fused_computation.8 | convolution fusion | flops 1615069184 | bytes 3162112 | tf_op jit(solution)/shard_map/kcis,ksj->kcij/dot_general | solution.py:387
  12.0 10.9 %shard_map.82 = (f32[16,2,128,128]{3,2,1,0:T(8,128)}, f32[16,2,128,128]{3,2,1,0:T(8,128)}) custom-call(bf16[16,4,128,128]{3,2,1,0:T(8,128)(2,1)} %fusion.10.win_ref, f32[2,128,128]{2,1,0:T(8,128)} %probe_ref.3, f32[2,128,128]{2,1,0:T(8,128)} %pad_maximum_fusion.prop_ref, bf16[2,256,768]{2,1,0:T(8,128)(2,1)} %constant.35.clone.left_ref, ...), custom_call_target="tpu_custom_call" | custom-call | tf_op jit(solution)/shard_map/pallas_call | solution.py:307
  22.9 0.7 %pad_add_fusion.parity_ref = s32[2]{0:T(128)} fusion(s32[1]{0:T(128)} %bitcast.1, s32[1]{0:T(128)} %bitcast), kind=kLoop, calls=%fused_computation.24 | loop fusion | flops 2 | bytes 16 | tf_op jit(solution)/shard_map/stack | solution.py:393
  23.6 0.6 pad_maximum_fusion.1.border_ref
  24.2 0.2 select_reduce_fusion
  24.4 0.6 add_clamp_fusion.target_ref
  25.0 1.0 %copy-done.1 = bf16[16,2,128,128]{3,2,1,0:T(8,128)(2,1)} copy-done((bf16[16,2,128,128]{3,2,1,0:T(8,128)(2,1)}, bf16[16,2,128,128]{3,2,1,0:T(8,128)(2,1)S(1)}, u32[]{:S(2)}) %copy-start.1) | copy-done | bytes 1048600
  26.0 17.0 %shard_map.83 = (f32[4,256,256]{2,1,0:T(8,128)}, f32[4,256]{1,0:T(4,128)}, f32[4,256]{1,0:T(4,128)}, f32[4,256]{1,0:T(4,128)}, f32[4,256]{1,0:T(4,128)}) custom-call(s32[16]{0:T(128)} %add_clamp_fusion.target_ref, s32[16]{0:T(128)} %copy-done.4, s32[16]{0:T(128)} %copy-done.3, s32[2]{0:T(128)} %pad_add_fusion.parity_ref, bf16[32,128,128]{2,1,0:T(8,128)(2,1)} %bitcast.44, ...), custom_call_target="tpu_custom_call" | custom-call | tf_op jit(solution)/shard_map/pallas_call | solution.py:354
  43.0 1.3 %collective-permute-start = (f32[4,256]{1,0:T(4,128)}, f32[4,256]{1,0:T(4,128)S(1)}, u32[]{:S(2)}, u32[]{:S(2)}) collective-permute-start(f32[4,256]{1,0:T(4,128)} %get-tuple-element.15.row_even_ref), channel_id=1, source_target_pairs={{0,16},{32,48},{64,80},{96,112},{16,0},{48,32},{80,64},{112,96},{1... | collective-permute-start | bytes 12296 | tf_op jit(solution)/shard_map/ppermute | solution.py:26
  44.3 3.4 %collective-permute-start.1 = (f32[4,256]{1,0:T(4,128)}, f32[4,256]{1,0:T(4,128)S(1)}, u32[]{:S(2)}, u32[]{:S(2)}) collective-permute-start(f32[4,256]{1,0:T(4,128)} %get-tuple-element.16.row_odd_ref), channel_id=1, source_target_pairs={{16,32},{48,64},{80,96},{32,16},{64,48},{96,80},{17,33},{49,65},{8... | collective-permute-start | bytes 12296 | tf_op jit(solution)/shard_map/ppermute | solution.py:26
  47.8 1.3 %collective-permute-start.2 = (f32[4,256]{1,0:T(4,128)}, f32[4,256]{1,0:T(4,128)S(1)}, u32[]{:S(2)}, u32[]{:S(2)}) collective-permute-start(f32[4,256]{1,0:T(4,128)} %get-tuple-element.17.col_even_ref), channel_id=1, source_target_pairs={{0,1},{2,3},{4,5},{6,7},{8,9},{10,11},{12,13},{14,15},{1,0},{3,2},... | collective-permute-start | bytes 12296 | tf_op jit(solution)/shard_map/ppermute | solution.py:26
  49.0 4.0 %collective-permute-start.3 = (f32[4,256]{1,0:T(4,128)}, f32[4,256]{1,0:T(4,128)S(1)}, u32[]{:S(2)}, u32[]{:S(2)}) collective-permute-start(f32[4,256]{1,0:T(4,128)} %get-tuple-element.18.col_odd_ref), channel_id=1, source_target_pairs={{1,2},{3,4},{5,6},{7,8},{9,10},{11,12},{13,14},{2,1},{4,3},{6,5},{... | collective-permute-start | bytes 12296 | tf_op jit(solution)/shard_map/ppermute | solution.py:26
  53.0 3.9 %shard_map.84.inner_ref = f32[4,256,256]{2,1,0:T(8,128)} custom-call(f32[4,256,256]{2,1,0:T(8,128)} %field_ref.1, f32[4,256,256]{2,1,0:T(8,128)} %get-tuple-element.14.total_ref), custom_call_target="tpu_custom_call" | custom-call | tf_op jit(solution)/shard_map/pallas_call | solution.py:111
  57.0 0.5 copy-done.5
  57.6 0.0 copy-done.7
  57.6 0.6 copy-done.8
  58.2 2.7 %shard_map.85 = f32[4,256,256]{2,1,0:T(8,128)} custom-call(s32[2]{0:T(128)} %pad_add_fusion.parity_ref, f32[4,256,256]{2,1,0:T(8,128)} %shard_map.84.inner_ref, f32[4,256]{1,0:T(4,128)} %get-tuple-element.15.row_even_ref, f32[4,256]{1,0:T(4,128)} %get-tuple-element.16.row_odd_ref, ...), custom_call_target="tpu_custom_call", output_to_operand_aliasing={{}: (1, {})} | custom-call | tf_op jit(solution)/shard_map/pallas_call | solution.py:123
  (26 shorter events, 0.1 us)
Async XLA Ops:
  0.0 6.8 %copy-start.9 = (s32[1,1,16,2]{2,3,1,0:T(2,128)S(1)}, s32[1,1,16,2]{2,3,1,0:T(2,128)}, u32[]{:S(2)}) copy-start(s32[1,1,16,2]{2,3,1,0:T(2,128)} %param.12) | copy-start | bytes 388
  0.0 6.8 %copy-start.2 = (f32[128,128]{1,0:T(8,128)S(1)}, f32[128,128]{1,0:T(8,128)}, u32[]{:S(2)}) copy-start(f32[128,128]{1,0:T(8,128)} %param.10) | copy-start | bytes 196612
  0.0 7.1 %copy-start = (f32[4,256,256]{2,1,0:T(8,128)S(1)}, f32[4,256,256]{2,1,0:T(8,128)}, u32[]{:S(2)}) copy-start(f32[4,256,256]{2,1,0:T(8,128)} %field_ref.1) | copy-start | bytes 3145732
  0.0 25.0 %all-to-all-start = ((bf16[16,2,128,128]{3,2,1,0:T(8,128)(2,1)}), bf16[16,2,128,128]{3,2,1,0:T(8,128)(2,1)S(1)}, u32[]{:S(2)}, u32[]{:S(2)}) async-start(bf16[16,2,128,128]{3,2,1,0:T(8,128)(2,1)} %bitcast.45), calls=%async_computation | async-start | bytes 2097152 | tf_op jit(solution)/shard_map/all_to_all | solution.py:373
  6.8 5.2 %copy-start.3 = (s32[16]{0:T(128)}, s32[16]{0:T(128)S(1)}, u32[]{:S(2)}) copy-start(s32[16]{0:T(128)S(1)} %get-tuple-element.25.lefts_ref) | copy-start | bytes 196
  6.8 5.2 %copy-start.4 = (s32[16]{0:T(128)}, s32[16]{0:T(128)S(1)}, u32[]{:S(2)}) copy-start(s32[16]{0:T(128)S(1)} %get-tuple-element.26.tops_ref) | copy-start | bytes 196
  12.0 12.2 %copy-start.10 = (s32[1,1,16,1]{2,3,1,0:T(1,128)S(1)}, s32[1,1,16,1]{2,3,1,0:T(1,128)}, u32[]{:S(2)}) copy-start(s32[1,1,16,1]{2,3,1,0:T(1,128)} %param.13) | copy-start | bytes 196
  25.0 1.0 %copy-start.1 = (bf16[16,2,128,128]{3,2,1,0:T(8,128)(2,1)}, bf16[16,2,128,128]{3,2,1,0:T(8,128)(2,1)S(1)}, u32[]{:S(2)}) copy-start(bf16[16,2,128,128]{3,2,1,0:T(8,128)(2,1)S(1)} %all-to-all-done) | copy-start | bytes 3145732
  43.0 14.0 %collective-permute-start = (f32[4,256]{1,0:T(4,128)}, f32[4,256]{1,0:T(4,128)S(1)}, u32[]{:S(2)}, u32[]{:S(2)}) collective-permute-start(f32[4,256]{1,0:T(4,128)} %get-tuple-element.15.row_even_ref), channel_id=1, source_target_pairs={{0,16},{32,48},{64,80},{96,112},{16,0},{48,32},{80,64},{112,96},{1... | collective-permute-start | bytes 12296 | tf_op jit(solution)/shard_map/ppermute | solution.py:26
  44.3 12.6 %collective-permute-start.1 = (f32[4,256]{1,0:T(4,128)}, f32[4,256]{1,0:T(4,128)S(1)}, u32[]{:S(2)}, u32[]{:S(2)}) collective-permute-start(f32[4,256]{1,0:T(4,128)} %get-tuple-element.16.row_odd_ref), channel_id=1, source_target_pairs={{16,32},{48,64},{80,96},{32,16},{64,48},{96,80},{17,33},{49,65},{8... | collective-permute-start | bytes 12296 | tf_op jit(solution)/shard_map/ppermute | solution.py:26
  47.8 9.2 %collective-permute-start.2 = (f32[4,256]{1,0:T(4,128)}, f32[4,256]{1,0:T(4,128)S(1)}, u32[]{:S(2)}, u32[]{:S(2)}) collective-permute-start(f32[4,256]{1,0:T(4,128)} %get-tuple-element.17.col_even_ref), channel_id=1, source_target_pairs={{0,1},{2,3},{4,5},{6,7},{8,9},{10,11},{12,13},{14,15},{1,0},{3,2},... | collective-permute-start | bytes 12296 | tf_op jit(solution)/shard_map/ppermute | solution.py:26
  49.0 8.0 %collective-permute-start.3 = (f32[4,256]{1,0:T(4,128)}, f32[4,256]{1,0:T(4,128)S(1)}, u32[]{:S(2)}, u32[]{:S(2)}) collective-permute-start(f32[4,256]{1,0:T(4,128)} %get-tuple-element.18.col_odd_ref), channel_id=1, source_target_pairs={{1,2},{3,4},{5,6},{7,8},{9,10},{11,12},{13,14},{2,1},{4,3},{6,5},{... | collective-permute-start | bytes 12296 | tf_op jit(solution)/shard_map/ppermute | solution.py:26
  57.0 0.6 copy-start.5
  57.0 0.6 copy-start.6
  57.0 0.6 copy-start.7
  57.6 0.6 copy-start.8

commit v12 on v11

--- a/solution.py
+++ b/solution.py
@@ -58,8 +58,8 @@
                  got_row_even_ref, got_row_odd_ref, got_col_even_ref, got_col_odd_ref, out_ref):
     size, lanes = inner_ref.shape[1], inner_ref.shape[2]
     block = pl.program_id(0)
-    row_parity = parity_ref[0]
-    col_parity = parity_ref[1]
+    row_parity = parity_ref[parity_ref.shape[0] - 2]
+    col_parity = parity_ref[parity_ref.shape[0] - 1]
     row_even, row_odd = row_even_ref[...], row_odd_ref[...]
     col_even, col_odd = col_even_ref[...], col_odd_ref[...]
     got_row_even, got_row_odd = got_row_even_ref[...], got_row_odd_ref[...]
@@ -218,19 +218,20 @@
 
 
 def _backward_kernel(
-    target_ref, tops_ref, lefts_ref, parity_ref, amp_ref, far_ref, inc_ref, win_ref, probe_ref,
+    scalar_ref, amp_ref, far_ref, inc_ref, win_ref, probe_ref,
     prop_ref, left_ref, right_ref, border_ref, out_ref, row_even_ref, row_odd_ref, col_even_ref,
     col_odd_ref
 ):
     group, width = win_ref.shape[0], probe_ref.shape[-1]
     step = pl.program_id(0)
+    count = group * pl.num_programs(0)
     transform = _transformer(left_ref, right_ref, group, width)
     layers = _layers(win_ref)
     slices = len(layers)
     probe = (probe_ref[0][None], probe_ref[1][None])
     kernel_conj = (prop_ref[0][None], -prop_ref[1][None])
     amplitude = jnp.stack(
-        [amp_ref[target_ref[step * group + g]].astype(jnp.float32) for g in range(group)]
+        [amp_ref[scalar_ref[step * group + g]].astype(jnp.float32) for g in range(group)]
     )
     far = (far_ref[:, 0], far_ref[:, 1])
     magnitude = jnp.sqrt(far[0] * far[0] + far[1] * far[1] + 1.0)
@@ -249,8 +250,8 @@
         jnp.int32, (width, tile), 0)
     placed, col_picks = [], []
     for g in range(group):
-        top = tops_ref[step * group + g]
-        left = lefts_ref[step * group + g]
+        top = scalar_ref[count + step * group + g]
+        left = scalar_ref[2 * count + step * group + g]
         row_pick = (down == top).astype(jnp.bfloat16)
         col_picks.append((across == left).astype(jnp.bfloat16))
         stacked = jnp.concatenate([plane[g] for plane in planes], axis=1)
@@ -275,8 +276,8 @@
         lanes = lax.broadcasted_iota(jnp.int32, (8, tile), 1)
         which = jnp.where(lax.broadcasted_iota(jnp.int32, (8, tile), 0) == 0, 0, tile - 1)
         pick = (lanes == which).astype(jnp.bfloat16)
-        row_parity = parity_ref[0]
-        col_parity = parity_ref[1]
+        row_parity = scalar_ref[3 * count]
+        col_parity = scalar_ref[3 * count + 1]
         for c in range(channels):
             plane = out_ref[c]
             top = border_ref[0, c:c + 1, :] - step_rate * plane[0:1, :]
@@ -325,8 +326,8 @@
     )(windows, probe, kernel, left_tables, right_tables)
 
 
-def backward_gradients(target, tops, lefts, parity, amplitudes, far, incoming, windows, probe,
-                       kernel, tables, border, group=8):
+def backward_gradients(scalars, amplitudes, far, incoming, windows, probe, kernel, tables, border,
+                       group=8):
     count, channels, width, _ = windows.shape
     tile = border.shape[-1]
     group = math.gcd(count, group)
@@ -335,7 +336,7 @@
     batch = lambda k, *_: (k, 0, 0, 0)
     line = pl.BlockSpec((channels, tile), lambda k, *_: (0, 0))
     grid_spec = pltpu.PrefetchScalarGridSpec(
-        num_scalar_prefetch=4,
+        num_scalar_prefetch=1,
         grid=(count // group,),
         in_specs=[
             pl.BlockSpec(amplitudes.shape, fixed),
@@ -355,8 +356,7 @@
         _backward_kernel,
         grid_spec=grid_spec,
         out_shape=[jax.ShapeDtypeStruct((channels, tile, tile), jnp.float32), edge, edge, edge, edge],
-    )(target, tops, lefts, parity, amplitudes, far, incoming, windows, probe, kernel, left_tables,
-      right_tables, border)
+    )(scalars, amplitudes, far, incoming, windows, probe, kernel, left_tables, right_tables, border)
 
 
 def per_device(object_init, probe, propagator_phase, measured, corners, owner_column):
@@ -390,13 +390,14 @@
     tables = block_tables(width)
     kernel = jnp.stack([jnp.cos(propagator_phase), jnp.sin(propagator_phase)])
     far, incoming = forward_waves(windows, probe, kernel, tables)
-    parity = jnp.stack([lax.axis_index("tx") % 2, lax.axis_index("ty") % 2]).astype(jnp.int32)
+    parity = jnp.stack([lax.axis_index("tx") % 2, lax.axis_index("ty") % 2])
+    scalars = jnp.concatenate([target, tops, lefts, parity]).astype(jnp.int32)
     border = jnp.stack([field[:, 0, :], field[:, -1, :], field[:, :, 0], field[:, :, -1]])
     total, *payloads = backward_gradients(
-        target, tops, lefts, parity, gathered, far, incoming, windows, probe, kernel, tables, border
+        scalars, gathered, far, incoming, windows, probe, kernel, tables, border
     )
     received = _swap("tx", payloads[0], payloads[1]) + _swap("ty", payloads[2], payloads[3])
-    return smooth_update(field, total, parity, payloads, received)
+    return smooth_update(field, total, scalars, payloads, received)
 
 
 def solution(mesh):

time: 61.2 us -> 60.5 us (0.989)
  other arithmetic: 2.76 us -> 1.51 us
    another operation x1 -> x0, other arithmetic: 0.65 us -> none  [per_device(): jnp.stack([lax.axis_index('tx') % 2, lax.axis_index('ty') % 2])]
    unnamed x24 -> x20, local copies, waits for them, and re-layouts: 2.54 us -> 2.53 us
  transfers between devices with their start and end apart: 5 -> 5, of which waited for: 0 -> 0; matrix products, arithmetic and copies ran while one was open for 12% -> 11% of each run, Pallas kernels for 24% -> 25%
where the time goes in v12:
time: 60.5 us; the launch traced here: 60.2 us
  Pallas kernels  34.6 us (57%)
  starting transfers between devices  16.7 us (28%)
  matrix products  3.62 us (6%)
  local copies, waits for them, and re-layouts  3.57 us (6%)
  other arithmetic  1.51 us (2%)
    pallas_call x1, Pallas kernels, backward_gradients(): pl.pallas_call(_backward_kernel, grid_spec=grid_spec, out_shape=[jax.Shap...  17 us
    pallas_call x1, Pallas kernels, forward_waves(): pl.pallas_call(_forward_kernel, grid=(count // group,), in_specs=[pl.Bloc...  10.9 us
    ppermute x2, starting transfers between devices, _swap(): lax.ppermute(odd_payload, axis, odd)  7.41 us
    all_to_all x1, starting transfers between devices, per_device(): lax.all_to_all(measured[0, 0], 'ty', split_axis=0, concat_axis=0, tiled=T...  6.75 us
    pallas_call x1, Pallas kernels, smooth_update(): pl.pallas_call(_inner_kernel, grid=(channels // 2,), in_specs=[plane, pla...  3.93 us
    dot_general x1, matrix products, per_device(): jnp.einsum('kcis,ksj->kcij', rows, col_pick, preferred_element_type=jnp.f...  3.62 us
    pallas_call x1, Pallas kernels, smooth_update(): pl.pallas_call(_edge_kernel, grid=(size // lanes,), in_specs=[scalars, ha...  2.73 us
    ppermute x2, starting transfers between devices, _swap(): lax.ppermute(even_payload, axis, even)  2.58 us
  transfers between devices with their start and end apart: 5, of which 0 were waited for; matrix products, arithmetic and copies ran while one was open for 11% of the time, Pallas kernels for 25%

profile of v12, /device:TPU:25, one launch (start us, length us, event | category | flops | bytes accessed | tf_op | source)
XLA Modules:
  0.0 60.2 jit_solution(1620954885733250323)
XLA Ops:
  0.0 0.0 copy-start
  0.0 6.8 %all-to-all-start = ((bf16[16,2,128,128]{3,2,1,0:T(8,128)(2,1)}), bf16[16,2,128,128]{3,2,1,0:T(8,128)(2,1)S(1)}, u32[]{:S(2)}, u32[]{:S(2)}) async-start(bf16[16,2,128,128]{3,2,1,0:T(8,128)(2,1)} %bitcast.45), calls=%async_computation | async-start | bytes 2097152 | tf_op jit(solution)/shard_map/all_to_all | solution.py:373
  6.8 0.2 select_reduce_fusion
  7.0 0.2 cosine_bitcast_fusion
  7.3 0.2 fusion.26
  7.5 0.2 copy.22
  7.6 0.2 copy.23
  7.8 0.1 iota_add_fusion
  7.9 0.6 concatenate.3.scalar_ref.parity_ref
  8.5 0.6 %pad_maximum_fusion.prop_ref = f32[2,128,128]{2,1,0:T(8,128)} fusion(f32[1,128,128]{2,1,0:T(8,128)S(1)} %get-tuple-element.24, f32[1,128,128]{2,1,0:T(8,128)S(1)} %get-tuple-element.23), kind=kLoop, calls=%fused_computation.13 | loop fusion | flops 32768 | bytes 262144 | tf_op jit(solution)/shard_map/stack | solution.py:391
  9.1 3.6 %fusion.10.win_ref = bf16[16,4,128,128]{3,2,1,0:T(8,128)(2,1)} fusion(s32[16,128]{1,0:T(8,128)S(1)} %get-tuple-element.27, s32[16,128]{1,0:T(8,128)S(1)} %get-tuple-element.28, f32[4,256,256]{2,1,0:T(8,128)S(1)} %copy-done), kind=kOutput, calls=%fused_computation.8 | convolution fusion | flops 1615069184 | bytes 3162112 | tf_op jit(solution)/shard_map/kcis,ksj->kcij/dot_general | solution.py:387
  12.8 10.9 %shard_map.82 = (f32[16,2,128,128]{3,2,1,0:T(8,128)}, f32[16,2,128,128]{3,2,1,0:T(8,128)}) custom-call(bf16[16,4,128,128]{3,2,1,0:T(8,128)(2,1)} %fusion.10.win_ref, f32[2,128,128]{2,1,0:T(8,128)} %probe_ref.3, f32[2,128,128]{2,1,0:T(8,128)} %pad_maximum_fusion.prop_ref, bf16[2,256,768]{2,1,0:T(8,128)(2,1)} %constant.35.clone.left_ref, ...), custom_call_target="tpu_custom_call" | custom-call | tf_op jit(solution)/shard_map/pallas_call | solution.py:308
  23.7 0.6 pad_maximum_fusion.1.border_ref
  24.3 1.0 %copy-done.1 = bf16[16,2,128,128]{3,2,1,0:T(8,128)(2,1)} copy-done((bf16[16,2,128,128]{3,2,1,0:T(8,128)(2,1)}, bf16[16,2,128,128]{3,2,1,0:T(8,128)(2,1)S(1)}, u32[]{:S(2)}) %copy-start.1) | copy-done | bytes 1048600
  25.3 17.0 %shard_map.83 = (f32[4,256,256]{2,1,0:T(8,128)}, f32[4,256]{1,0:T(4,128)}, f32[4,256]{1,0:T(4,128)}, f32[4,256]{1,0:T(4,128)}, f32[4,256]{1,0:T(4,128)}) custom-call(s32[50]{0:T(128)} %concatenate.3.scalar_ref.parity_ref, bf16[32,128,128]{2,1,0:T(8,128)(2,1)} %bitcast.44, f32[16,2,128,128]{3,2,1,0:T(8,128)} %get-tuple-element.12.far_ref, ...), custom_call_target="tpu_custom_call" | custom-call | tf_op jit(solution)/shard_map/pallas_call | solution.py:355
  42.3 1.3 %collective-permute-start = (f32[4,256]{1,0:T(4,128)}, f32[4,256]{1,0:T(4,128)S(1)}, u32[]{:S(2)}, u32[]{:S(2)}) collective-permute-start(f32[4,256]{1,0:T(4,128)} %get-tuple-element.15.row_even_ref), channel_id=1, source_target_pairs={{0,16},{32,48},{64,80},{96,112},{16,0},{48,32},{80,64},{112,96},{1... | collective-permute-start | bytes 12296 | tf_op jit(solution)/shard_map/ppermute | solution.py:26
  43.7 3.4 %collective-permute-start.1 = (f32[4,256]{1,0:T(4,128)}, f32[4,256]{1,0:T(4,128)S(1)}, u32[]{:S(2)}, u32[]{:S(2)}) collective-permute-start(f32[4,256]{1,0:T(4,128)} %get-tuple-element.16.row_odd_ref), channel_id=1, source_target_pairs={{16,32},{48,64},{80,96},{32,16},{64,48},{96,80},{17,33},{49,65},{8... | collective-permute-start | bytes 12296 | tf_op jit(solution)/shard_map/ppermute | solution.py:26
  47.1 1.3 %collective-permute-start.2 = (f32[4,256]{1,0:T(4,128)}, f32[4,256]{1,0:T(4,128)S(1)}, u32[]{:S(2)}, u32[]{:S(2)}) collective-permute-start(f32[4,256]{1,0:T(4,128)} %get-tuple-element.17.col_even_ref), channel_id=1, source_target_pairs={{0,1},{2,3},{4,5},{6,7},{8,9},{10,11},{12,13},{14,15},{1,0},{3,2},... | collective-permute-start | bytes 12296 | tf_op jit(solution)/shard_map/ppermute | solution.py:26
  48.4 4.0 %collective-permute-start.3 = (f32[4,256]{1,0:T(4,128)}, f32[4,256]{1,0:T(4,128)S(1)}, u32[]{:S(2)}, u32[]{:S(2)}) collective-permute-start(f32[4,256]{1,0:T(4,128)} %get-tuple-element.18.col_odd_ref), channel_id=1, source_target_pairs={{1,2},{3,4},{5,6},{7,8},{9,10},{11,12},{13,14},{2,1},{4,3},{6,5},{... | collective-permute-start | bytes 12296 | tf_op jit(solution)/shard_map/ppermute | solution.py:26
  52.3 3.9 %shard_map.84.inner_ref = f32[4,256,256]{2,1,0:T(8,128)} custom-call(f32[4,256,256]{2,1,0:T(8,128)} %field_ref.1, f32[4,256,256]{2,1,0:T(8,128)} %get-tuple-element.14.total_ref), custom_call_target="tpu_custom_call" | custom-call | tf_op jit(solution)/shard_map/pallas_call | solution.py:111
  56.3 0.5 copy-done.3
  56.9 0.0 copy-done.5
  56.9 0.6 copy-done.6
  57.5 2.7 %shard_map.85 = f32[4,256,256]{2,1,0:T(8,128)} custom-call(s32[50]{0:T(128)} %concatenate.3.scalar_ref.parity_ref, f32[4,256,256]{2,1,0:T(8,128)} %shard_map.84.inner_ref, f32[4,256]{1,0:T(4,128)} %get-tuple-element.15.row_even_ref, f32[4,256]{1,0:T(4,128)} %get-tuple-element.16.row_odd_ref, ...), custom_call_target="tpu_custom_call", output_to_operand_aliasing={{}: (1, {})} | custom-call | tf_op jit(solution)/shard_map/pallas_call | solution.py:123
  (22 shorter events, 0.1 us)
Async XLA Ops:
  0.0 6.8 %copy-start.8 = (s32[1,1,16,1]{2,3,1,0:T(1,128)S(1)}, s32[1,1,16,1]{2,3,1,0:T(1,128)}, u32[]{:S(2)}) copy-start(s32[1,1,16,1]{2,3,1,0:T(1,128)} %param.13) | copy-start | bytes 196
  0.0 7.0 %copy-start.7 = (s32[1,1,16,2]{2,3,1,0:T(2,128)S(1)}, s32[1,1,16,2]{2,3,1,0:T(2,128)}, u32[]{:S(2)}) copy-start(s32[1,1,16,2]{2,3,1,0:T(2,128)} %param.12) | copy-start | bytes 388
  0.0 7.0 %copy-start.2 = (f32[128,128]{1,0:T(8,128)S(1)}, f32[128,128]{1,0:T(8,128)}, u32[]{:S(2)}) copy-start(f32[128,128]{1,0:T(8,128)} %param.10) | copy-start | bytes 196612
  0.0 7.2 %copy-start = (f32[4,256,256]{2,1,0:T(8,128)S(1)}, f32[4,256,256]{2,1,0:T(8,128)}, u32[]{:S(2)}) copy-start(f32[4,256,256]{2,1,0:T(8,128)} %field_ref.1) | copy-start | bytes 3145732
  0.0 24.3 %all-to-all-start = ((bf16[16,2,128,128]{3,2,1,0:T(8,128)(2,1)}), bf16[16,2,128,128]{3,2,1,0:T(8,128)(2,1)S(1)}, u32[]{:S(2)}, u32[]{:S(2)}) async-start(bf16[16,2,128,128]{3,2,1,0:T(8,128)(2,1)} %bitcast.45), calls=%async_computation | async-start | bytes 2097152 | tf_op jit(solution)/shard_map/all_to_all | solution.py:373
  24.3 1.0 %copy-start.1 = (bf16[16,2,128,128]{3,2,1,0:T(8,128)(2,1)}, bf16[16,2,128,128]{3,2,1,0:T(8,128)(2,1)S(1)}, u32[]{:S(2)}) copy-start(bf16[16,2,128,128]{3,2,1,0:T(8,128)(2,1)S(1)} %all-to-all-done) | copy-start | bytes 3145732
  42.3 13.9 %collective-permute-start = (f32[4,256]{1,0:T(4,128)}, f32[4,256]{1,0:T(4,128)S(1)}, u32[]{:S(2)}, u32[]{:S(2)}) collective-permute-start(f32[4,256]{1,0:T(4,128)} %get-tuple-element.15.row_even_ref), channel_id=1, source_target_pairs={{0,16},{32,48},{64,80},{96,112},{16,0},{48,32},{80,64},{112,96},{1... | collective-permute-start | bytes 12296 | tf_op jit(solution)/shard_map/ppermute | solution.py:26
  43.7 12.6 %collective-permute-start.1 = (f32[4,256]{1,0:T(4,128)}, f32[4,256]{1,0:T(4,128)S(1)}, u32[]{:S(2)}, u32[]{:S(2)}) collective-permute-start(f32[4,256]{1,0:T(4,128)} %get-tuple-element.16.row_odd_ref), channel_id=1, source_target_pairs={{16,32},{48,64},{80,96},{32,16},{64,48},{96,80},{17,33},{49,65},{8... | collective-permute-start | bytes 12296 | tf_op jit(solution)/shard_map/ppermute | solution.py:26
  47.1 9.2 %collective-permute-start.2 = (f32[4,256]{1,0:T(4,128)}, f32[4,256]{1,0:T(4,128)S(1)}, u32[]{:S(2)}, u32[]{:S(2)}) collective-permute-start(f32[4,256]{1,0:T(4,128)} %get-tuple-element.17.col_even_ref), channel_id=1, source_target_pairs={{0,1},{2,3},{4,5},{6,7},{8,9},{10,11},{12,13},{14,15},{1,0},{3,2},... | collective-permute-start | bytes 12296 | tf_op jit(solution)/shard_map/ppermute | solution.py:26
  48.4 8.0 %collective-permute-start.3 = (f32[4,256]{1,0:T(4,128)}, f32[4,256]{1,0:T(4,128)S(1)}, u32[]{:S(2)}, u32[]{:S(2)}) collective-permute-start(f32[4,256]{1,0:T(4,128)} %get-tuple-element.18.col_odd_ref), channel_id=1, source_target_pairs={{1,2},{3,4},{5,6},{7,8},{9,10},{11,12},{13,14},{2,1},{4,3},{6,5},{... | collective-permute-start | bytes 12296 | tf_op jit(solution)/shard_map/ppermute | solution.py:26
  56.3 0.6 copy-start.3
  56.3 0.6 copy-start.4
  56.3 0.6 copy-start.5
  56.9 0.6 copy-start.6

commit v13 on v12

--- a/solution.py
+++ b/solution.py
@@ -74,18 +74,25 @@
     right = jnp.where(col_parity == 0, got_col_even, got_col_odd)
     rows = lax.broadcasted_iota(jnp.int32, (size, lanes), 0)
     cols = lax.broadcasted_iota(jnp.int32, (size, lanes), 1)
-    square = lax.broadcasted_iota(jnp.int32, (lanes, lanes), 0) == lax.broadcasted_iota(
-        jnp.int32, (lanes, lanes), 1)
+    eye = (lax.broadcasted_iota(jnp.int32, (lanes, lanes), 0) == lax.broadcasted_iota(
+        jnp.int32, (lanes, lanes), 1)).astype(jnp.bfloat16)
 
     def as_column(line):
-        return jnp.concatenate(
-            [
-                jnp.sum(jnp.where(square, line[:, h * lanes:(h + 1) * lanes], 0.0), axis=1,
-                        keepdims=True)
-                for h in range(size // lanes)
-            ],
-            axis=0,
-        )
+        high = line.astype(jnp.bfloat16)
+        rest = line - high.astype(jnp.float32)
+        middle = rest.astype(jnp.bfloat16)
+        low = (rest - middle.astype(jnp.float32)).astype(jnp.bfloat16)
+        chunks = []
+        for h in range(size // lanes):
+            spread = None
+            for part in (high, middle, low):
+                rows_of = jnp.broadcast_to(part[:, h * lanes:(h + 1) * lanes], (lanes, lanes))
+                term = lax.dot_general(
+                    eye, rows_of, (((1,), (1,)), ((), ())), preferred_element_type=jnp.float32
+                )
+                spread = term if spread is None else spread + term
+            chunks.append(spread)
+        return jnp.concatenate(chunks, axis=0)
 
     edge_col = jnp.where(block == 0, 0, lanes - 1)
     for s in range(inner_ref.shape[0] // 2):

time: 60.5 us -> 61.1 us (level)
  transfers between devices with their start and end apart: 5 -> 5, of which waited for: 0 -> 0; matrix products, arithmetic and copies ran while one was open for 11% -> 11% of each run, Pallas kernels for 25% -> 24%
where the time goes in v13:
time: 61.1 us; the launch traced here: 60.8 us
  Pallas kernels  35.2 us (58%)
  starting transfers between devices  16.7 us (27%)
  matrix products  3.62 us (6%)
  local copies, waits for them, and re-layouts  3.57 us (6%)
  other arithmetic  1.51 us (2%)
    pallas_call x1, Pallas kernels, backward_gradients(): pl.pallas_call(_backward_kernel, grid_spec=grid_spec, out_shape=[jax.Shap...  17 us
    pallas_call x1, Pallas kernels, forward_waves(): pl.pallas_call(_forward_kernel, grid=(count // group,), in_specs=[pl.Bloc...  10.9 us
    ppermute x2, starting transfers between devices, _swap(): lax.ppermute(odd_payload, axis, odd)  7.41 us
    all_to_all x1, starting transfers between devices, per_device(): lax.all_to_all(measured[0, 0], 'ty', split_axis=0, concat_axis=0, tiled=T...  6.75 us
    pallas_call x1, Pallas kernels, smooth_update(): pl.pallas_call(_inner_kernel, grid=(channels // 2,), in_specs=[plane, pla...  3.93 us
    dot_general x1, matrix products, per_device(): jnp.einsum('kcis,ksj->kcij', rows, col_pick, preferred_element_type=jnp.f...  3.62 us
    pallas_call x1, Pallas kernels, smooth_update(): pl.pallas_call(_edge_kernel, grid=(size // lanes,), in_specs=[scalars, ha...  3.3 us
    ppermute x2, starting transfers between devices, _swap(): lax.ppermute(even_payload, axis, even)  2.58 us
  transfers between devices with their start and end apart: 5, of which 0 were waited for; matrix products, arithmetic and copies ran while one was open for 11% of the time, Pallas kernels for 24%

profile of v13, /device:TPU:25, one launch (start us, length us, event | category | flops | bytes accessed | tf_op | source)
XLA Modules:
  0.0 60.8 jit_solution(14659839978424800554)
XLA Ops:
  0.0 6.8 %all-to-all-start = ((bf16[16,2,128,128]{3,2,1,0:T(8,128)(2,1)}), bf16[16,2,128,128]{3,2,1,0:T(8,128)(2,1)S(1)}, u32[]{:S(2)}, u32[]{:S(2)}) async-start(bf16[16,2,128,128]{3,2,1,0:T(8,128)(2,1)} %bitcast.45), calls=%async_computation | async-start | bytes 2097152 | tf_op jit(solution)/shard_map/all_to_all | solution.py:380
  6.8 0.2 select_reduce_fusion
  7.0 0.2 cosine_bitcast_fusion
  7.3 0.2 fusion.26
  7.5 0.2 copy.22
  7.6 0.2 copy.23
  7.8 0.1 iota_add_fusion
  7.9 0.6 concatenate.3.scalar_ref.parity_ref
  8.5 0.6 %pad_maximum_fusion.prop_ref = f32[2,128,128]{2,1,0:T(8,128)} fusion(f32[1,128,128]{2,1,0:T(8,128)S(1)} %get-tuple-element.24, f32[1,128,128]{2,1,0:T(8,128)S(1)} %get-tuple-element.23), kind=kLoop, calls=%fused_computation.13 | loop fusion | flops 32768 | bytes 262144 | tf_op jit(solution)/shard_map/stack | solution.py:398
  9.1 3.6 %fusion.10.win_ref = bf16[16,4,128,128]{3,2,1,0:T(8,128)(2,1)} fusion(s32[16,128]{1,0:T(8,128)S(1)} %get-tuple-element.27, s32[16,128]{1,0:T(8,128)S(1)} %get-tuple-element.28, f32[4,256,256]{2,1,0:T(8,128)S(1)} %copy-done), kind=kOutput, calls=%fused_computation.8 | convolution fusion | flops 1615069184 | bytes 3162112 | tf_op jit(solution)/shard_map/kcis,ksj->kcij/dot_general | solution.py:394
  12.8 10.9 %shard_map.82 = (f32[16,2,128,128]{3,2,1,0:T(8,128)}, f32[16,2,128,128]{3,2,1,0:T(8,128)}) custom-call(bf16[16,4,128,128]{3,2,1,0:T(8,128)(2,1)} %fusion.10.win_ref, f32[2,128,128]{2,1,0:T(8,128)} %probe_ref.3, f32[2,128,128]{2,1,0:T(8,128)} %pad_maximum_fusion.prop_ref, bf16[2,256,768]{2,1,0:T(8,128)(2,1)} %constant.35.clone.left_ref, ...), custom_call_target="tpu_custom_call" | custom-call | tf_op jit(solution)/shard_map/pallas_call | solution.py:315
  23.7 0.6 pad_maximum_fusion.1.border_ref
  24.3 1.0 %copy-done.1 = bf16[16,2,128,128]{3,2,1,0:T(8,128)(2,1)} copy-done((bf16[16,2,128,128]{3,2,1,0:T(8,128)(2,1)}, bf16[16,2,128,128]{3,2,1,0:T(8,128)(2,1)S(1)}, u32[]{:S(2)}) %copy-start.1) | copy-done | bytes 1048600
  25.3 17.0 %shard_map.83 = (f32[4,256,256]{2,1,0:T(8,128)}, f32[4,256]{1,0:T(4,128)}, f32[4,256]{1,0:T(4,128)}, f32[4,256]{1,0:T(4,128)}, f32[4,256]{1,0:T(4,128)}) custom-call(s32[50]{0:T(128)} %concatenate.3.scalar_ref.parity_ref, bf16[32,128,128]{2,1,0:T(8,128)(2,1)} %bitcast.44, f32[16,2,128,128]{3,2,1,0:T(8,128)} %get-tuple-element.12.far_ref, ...), custom_call_target="tpu_custom_call" | custom-call | tf_op jit(solution)/shard_map/pallas_call | solution.py:362
  42.3 1.3 %collective-permute-start = (f32[4,256]{1,0:T(4,128)}, f32[4,256]{1,0:T(4,128)S(1)}, u32[]{:S(2)}, u32[]{:S(2)}) collective-permute-start(f32[4,256]{1,0:T(4,128)} %get-tuple-element.15.row_even_ref), channel_id=1, source_target_pairs={{0,16},{32,48},{64,80},{96,112},{16,0},{48,32},{80,64},{112,96},{1... | collective-permute-start | bytes 12296 | tf_op jit(solution)/shard_map/ppermute | solution.py:26
  43.7 3.4 %collective-permute-start.1 = (f32[4,256]{1,0:T(4,128)}, f32[4,256]{1,0:T(4,128)S(1)}, u32[]{:S(2)}, u32[]{:S(2)}) collective-permute-start(f32[4,256]{1,0:T(4,128)} %get-tuple-element.16.row_odd_ref), channel_id=1, source_target_pairs={{16,32},{48,64},{80,96},{32,16},{64,48},{96,80},{17,33},{49,65},{8... | collective-permute-start | bytes 12296 | tf_op jit(solution)/shard_map/ppermute | solution.py:26
  47.1 1.3 %collective-permute-start.2 = (f32[4,256]{1,0:T(4,128)}, f32[4,256]{1,0:T(4,128)S(1)}, u32[]{:S(2)}, u32[]{:S(2)}) collective-permute-start(f32[4,256]{1,0:T(4,128)} %get-tuple-element.17.col_even_ref), channel_id=1, source_target_pairs={{0,1},{2,3},{4,5},{6,7},{8,9},{10,11},{12,13},{14,15},{1,0},{3,2},... | collective-permute-start | bytes 12296 | tf_op jit(solution)/shard_map/ppermute | solution.py:26
  48.4 4.0 %collective-permute-start.3 = (f32[4,256]{1,0:T(4,128)}, f32[4,256]{1,0:T(4,128)S(1)}, u32[]{:S(2)}, u32[]{:S(2)}) collective-permute-start(f32[4,256]{1,0:T(4,128)} %get-tuple-element.18.col_odd_ref), channel_id=1, source_target_pairs={{1,2},{3,4},{5,6},{7,8},{9,10},{11,12},{13,14},{2,1},{4,3},{6,5},{... | collective-permute-start | bytes 12296 | tf_op jit(solution)/shard_map/ppermute | solution.py:26
  52.3 3.9 %shard_map.84.inner_ref = f32[4,256,256]{2,1,0:T(8,128)} custom-call(f32[4,256,256]{2,1,0:T(8,128)} %field_ref.1, f32[4,256,256]{2,1,0:T(8,128)} %get-tuple-element.14.total_ref), custom_call_target="tpu_custom_call" | custom-call | tf_op jit(solution)/shard_map/pallas_call | solution.py:118
  56.3 0.5 copy-done.3
  56.9 0.0 copy-done.4
  56.9 0.0 copy-done.5
  56.9 0.6 copy-done.6
  57.5 3.3 %shard_map.85 = f32[4,256,256]{2,1,0:T(8,128)} custom-call(s32[50]{0:T(128)} %concatenate.3.scalar_ref.parity_ref, f32[4,256,256]{2,1,0:T(8,128)} %shard_map.84.inner_ref, f32[4,256]{1,0:T(4,128)} %get-tuple-element.15.row_even_ref, f32[4,256]{1,0:T(4,128)} %get-tuple-element.16.row_odd_ref, ...), custom_call_target="tpu_custom_call", output_to_operand_aliasing={{}: (1, {})} | custom-call | tf_op jit(solution)/shard_map/pallas_call | solution.py:130
  (22 shorter events, 0.1 us)
Async XLA Ops:
  0.0 6.8 %copy-start.8 = (s32[1,1,16,1]{2,3,1,0:T(1,128)S(1)}, s32[1,1,16,1]{2,3,1,0:T(1,128)}, u32[]{:S(2)}) copy-start(s32[1,1,16,1]{2,3,1,0:T(1,128)} %param.13) | copy-start | bytes 196
  0.0 7.0 %copy-start.7 = (s32[1,1,16,2]{2,3,1,0:T(2,128)S(1)}, s32[1,1,16,2]{2,3,1,0:T(2,128)}, u32[]{:S(2)}) copy-start(s32[1,1,16,2]{2,3,1,0:T(2,128)} %param.12) | copy-start | bytes 388
  0.0 7.0 %copy-start.2 = (f32[128,128]{1,0:T(8,128)S(1)}, f32[128,128]{1,0:T(8,128)}, u32[]{:S(2)}) copy-start(f32[128,128]{1,0:T(8,128)} %param.10) | copy-start | bytes 196612
  0.0 7.2 %copy-start = (f32[4,256,256]{2,1,0:T(8,128)S(1)}, f32[4,256,256]{2,1,0:T(8,128)}, u32[]{:S(2)}) copy-start(f32[4,256,256]{2,1,0:T(8,128)} %field_ref.1) | copy-start | bytes 3145732
  0.0 24.3 %all-to-all-start = ((bf16[16,2,128,128]{3,2,1,0:T(8,128)(2,1)}), bf16[16,2,128,128]{3,2,1,0:T(8,128)(2,1)S(1)}, u32[]{:S(2)}, u32[]{:S(2)}) async-start(bf16[16,2,128,128]{3,2,1,0:T(8,128)(2,1)} %bitcast.45), calls=%async_computation | async-start | bytes 2097152 | tf_op jit(solution)/shard_map/all_to_all | solution.py:380
  24.3 1.0 %copy-start.1 = (bf16[16,2,128,128]{3,2,1,0:T(8,128)(2,1)}, bf16[16,2,128,128]{3,2,1,0:T(8,128)(2,1)S(1)}, u32[]{:S(2)}) copy-start(bf16[16,2,128,128]{3,2,1,0:T(8,128)(2,1)S(1)} %all-to-all-done) | copy-start | bytes 3145732
  42.3 13.9 %collective-permute-start = (f32[4,256]{1,0:T(4,128)}, f32[4,256]{1,0:T(4,128)S(1)}, u32[]{:S(2)}, u32[]{:S(2)}) collective-permute-start(f32[4,256]{1,0:T(4,128)} %get-tuple-element.15.row_even_ref), channel_id=1, source_target_pairs={{0,16},{32,48},{64,80},{96,112},{16,0},{48,32},{80,64},{112,96},{1... | collective-permute-start | bytes 12296 | tf_op jit(solution)/shard_map/ppermute | solution.py:26
  43.7 12.6 %collective-permute-start.1 = (f32[4,256]{1,0:T(4,128)}, f32[4,256]{1,0:T(4,128)S(1)}, u32[]{:S(2)}, u32[]{:S(2)}) collective-permute-start(f32[4,256]{1,0:T(4,128)} %get-tuple-element.16.row_odd_ref), channel_id=1, source_target_pairs={{16,32},{48,64},{80,96},{32,16},{64,48},{96,80},{17,33},{49,65},{8... | collective-permute-start | bytes 12296 | tf_op jit(solution)/shard_map/ppermute | solution.py:26
  47.1 9.2 %collective-permute-start.2 = (f32[4,256]{1,0:T(4,128)}, f32[4,256]{1,0:T(4,128)S(1)}, u32[]{:S(2)}, u32[]{:S(2)}) collective-permute-start(f32[4,256]{1,0:T(4,128)} %get-tuple-element.17.col_even_ref), channel_id=1, source_target_pairs={{0,1},{2,3},{4,5},{6,7},{8,9},{10,11},{12,13},{14,15},{1,0},{3,2},... | collective-permute-start | bytes 12296 | tf_op jit(solution)/shard_map/ppermute | solution.py:26
  48.4 8.0 %collective-permute-start.3 = (f32[4,256]{1,0:T(4,128)}, f32[4,256]{1,0:T(4,128)S(1)}, u32[]{:S(2)}, u32[]{:S(2)}) collective-permute-start(f32[4,256]{1,0:T(4,128)} %get-tuple-element.18.col_odd_ref), channel_id=1, source_target_pairs={{1,2},{3,4},{5,6},{7,8},{9,10},{11,12},{13,14},{2,1},{4,3},{6,5},{... | collective-permute-start | bytes 12296 | tf_op jit(solution)/shard_map/ppermute | solution.py:26
  56.3 0.6 copy-start.3
  56.3 0.6 copy-start.4
  56.3 0.6 copy-start.5
  56.9 0.6 copy-start.6

commit v14 on v12

--- a/solution.py
+++ b/solution.py
@@ -300,7 +300,7 @@
             col_odd_ref[c:c + 1, :] = jnp.where(col_parity == 1, last, first)
 
 
-def forward_waves(windows, probe, kernel, tables, group=8):
+def forward_waves(windows, probe, kernel, tables, group=4):
     count, channels, width, _ = windows.shape
     group = math.gcd(count, group)
     left_tables, right_tables = tables
@@ -327,7 +327,7 @@
 
 
 def backward_gradients(scalars, amplitudes, far, incoming, windows, probe, kernel, tables, border,
-                       group=8):
+                       group=4):
     count, channels, width, _ = windows.shape
     tile = border.shape[-1]
     group = math.gcd(count, group)

time: 60.5 us -> 65.1 us (1.076)
  Pallas kernels: 34.6 us -> 39.2 us
    pallas_call x1, Pallas kernels: 17 us -> 19.7 us  [backward_gradients(): pl.pallas_call(_backward_kernel, grid_spec=grid_spec, out_shape=[jax.Shap...]
    pallas_call x1, Pallas kernels: 10.9 us -> 12.8 us  [forward_waves(): pl.pallas_call(_forward_kernel, grid=(count // group,), in_specs=[pl.Bloc...]
  transfers between devices with their start and end apart: 5 -> 5, of which waited for: 0 -> 0; matrix products, arithmetic and copies ran while one was open for 11% -> 10% of each run, Pallas kernels for 25% -> 26%
where the time goes in v14:
time: 65.1 us; the launch traced here: 64.8 us
  Pallas kernels  39.2 us (60%)
  starting transfers between devices  16.7 us (26%)
  matrix products  3.62 us (6%)
  local copies, waits for them, and re-layouts  3.57 us (5%)
  other arithmetic  1.51 us (2%)
    pallas_call x1, Pallas kernels, backward_gradients(): pl.pallas_call(_backward_kernel, grid_spec=grid_spec, out_shape=[jax.Shap...  19.7 us
    pallas_call x1, Pallas kernels, forward_waves(): pl.pallas_call(_forward_kernel, grid=(count // group,), in_specs=[pl.Bloc...  12.8 us
    ppermute x2, starting transfers between devices, _swap(): lax.ppermute(odd_payload, axis, odd)  7.41 us
    all_to_all x1, starting transfers between devices, per_device(): lax.all_to_all(measured[0, 0], 'ty', split_axis=0, concat_axis=0, tiled=T...  6.75 us
    pallas_call x1, Pallas kernels, smooth_update(): pl.pallas_call(_inner_kernel, grid=(channels // 2,), in_specs=[plane, pla...  3.93 us
    dot_general x1, matrix products, per_device(): jnp.einsum('kcis,ksj->kcij', rows, col_pick, preferred_element_type=jnp.f...  3.62 us
    pallas_call x1, Pallas kernels, smooth_update(): pl.pallas_call(_edge_kernel, grid=(size // lanes,), in_specs=[scalars, ha...  2.73 us
    ppermute x2, starting transfers between devices, _swap(): lax.ppermute(even_payload, axis, even)  2.58 us
  transfers between devices with their start and end apart: 5, of which 0 were waited for; matrix products, arithmetic and copies ran while one was open for 10% of the time, Pallas kernels for 26%

profile of v14, /device:TPU:25, one launch (start us, length us, event | category | flops | bytes accessed | tf_op | source)
XLA Modules:
  0.0 64.8 jit_solution(8234215392718357418)
XLA Ops:
  0.0 6.8 %all-to-all-start = ((bf16[16,2,128,128]{3,2,1,0:T(8,128)(2,1)}), bf16[16,2,128,128]{3,2,1,0:T(8,128)(2,1)S(1)}, u32[]{:S(2)}, u32[]{:S(2)}) async-start(bf16[16,2,128,128]{3,2,1,0:T(8,128)(2,1)} %bitcast.45), calls=%async_computation | async-start | bytes 2097152 | tf_op jit(solution)/shard_map/all_to_all | solution.py:373
  6.8 0.2 select_reduce_fusion
  7.0 0.2 cosine_bitcast_fusion
  7.3 0.2 fusion.26
  7.5 0.2 copy.22
  7.6 0.2 copy.23
  7.8 0.1 iota_add_fusion
  7.9 0.6 concatenate.3.scalar_ref.parity_ref
  8.5 0.6 pad_maximum_fusion.prop_ref
  9.1 3.6 %fusion.10.win_ref = bf16[16,4,128,128]{3,2,1,0:T(8,128)(2,1)} fusion(s32[16,128]{1,0:T(8,128)S(1)} %get-tuple-element.27, s32[16,128]{1,0:T(8,128)S(1)} %get-tuple-element.28, f32[4,256,256]{2,1,0:T(8,128)S(1)} %copy-done), kind=kOutput, calls=%fused_computation.8 | convolution fusion | flops 1615069184 | bytes 3162112 | tf_op jit(solution)/shard_map/kcis,ksj->kcij/dot_general | solution.py:387
  12.8 12.8 %shard_map.82 = (f32[16,2,128,128]{3,2,1,0:T(8,128)}, f32[16,2,128,128]{3,2,1,0:T(8,128)}) custom-call(bf16[16,4,128,128]{3,2,1,0:T(8,128)(2,1)} %fusion.10.win_ref, f32[2,128,128]{2,1,0:T(8,128)} %probe_ref.3, f32[2,128,128]{2,1,0:T(8,128)} %pad_maximum_fusion.prop_ref, bf16[2,256,768]{2,1,0:T(8,128)(2,1)} %constant.35.clone.left_ref, ...), custom_call_target="tpu_custom_call" | custom-call | tf_op jit(solution)/shard_map/pallas_call | solution.py:308
  25.6 0.6 pad_maximum_fusion.1.border_ref
  26.2 1.0 %copy-done.1 = bf16[16,2,128,128]{3,2,1,0:T(8,128)(2,1)} copy-done((bf16[16,2,128,128]{3,2,1,0:T(8,128)(2,1)}, bf16[16,2,128,128]{3,2,1,0:T(8,128)(2,1)S(1)}, u32[]{:S(2)}) %copy-start.1) | copy-done | bytes 1048600
  27.2 19.7 %shard_map.83 = (f32[4,256,256]{2,1,0:T(8,128)}, f32[4,256]{1,0:T(4,128)}, f32[4,256]{1,0:T(4,128)}, f32[4,256]{1,0:T(4,128)}, f32[4,256]{1,0:T(4,128)}) custom-call(s32[50]{0:T(128)} %concatenate.3.scalar_ref.parity_ref, bf16[32,128,128]{2,1,0:T(8,128)(2,1)} %bitcast.44, f32[16,2,128,128]{3,2,1,0:T(8,128)} %get-tuple-element.12.far_ref, ...), custom_call_target="tpu_custom_call" | custom-call | tf_op jit(solution)/shard_map/pallas_call | solution.py:355
  46.9 1.3 %collective-permute-start = (f32[4,256]{1,0:T(4,128)}, f32[4,256]{1,0:T(4,128)S(1)}, u32[]{:S(2)}, u32[]{:S(2)}) collective-permute-start(f32[4,256]{1,0:T(4,128)} %get-tuple-element.15.row_even_ref), channel_id=1, source_target_pairs={{0,16},{32,48},{64,80},{96,112},{16,0},{48,32},{80,64},{112,96},{1... | collective-permute-start | bytes 12296 | tf_op jit(solution)/shard_map/ppermute | solution.py:26
  48.2 3.4 %collective-permute-start.1 = (f32[4,256]{1,0:T(4,128)}, f32[4,256]{1,0:T(4,128)S(1)}, u32[]{:S(2)}, u32[]{:S(2)}) collective-permute-start(f32[4,256]{1,0:T(4,128)} %get-tuple-element.16.row_odd_ref), channel_id=1, source_target_pairs={{16,32},{48,64},{80,96},{32,16},{64,48},{96,80},{17,33},{49,65},{8... | collective-permute-start | bytes 12296 | tf_op jit(solution)/shard_map/ppermute | solution.py:26
  51.7 1.3 %collective-permute-start.2 = (f32[4,256]{1,0:T(4,128)}, f32[4,256]{1,0:T(4,128)S(1)}, u32[]{:S(2)}, u32[]{:S(2)}) collective-permute-start(f32[4,256]{1,0:T(4,128)} %get-tuple-element.17.col_even_ref), channel_id=1, source_target_pairs={{0,1},{2,3},{4,5},{6,7},{8,9},{10,11},{12,13},{14,15},{1,0},{3,2},... | collective-permute-start | bytes 12296 | tf_op jit(solution)/shard_map/ppermute | solution.py:26
  52.9 4.0 %collective-permute-start.3 = (f32[4,256]{1,0:T(4,128)}, f32[4,256]{1,0:T(4,128)S(1)}, u32[]{:S(2)}, u32[]{:S(2)}) collective-permute-start(f32[4,256]{1,0:T(4,128)} %get-tuple-element.18.col_odd_ref), channel_id=1, source_target_pairs={{1,2},{3,4},{5,6},{7,8},{9,10},{11,12},{13,14},{2,1},{4,3},{6,5},{... | collective-permute-start | bytes 12296 | tf_op jit(solution)/shard_map/ppermute | solution.py:26
  56.9 3.9 %shard_map.84.inner_ref = f32[4,256,256]{2,1,0:T(8,128)} custom-call(f32[4,256,256]{2,1,0:T(8,128)} %field_ref.1, f32[4,256,256]{2,1,0:T(8,128)} %get-tuple-element.14.total_ref), custom_call_target="tpu_custom_call" | custom-call | tf_op jit(solution)/shard_map/pallas_call | solution.py:111
  60.9 0.5 copy-done.3
  61.4 0.0 copy-done.4
  61.4 0.0 copy-done.5
  61.5 0.6 copy-done.6
  62.1 2.7 %shard_map.85 = f32[4,256,256]{2,1,0:T(8,128)} custom-call(s32[50]{0:T(128)} %concatenate.3.scalar_ref.parity_ref, f32[4,256,256]{2,1,0:T(8,128)} %shard_map.84.inner_ref, f32[4,256]{1,0:T(4,128)} %get-tuple-element.15.row_even_ref, f32[4,256]{1,0:T(4,128)} %get-tuple-element.16.row_odd_ref, ...), custom_call_target="tpu_custom_call", output_to_operand_aliasing={{}: (1, {})} | custom-call | tf_op jit(solution)/shard_map/pallas_call | solution.py:123
  (22 shorter events, 0.1 us)
Async XLA Ops:
  0.0 6.8 %copy-start.8 = (s32[1,1,16,1]{2,3,1,0:T(1,128)S(1)}, s32[1,1,16,1]{2,3,1,0:T(1,128)}, u32[]{:S(2)}) copy-start(s32[1,1,16,1]{2,3,1,0:T(1,128)} %param.13) | copy-start | bytes 196
  0.0 7.0 %copy-start.7 = (s32[1,1,16,2]{2,3,1,0:T(2,128)S(1)}, s32[1,1,16,2]{2,3,1,0:T(2,128)}, u32[]{:S(2)}) copy-start(s32[1,1,16,2]{2,3,1,0:T(2,128)} %param.12) | copy-start | bytes 388
  0.0 7.0 %copy-start.2 = (f32[128,128]{1,0:T(8,128)S(1)}, f32[128,128]{1,0:T(8,128)}, u32[]{:S(2)}) copy-start(f32[128,128]{1,0:T(8,128)} %param.10) | copy-start | bytes 196612
  0.0 7.2 %copy-start = (f32[4,256,256]{2,1,0:T(8,128)S(1)}, f32[4,256,256]{2,1,0:T(8,128)}, u32[]{:S(2)}) copy-start(f32[4,256,256]{2,1,0:T(8,128)} %field_ref.1) | copy-start | bytes 3145732
  0.0 26.2 %all-to-all-start = ((bf16[16,2,128,128]{3,2,1,0:T(8,128)(2,1)}), bf16[16,2,128,128]{3,2,1,0:T(8,128)(2,1)S(1)}, u32[]{:S(2)}, u32[]{:S(2)}) async-start(bf16[16,2,128,128]{3,2,1,0:T(8,128)(2,1)} %bitcast.45), calls=%async_computation | async-start | bytes 2097152 | tf_op jit(solution)/shard_map/all_to_all | solution.py:373
  26.2 1.0 %copy-start.1 = (bf16[16,2,128,128]{3,2,1,0:T(8,128)(2,1)}, bf16[16,2,128,128]{3,2,1,0:T(8,128)(2,1)S(1)}, u32[]{:S(2)}) copy-start(bf16[16,2,128,128]{3,2,1,0:T(8,128)(2,1)S(1)} %all-to-all-done) | copy-start | bytes 3145732
  46.9 13.9 %collective-permute-start = (f32[4,256]{1,0:T(4,128)}, f32[4,256]{1,0:T(4,128)S(1)}, u32[]{:S(2)}, u32[]{:S(2)}) collective-permute-start(f32[4,256]{1,0:T(4,128)} %get-tuple-element.15.row_even_ref), channel_id=1, source_target_pairs={{0,16},{32,48},{64,80},{96,112},{16,0},{48,32},{80,64},{112,96},{1... | collective-permute-start | bytes 12296 | tf_op jit(solution)/shard_map/ppermute | solution.py:26
  48.2 12.6 %collective-permute-start.1 = (f32[4,256]{1,0:T(4,128)}, f32[4,256]{1,0:T(4,128)S(1)}, u32[]{:S(2)}, u32[]{:S(2)}) collective-permute-start(f32[4,256]{1,0:T(4,128)} %get-tuple-element.16.row_odd_ref), channel_id=1, source_target_pairs={{16,32},{48,64},{80,96},{32,16},{64,48},{96,80},{17,33},{49,65},{8... | collective-permute-start | bytes 12296 | tf_op jit(solution)/shard_map/ppermute | solution.py:26
  51.7 9.2 %collective-permute-start.2 = (f32[4,256]{1,0:T(4,128)}, f32[4,256]{1,0:T(4,128)S(1)}, u32[]{:S(2)}, u32[]{:S(2)}) collective-permute-start(f32[4,256]{1,0:T(4,128)} %get-tuple-element.17.col_even_ref), channel_id=1, source_target_pairs={{0,1},{2,3},{4,5},{6,7},{8,9},{10,11},{12,13},{14,15},{1,0},{3,2},... | collective-permute-start | bytes 12296 | tf_op jit(solution)/shard_map/ppermute | solution.py:26
  52.9 8.0 %collective-permute-start.3 = (f32[4,256]{1,0:T(4,128)}, f32[4,256]{1,0:T(4,128)S(1)}, u32[]{:S(2)}, u32[]{:S(2)}) collective-permute-start(f32[4,256]{1,0:T(4,128)} %get-tuple-element.18.col_odd_ref), channel_id=1, source_target_pairs={{1,2},{3,4},{5,6},{7,8},{9,10},{11,12},{13,14},{2,1},{4,3},{6,5},{... | collective-permute-start | bytes 12296 | tf_op jit(solution)/shard_map/ppermute | solution.py:26
  60.8 0.6 copy-start.3
  60.9 0.6 copy-start.4
  60.9 0.6 copy-start.5
  61.5 0.6 copy-start.6

commit v15 on v14

--- a/solution.py
+++ b/solution.py
@@ -300,7 +300,7 @@
             col_odd_ref[c:c + 1, :] = jnp.where(col_parity == 1, last, first)
 
 
-def forward_waves(windows, probe, kernel, tables, group=4):
+def forward_waves(windows, probe, kernel, tables, group=16):
     count, channels, width, _ = windows.shape
     group = math.gcd(count, group)
     left_tables, right_tables = tables
@@ -327,7 +327,7 @@
 
 
 def backward_gradients(scalars, amplitudes, far, incoming, windows, probe, kernel, tables, border,
-                       group=4):
+                       group=16):
     count, channels, width, _ = windows.shape
     tile = border.shape[-1]
     group = math.gcd(count, group)

time: 65.1 us -> 59.5 us (0.914)
  Pallas kernels: 39.2 us -> 33.8 us
    pallas_call x1, Pallas kernels: 19.7 us -> 16.1 us  [backward_gradients(): pl.pallas_call(_backward_kernel, grid_spec=grid_spec, out_shape=[jax.Shap...]
    pallas_call x1, Pallas kernels: 12.8 us -> 11 us  [forward_waves(): pl.pallas_call(_forward_kernel, grid=(count // group,), in_specs=[pl.Bloc...]
  transfers between devices with their start and end apart: 5 -> 5, of which waited for: 0 -> 0; matrix products, arithmetic and copies ran while one was open for 10% -> 11% of each run, Pallas kernels for 26% -> 25%
where the time goes in v15:
time: 59.5 us; the launch traced here: 59.2 us
  Pallas kernels  33.8 us (57%)
  starting transfers between devices  16.7 us (28%)
  matrix products  3.62 us (6%)
  local copies, waits for them, and re-layouts  3.57 us (6%)
  other arithmetic  1.51 us (3%)
    pallas_call x1, Pallas kernels, backward_gradients(): pl.pallas_call(_backward_kernel, grid_spec=grid_spec, out_shape=[jax.Shap...  16.1 us
    pallas_call x1, Pallas kernels, forward_waves(): pl.pallas_call(_forward_kernel, grid=(count // group,), in_specs=[pl.Bloc...  11 us
    ppermute x2, starting transfers between devices, _swap(): lax.ppermute(odd_payload, axis, odd)  7.4 us
    all_to_all x1, starting transfers between devices, per_device(): lax.all_to_all(measured[0, 0], 'ty', split_axis=0, concat_axis=0, tiled=T...  6.75 us
    pallas_call x1, Pallas kernels, smooth_update(): pl.pallas_call(_inner_kernel, grid=(channels // 2,), in_specs=[plane, pla...  3.93 us
    dot_general x1, matrix products, per_device(): jnp.einsum('kcis,ksj->kcij', rows, col_pick, preferred_element_type=jnp.f...  3.62 us
    pallas_call x1, Pallas kernels, smooth_update(): pl.pallas_call(_edge_kernel, grid=(size // lanes,), in_specs=[scalars, ha...  2.73 us
    unnamed x20, local copies, waits for them, and re-layouts  2.53 us
  transfers between devices with their start and end apart: 5, of which 0 were waited for; matrix products, arithmetic and copies ran while one was open for 11% of the time, Pallas kernels for 25%

profile of v15, /device:TPU:25, one launch (start us, length us, event | category | flops | bytes accessed | tf_op | source)
XLA Modules:
  0.0 59.2 jit_solution(5518901848110965399)
XLA Ops:
  0.0 6.8 %all-to-all-start = ((bf16[16,2,128,128]{3,2,1,0:T(8,128)(2,1)}), bf16[16,2,128,128]{3,2,1,0:T(8,128)(2,1)S(1)}, u32[]{:S(2)}, u32[]{:S(2)}) async-start(bf16[16,2,128,128]{3,2,1,0:T(8,128)(2,1)} %bitcast.45), calls=%async_computation | async-start | bytes 2097152 | tf_op jit(solution)/shard_map/all_to_all | solution.py:373
  6.8 0.2 select_reduce_fusion
  7.0 0.2 cosine_bitcast_fusion
  7.3 0.2 fusion.26
  7.5 0.2 copy.22
  7.6 0.2 copy.23
  7.8 0.1 iota_add_fusion
  7.9 0.6 concatenate.3.scalar_ref.parity_ref
  8.5 0.6 %pad_maximum_fusion.prop_ref = f32[2,128,128]{2,1,0:T(8,128)} fusion(f32[1,128,128]{2,1,0:T(8,128)S(1)} %get-tuple-element.24, f32[1,128,128]{2,1,0:T(8,128)S(1)} %get-tuple-element.23), kind=kLoop, calls=%fused_computation.13 | loop fusion | flops 32768 | bytes 262144 | tf_op jit(solution)/shard_map/stack | solution.py:391
  9.1 3.6 %fusion.10.win_ref = bf16[16,4,128,128]{3,2,1,0:T(8,128)(2,1)} fusion(s32[16,128]{1,0:T(8,128)S(1)} %get-tuple-element.27, s32[16,128]{1,0:T(8,128)S(1)} %get-tuple-element.28, f32[4,256,256]{2,1,0:T(8,128)S(1)} %copy-done), kind=kOutput, calls=%fused_computation.8 | convolution fusion | flops 1615069184 | bytes 3162112 | tf_op jit(solution)/shard_map/kcis,ksj->kcij/dot_general | solution.py:387
  12.8 11.0 %shard_map.82 = (f32[16,2,128,128]{3,2,1,0:T(8,128)}, f32[16,2,128,128]{3,2,1,0:T(8,128)}) custom-call(bf16[16,4,128,128]{3,2,1,0:T(8,128)(2,1)} %fusion.10.win_ref, f32[2,128,128]{2,1,0:T(8,128)} %probe_ref.3, f32[2,128,128]{2,1,0:T(8,128)} %pad_maximum_fusion.prop_ref, bf16[2,256,768]{2,1,0:T(8,128)(2,1)} %constant.35.clone.left_ref, ...), custom_call_target="tpu_custom_call" | custom-call | tf_op jit(solution)/shard_map/pallas_call | solution.py:308
  23.8 0.6 %pad_maximum_fusion.1.border_ref = f32[4,4,256]{2,1,0:T(4,128)} fusion(f32[1,4,256]{2,1,0:T(4,128)S(1)} %bitcast.47, f32[1,4,256]{2,1,0:T(4,128)S(1)} %bitcast.46, f32[1,4,256]{2,1,0:T(4,128)S(1)} %get-tuple-element.29, f32[1,4,256]{2,1,0:T(4,128)S(1)} %get-tuple-element.30), kind=kLoop, calls=%fused_computation.16 | loop fusion | flops 12288 | bytes 32768 | tf_op jit(solution)/shard_map/stack | solution.py:395
  24.4 1.0 %copy-done.1 = bf16[16,2,128,128]{3,2,1,0:T(8,128)(2,1)} copy-done((bf16[16,2,128,128]{3,2,1,0:T(8,128)(2,1)}, bf16[16,2,128,128]{3,2,1,0:T(8,128)(2,1)S(1)}, u32[]{:S(2)}) %copy-start.1) | copy-done | bytes 1048600
  25.4 16.1 %shard_map.83 = (f32[4,256,256]{2,1,0:T(8,128)}, f32[4,256]{1,0:T(4,128)}, f32[4,256]{1,0:T(4,128)}, f32[4,256]{1,0:T(4,128)}, f32[4,256]{1,0:T(4,128)}) custom-call(s32[50]{0:T(128)} %concatenate.3.scalar_ref.parity_ref, bf16[32,128,128]{2,1,0:T(8,128)(2,1)} %bitcast.44, f32[16,2,128,128]{3,2,1,0:T(8,128)} %get-tuple-element.12.far_ref, ...), custom_call_target="tpu_custom_call" | custom-call | tf_op jit(solution)/shard_map/pallas_call | solution.py:355
  41.4 1.2 %collective-permute-start = (f32[4,256]{1,0:T(4,128)}, f32[4,256]{1,0:T(4,128)S(1)}, u32[]{:S(2)}, u32[]{:S(2)}) collective-permute-start(f32[4,256]{1,0:T(4,128)} %get-tuple-element.15.row_even_ref), channel_id=1, source_target_pairs={{0,16},{32,48},{64,80},{96,112},{16,0},{48,32},{80,64},{112,96},{1... | collective-permute-start | bytes 12296 | tf_op jit(solution)/shard_map/ppermute | solution.py:26
  42.7 3.4 %collective-permute-start.1 = (f32[4,256]{1,0:T(4,128)}, f32[4,256]{1,0:T(4,128)S(1)}, u32[]{:S(2)}, u32[]{:S(2)}) collective-permute-start(f32[4,256]{1,0:T(4,128)} %get-tuple-element.16.row_odd_ref), channel_id=1, source_target_pairs={{16,32},{48,64},{80,96},{32,16},{64,48},{96,80},{17,33},{49,65},{8... | collective-permute-start | bytes 12296 | tf_op jit(solution)/shard_map/ppermute | solution.py:26
  46.1 1.3 %collective-permute-start.2 = (f32[4,256]{1,0:T(4,128)}, f32[4,256]{1,0:T(4,128)S(1)}, u32[]{:S(2)}, u32[]{:S(2)}) collective-permute-start(f32[4,256]{1,0:T(4,128)} %get-tuple-element.17.col_even_ref), channel_id=1, source_target_pairs={{0,1},{2,3},{4,5},{6,7},{8,9},{10,11},{12,13},{14,15},{1,0},{3,2},... | collective-permute-start | bytes 12296 | tf_op jit(solution)/shard_map/ppermute | solution.py:26
  47.4 4.0 %collective-permute-start.3 = (f32[4,256]{1,0:T(4,128)}, f32[4,256]{1,0:T(4,128)S(1)}, u32[]{:S(2)}, u32[]{:S(2)}) collective-permute-start(f32[4,256]{1,0:T(4,128)} %get-tuple-element.18.col_odd_ref), channel_id=1, source_target_pairs={{1,2},{3,4},{5,6},{7,8},{9,10},{11,12},{13,14},{2,1},{4,3},{6,5},{... | collective-permute-start | bytes 12296 | tf_op jit(solution)/shard_map/ppermute | solution.py:26
  51.4 3.9 %shard_map.84.inner_ref = f32[4,256,256]{2,1,0:T(8,128)} custom-call(f32[4,256,256]{2,1,0:T(8,128)} %field_ref.1, f32[4,256,256]{2,1,0:T(8,128)} %get-tuple-element.14.total_ref), custom_call_target="tpu_custom_call" | custom-call | tf_op jit(solution)/shard_map/pallas_call | solution.py:111
  55.4 0.5 copy-done.3
  55.9 0.0 copy-done.4
  55.9 0.0 copy-done.5
  55.9 0.6 copy-done.6
  56.5 2.7 %shard_map.85 = f32[4,256,256]{2,1,0:T(8,128)} custom-call(s32[50]{0:T(128)} %concatenate.3.scalar_ref.parity_ref, f32[4,256,256]{2,1,0:T(8,128)} %shard_map.84.inner_ref, f32[4,256]{1,0:T(4,128)} %get-tuple-element.15.row_even_ref, f32[4,256]{1,0:T(4,128)} %get-tuple-element.16.row_odd_ref, ...), custom_call_target="tpu_custom_call", output_to_operand_aliasing={{}: (1, {})} | custom-call | tf_op jit(solution)/shard_map/pallas_call | solution.py:123
  (22 shorter events, 0.1 us)
Async XLA Ops:
  0.0 6.8 %copy-start.8 = (s32[1,1,16,1]{2,3,1,0:T(1,128)S(1)}, s32[1,1,16,1]{2,3,1,0:T(1,128)}, u32[]{:S(2)}) copy-start(s32[1,1,16,1]{2,3,1,0:T(1,128)} %param.13) | copy-start | bytes 196
  0.0 7.0 %copy-start.7 = (s32[1,1,16,2]{2,3,1,0:T(2,128)S(1)}, s32[1,1,16,2]{2,3,1,0:T(2,128)}, u32[]{:S(2)}) copy-start(s32[1,1,16,2]{2,3,1,0:T(2,128)} %param.12) | copy-start | bytes 388
  0.0 7.0 %copy-start.2 = (f32[128,128]{1,0:T(8,128)S(1)}, f32[128,128]{1,0:T(8,128)}, u32[]{:S(2)}) copy-start(f32[128,128]{1,0:T(8,128)} %param.10) | copy-start | bytes 196612
  0.0 7.2 %copy-start = (f32[4,256,256]{2,1,0:T(8,128)S(1)}, f32[4,256,256]{2,1,0:T(8,128)}, u32[]{:S(2)}) copy-start(f32[4,256,256]{2,1,0:T(8,128)} %field_ref.1) | copy-start | bytes 3145732
  0.0 24.4 %all-to-all-start = ((bf16[16,2,128,128]{3,2,1,0:T(8,128)(2,1)}), bf16[16,2,128,128]{3,2,1,0:T(8,128)(2,1)S(1)}, u32[]{:S(2)}, u32[]{:S(2)}) async-start(bf16[16,2,128,128]{3,2,1,0:T(8,128)(2,1)} %bitcast.45), calls=%async_computation | async-start | bytes 2097152 | tf_op jit(solution)/shard_map/all_to_all | solution.py:373
  24.4 1.0 %copy-start.1 = (bf16[16,2,128,128]{3,2,1,0:T(8,128)(2,1)}, bf16[16,2,128,128]{3,2,1,0:T(8,128)(2,1)S(1)}, u32[]{:S(2)}) copy-start(bf16[16,2,128,128]{3,2,1,0:T(8,128)(2,1)S(1)} %all-to-all-done) | copy-start | bytes 3145732
  41.4 13.9 %collective-permute-start = (f32[4,256]{1,0:T(4,128)}, f32[4,256]{1,0:T(4,128)S(1)}, u32[]{:S(2)}, u32[]{:S(2)}) collective-permute-start(f32[4,256]{1,0:T(4,128)} %get-tuple-element.15.row_even_ref), channel_id=1, source_target_pairs={{0,16},{32,48},{64,80},{96,112},{16,0},{48,32},{80,64},{112,96},{1... | collective-permute-start | bytes 12296 | tf_op jit(solution)/shard_map/ppermute | solution.py:26
  42.7 12.6 %collective-permute-start.1 = (f32[4,256]{1,0:T(4,128)}, f32[4,256]{1,0:T(4,128)S(1)}, u32[]{:S(2)}, u32[]{:S(2)}) collective-permute-start(f32[4,256]{1,0:T(4,128)} %get-tuple-element.16.row_odd_ref), channel_id=1, source_target_pairs={{16,32},{48,64},{80,96},{32,16},{64,48},{96,80},{17,33},{49,65},{8... | collective-permute-start | bytes 12296 | tf_op jit(solution)/shard_map/ppermute | solution.py:26
  46.1 9.2 %collective-permute-start.2 = (f32[4,256]{1,0:T(4,128)}, f32[4,256]{1,0:T(4,128)S(1)}, u32[]{:S(2)}, u32[]{:S(2)}) collective-permute-start(f32[4,256]{1,0:T(4,128)} %get-tuple-element.17.col_even_ref), channel_id=1, source_target_pairs={{0,1},{2,3},{4,5},{6,7},{8,9},{10,11},{12,13},{14,15},{1,0},{3,2},... | collective-permute-start | bytes 12296 | tf_op jit(solution)/shard_map/ppermute | solution.py:26
  47.4 8.0 %collective-permute-start.3 = (f32[4,256]{1,0:T(4,128)}, f32[4,256]{1,0:T(4,128)S(1)}, u32[]{:S(2)}, u32[]{:S(2)}) collective-permute-start(f32[4,256]{1,0:T(4,128)} %get-tuple-element.18.col_odd_ref), channel_id=1, source_target_pairs={{1,2},{3,4},{5,6},{7,8},{9,10},{11,12},{13,14},{2,1},{4,3},{6,5},{... | collective-permute-start | bytes 12296 | tf_op jit(solution)/shard_map/ppermute | solution.py:26
  55.3 0.6 copy-start.3
  55.3 0.6 copy-start.4
  55.3 0.6 copy-start.5
  55.9 0.6 copy-start.6

commit v16 on v15

--- a/solution.py
+++ b/solution.py
@@ -35,23 +35,24 @@
     size = field_ref.shape[-1]
     rows = lax.broadcasted_iota(jnp.int32, (size, size), 0)
     cols = lax.broadcasted_iota(jnp.int32, (size, size), 1)
-    centers = [field_ref[p] - step_rate * total_ref[p] for p in range(2)]
-    views = []
-    for v in centers:
-        views.append((
-            jnp.where(rows == size - 1, v, pltpu.roll(v, size - 1, 0)),
-            jnp.where(rows == 0, v, pltpu.roll(v, 1, 0)),
-            jnp.where(cols == size - 1, v, pltpu.roll(v, size - 1, 1)),
-            jnp.where(cols == 0, v, pltpu.roll(v, 1, 1)),
-        ))
-    total_r = jnp.zeros_like(centers[0])
-    total_i = jnp.zeros_like(centers[1])
-    for n in range(4):
-        bent = _bend(views[0][n] - centers[0], views[1][n] - centers[1])
-        total_r = total_r + bent[0]
-        total_i = total_i + bent[1]
-    out_ref[0] = centers[0] + smooth_rate * total_r
-    out_ref[1] = centers[1] + smooth_rate * total_i
+    for s in range(field_ref.shape[0] // 2):
+        centers = [field_ref[2 * s + p] - step_rate * total_ref[2 * s + p] for p in range(2)]
+        views = []
+        for v in centers:
+            views.append((
+                jnp.where(rows == size - 1, v, pltpu.roll(v, size - 1, 0)),
+                jnp.where(rows == 0, v, pltpu.roll(v, 1, 0)),
+                jnp.where(cols == size - 1, v, pltpu.roll(v, size - 1, 1)),
+                jnp.where(cols == 0, v, pltpu.roll(v, 1, 1)),
+            ))
+        total_r = jnp.zeros_like(centers[0])
+        total_i = jnp.zeros_like(centers[1])
+        for n in range(4):
+            bent = _bend(views[0][n] - centers[0], views[1][n] - centers[1])
+            total_r = total_r + bent[0]
+            total_i = total_i + bent[1]
+        out_ref[2 * s] = centers[0] + smooth_rate * total_r
+        out_ref[2 * s + 1] = centers[1] + smooth_rate * total_i
 
 
 def _edge_kernel(parity_ref, inner_ref, row_even_ref, row_odd_ref, col_even_ref, col_odd_ref,
@@ -107,10 +108,10 @@
 
 def smooth_update(field, total, parity, payloads, received):
     channels, size, _ = field.shape
-    plane = pl.BlockSpec((2, size, size), lambda s: (s, 0, 0))
+    plane = pl.BlockSpec((channels, size, size), lambda s: (0, 0, 0))
     inner = pl.pallas_call(
         _inner_kernel,
-        grid=(channels // 2,),
+        grid=(1,),
         in_specs=[plane, plane],
         out_specs=plane,
         out_shape=jax.ShapeDtypeStruct(field.shape, jnp.float32),

time: 59.5 us -> 59.9 us (level)
  transfers between devices with their start and end apart: 5 -> 5, of which waited for: 0 -> 0; matrix products, arithmetic and copies ran while one was open for 11% -> 11% of each run, Pallas kernels for 25% -> 26%
where the time goes in v16:
time: 59.9 us; the launch traced here: 59.7 us
  Pallas kernels  34.2 us (57%)
  starting transfers between devices  16.7 us (28%)
  matrix products  3.62 us (6%)
  local copies, waits for them, and re-layouts  3.57 us (6%)
  other arithmetic  1.51 us (3%)
    pallas_call x1, Pallas kernels, backward_gradients(): pl.pallas_call(_backward_kernel, grid_spec=grid_spec, out_shape=[jax.Shap...  16.1 us
    pallas_call x1, Pallas kernels, forward_waves(): pl.pallas_call(_forward_kernel, grid=(count // group,), in_specs=[pl.Bloc...  11 us
    ppermute x2, starting transfers between devices, _swap(): lax.ppermute(odd_payload, axis, odd)  7.4 us
    all_to_all x1, starting transfers between devices, per_device(): lax.all_to_all(measured[0, 0], 'ty', split_axis=0, concat_axis=0, tiled=T...  6.75 us
    pallas_call x1, Pallas kernels, smooth_update(): pl.pallas_call(_inner_kernel, grid=(1,), in_specs=[plane, plane], out_spe...  4.34 us
    dot_general x1, matrix products, per_device(): jnp.einsum('kcis,ksj->kcij', rows, col_pick, preferred_element_type=jnp.f...  3.62 us
    pallas_call x1, Pallas kernels, smooth_update(): pl.pallas_call(_edge_kernel, grid=(size // lanes,), in_specs=[scalars, ha...  2.73 us
    unnamed x20, local copies, waits for them, and re-layouts  2.53 us
  transfers between devices with their start and end apart: 5, of which 0 were waited for; matrix products, arithmetic and copies ran while one was open for 11% of the time, Pallas kernels for 26%

profile of v16, /device:TPU:25, one launch (start us, length us, event | category | flops | bytes accessed | tf_op | source)
XLA Modules:
  0.0 59.7 jit_solution(6132904136016299348)
XLA Ops:
  0.0 6.8 %all-to-all-start = ((bf16[16,2,128,128]{3,2,1,0:T(8,128)(2,1)}), bf16[16,2,128,128]{3,2,1,0:T(8,128)(2,1)S(1)}, u32[]{:S(2)}, u32[]{:S(2)}) async-start(bf16[16,2,128,128]{3,2,1,0:T(8,128)(2,1)} %bitcast.45), calls=%async_computation | async-start | bytes 2097152 | tf_op jit(solution)/shard_map/all_to_all | solution.py:374
  6.8 0.2 select_reduce_fusion
  7.0 0.2 cosine_bitcast_fusion
  7.3 0.2 fusion.26
  7.5 0.2 copy.22
  7.6 0.2 copy.23
  7.8 0.1 iota_add_fusion
  7.9 0.6 concatenate.3.scalar_ref.parity_ref
  8.5 0.6 %pad_maximum_fusion.prop_ref = f32[2,128,128]{2,1,0:T(8,128)} fusion(f32[1,128,128]{2,1,0:T(8,128)S(1)} %get-tuple-element.24, f32[1,128,128]{2,1,0:T(8,128)S(1)} %get-tuple-element.23), kind=kLoop, calls=%fused_computation.13 | loop fusion | flops 32768 | bytes 262144 | tf_op jit(solution)/shard_map/stack | solution.py:392
  9.1 3.6 %fusion.10.win_ref = bf16[16,4,128,128]{3,2,1,0:T(8,128)(2,1)} fusion(s32[16,128]{1,0:T(8,128)S(1)} %get-tuple-element.27, s32[16,128]{1,0:T(8,128)S(1)} %get-tuple-element.28, f32[4,256,256]{2,1,0:T(8,128)S(1)} %copy-done), kind=kOutput, calls=%fused_computation.8 | convolution fusion | flops 1615069184 | bytes 3162112 | tf_op jit(solution)/shard_map/kcis,ksj->kcij/dot_general | solution.py:388
  12.8 11.0 %shard_map.82 = (f32[16,2,128,128]{3,2,1,0:T(8,128)}, f32[16,2,128,128]{3,2,1,0:T(8,128)}) custom-call(bf16[16,4,128,128]{3,2,1,0:T(8,128)(2,1)} %fusion.10.win_ref, f32[2,128,128]{2,1,0:T(8,128)} %probe_ref.3, f32[2,128,128]{2,1,0:T(8,128)} %pad_maximum_fusion.prop_ref, bf16[2,256,768]{2,1,0:T(8,128)(2,1)} %constant.35.clone.left_ref, ...), custom_call_target="tpu_custom_call" | custom-call | tf_op jit(solution)/shard_map/pallas_call | solution.py:309
  23.8 0.6 %pad_maximum_fusion.1.border_ref = f32[4,4,256]{2,1,0:T(4,128)} fusion(f32[1,4,256]{2,1,0:T(4,128)S(1)} %bitcast.47, f32[1,4,256]{2,1,0:T(4,128)S(1)} %bitcast.46, f32[1,4,256]{2,1,0:T(4,128)S(1)} %get-tuple-element.29, f32[1,4,256]{2,1,0:T(4,128)S(1)} %get-tuple-element.30), kind=kLoop, calls=%fused_computation.16 | loop fusion | flops 12288 | bytes 32768 | tf_op jit(solution)/shard_map/stack | solution.py:396
  24.4 1.0 %copy-done.1 = bf16[16,2,128,128]{3,2,1,0:T(8,128)(2,1)} copy-done((bf16[16,2,128,128]{3,2,1,0:T(8,128)(2,1)}, bf16[16,2,128,128]{3,2,1,0:T(8,128)(2,1)S(1)}, u32[]{:S(2)}) %copy-start.1) | copy-done | bytes 1048600
  25.4 16.1 %shard_map.83 = (f32[4,256,256]{2,1,0:T(8,128)}, f32[4,256]{1,0:T(4,128)}, f32[4,256]{1,0:T(4,128)}, f32[4,256]{1,0:T(4,128)}, f32[4,256]{1,0:T(4,128)}) custom-call(s32[50]{0:T(128)} %concatenate.3.scalar_ref.parity_ref, bf16[32,128,128]{2,1,0:T(8,128)(2,1)} %bitcast.44, f32[16,2,128,128]{3,2,1,0:T(8,128)} %get-tuple-element.12.far_ref, ...), custom_call_target="tpu_custom_call" | custom-call | tf_op jit(solution)/shard_map/pallas_call | solution.py:356
  41.4 1.2 %collective-permute-start = (f32[4,256]{1,0:T(4,128)}, f32[4,256]{1,0:T(4,128)S(1)}, u32[]{:S(2)}, u32[]{:S(2)}) collective-permute-start(f32[4,256]{1,0:T(4,128)} %get-tuple-element.15.row_even_ref), channel_id=1, source_target_pairs={{0,16},{32,48},{64,80},{96,112},{16,0},{48,32},{80,64},{112,96},{1... | collective-permute-start | bytes 12296 | tf_op jit(solution)/shard_map/ppermute | solution.py:26
  42.7 3.4 %collective-permute-start.1 = (f32[4,256]{1,0:T(4,128)}, f32[4,256]{1,0:T(4,128)S(1)}, u32[]{:S(2)}, u32[]{:S(2)}) collective-permute-start(f32[4,256]{1,0:T(4,128)} %get-tuple-element.16.row_odd_ref), channel_id=1, source_target_pairs={{16,32},{48,64},{80,96},{32,16},{64,48},{96,80},{17,33},{49,65},{8... | collective-permute-start | bytes 12296 | tf_op jit(solution)/shard_map/ppermute | solution.py:26
  46.1 1.3 %collective-permute-start.2 = (f32[4,256]{1,0:T(4,128)}, f32[4,256]{1,0:T(4,128)S(1)}, u32[]{:S(2)}, u32[]{:S(2)}) collective-permute-start(f32[4,256]{1,0:T(4,128)} %get-tuple-element.17.col_even_ref), channel_id=1, source_target_pairs={{0,1},{2,3},{4,5},{6,7},{8,9},{10,11},{12,13},{14,15},{1,0},{3,2},... | collective-permute-start | bytes 12296 | tf_op jit(solution)/shard_map/ppermute | solution.py:26
  47.4 4.0 %collective-permute-start.3 = (f32[4,256]{1,0:T(4,128)}, f32[4,256]{1,0:T(4,128)S(1)}, u32[]{:S(2)}, u32[]{:S(2)}) collective-permute-start(f32[4,256]{1,0:T(4,128)} %get-tuple-element.18.col_odd_ref), channel_id=1, source_target_pairs={{1,2},{3,4},{5,6},{7,8},{9,10},{11,12},{13,14},{2,1},{4,3},{6,5},{... | collective-permute-start | bytes 12296 | tf_op jit(solution)/shard_map/ppermute | solution.py:26
  51.4 4.3 %shard_map.84.inner_ref = f32[4,256,256]{2,1,0:T(8,128)} custom-call(f32[4,256,256]{2,1,0:T(8,128)} %field_ref.1, f32[4,256,256]{2,1,0:T(8,128)} %get-tuple-element.14.total_ref), custom_call_target="tpu_custom_call" | custom-call | tf_op jit(solution)/shard_map/pallas_call | solution.py:112
  55.8 0.5 copy-done.3
  56.3 0.0 copy-done.4
  56.3 0.0 copy-done.5
  56.3 0.6 copy-done.6
  56.9 2.7 %shard_map.85 = f32[4,256,256]{2,1,0:T(8,128)} custom-call(s32[50]{0:T(128)} %concatenate.3.scalar_ref.parity_ref, f32[4,256,256]{2,1,0:T(8,128)} %shard_map.84.inner_ref, f32[4,256]{1,0:T(4,128)} %get-tuple-element.15.row_even_ref, f32[4,256]{1,0:T(4,128)} %get-tuple-element.16.row_odd_ref, ...), custom_call_target="tpu_custom_call", output_to_operand_aliasing={{}: (1, {})} | custom-call | tf_op jit(solution)/shard_map/pallas_call | solution.py:124
  (22 shorter events, 0.1 us)
Async XLA Ops:
  0.0 6.8 %copy-start.8 = (s32[1,1,16,1]{2,3,1,0:T(1,128)S(1)}, s32[1,1,16,1]{2,3,1,0:T(1,128)}, u32[]{:S(2)}) copy-start(s32[1,1,16,1]{2,3,1,0:T(1,128)} %param.13) | copy-start | bytes 196
  0.0 7.0 %copy-start.7 = (s32[1,1,16,2]{2,3,1,0:T(2,128)S(1)}, s32[1,1,16,2]{2,3,1,0:T(2,128)}, u32[]{:S(2)}) copy-start(s32[1,1,16,2]{2,3,1,0:T(2,128)} %param.12) | copy-start | bytes 388
  0.0 7.0 %copy-start.2 = (f32[128,128]{1,0:T(8,128)S(1)}, f32[128,128]{1,0:T(8,128)}, u32[]{:S(2)}) copy-start(f32[128,128]{1,0:T(8,128)} %param.10) | copy-start | bytes 196612
  0.0 7.2 %copy-start = (f32[4,256,256]{2,1,0:T(8,128)S(1)}, f32[4,256,256]{2,1,0:T(8,128)}, u32[]{:S(2)}) copy-start(f32[4,256,256]{2,1,0:T(8,128)} %field_ref.1) | copy-start | bytes 3145732
  0.0 24.4 %all-to-all-start = ((bf16[16,2,128,128]{3,2,1,0:T(8,128)(2,1)}), bf16[16,2,128,128]{3,2,1,0:T(8,128)(2,1)S(1)}, u32[]{:S(2)}, u32[]{:S(2)}) async-start(bf16[16,2,128,128]{3,2,1,0:T(8,128)(2,1)} %bitcast.45), calls=%async_computation | async-start | bytes 2097152 | tf_op jit(solution)/shard_map/all_to_all | solution.py:374
  24.4 1.0 %copy-start.1 = (bf16[16,2,128,128]{3,2,1,0:T(8,128)(2,1)}, bf16[16,2,128,128]{3,2,1,0:T(8,128)(2,1)S(1)}, u32[]{:S(2)}) copy-start(bf16[16,2,128,128]{3,2,1,0:T(8,128)(2,1)S(1)} %all-to-all-done) | copy-start | bytes 3145732
  41.4 14.3 %collective-permute-start = (f32[4,256]{1,0:T(4,128)}, f32[4,256]{1,0:T(4,128)S(1)}, u32[]{:S(2)}, u32[]{:S(2)}) collective-permute-start(f32[4,256]{1,0:T(4,128)} %get-tuple-element.15.row_even_ref), channel_id=1, source_target_pairs={{0,16},{32,48},{64,80},{96,112},{16,0},{48,32},{80,64},{112,96},{1... | collective-permute-start | bytes 12296 | tf_op jit(solution)/shard_map/ppermute | solution.py:26
  42.7 13.0 %collective-permute-start.1 = (f32[4,256]{1,0:T(4,128)}, f32[4,256]{1,0:T(4,128)S(1)}, u32[]{:S(2)}, u32[]{:S(2)}) collective-permute-start(f32[4,256]{1,0:T(4,128)} %get-tuple-element.16.row_odd_ref), channel_id=1, source_target_pairs={{16,32},{48,64},{80,96},{32,16},{64,48},{96,80},{17,33},{49,65},{8... | collective-permute-start | bytes 12296 | tf_op jit(solution)/shard_map/ppermute | solution.py:26
  46.1 9.6 %collective-permute-start.2 = (f32[4,256]{1,0:T(4,128)}, f32[4,256]{1,0:T(4,128)S(1)}, u32[]{:S(2)}, u32[]{:S(2)}) collective-permute-start(f32[4,256]{1,0:T(4,128)} %get-tuple-element.17.col_even_ref), channel_id=1, source_target_pairs={{0,1},{2,3},{4,5},{6,7},{8,9},{10,11},{12,13},{14,15},{1,0},{3,2},... | collective-permute-start | bytes 12296 | tf_op jit(solution)/shard_map/ppermute | solution.py:26
  47.4 8.4 %collective-permute-start.3 = (f32[4,256]{1,0:T(4,128)}, f32[4,256]{1,0:T(4,128)S(1)}, u32[]{:S(2)}, u32[]{:S(2)}) collective-permute-start(f32[4,256]{1,0:T(4,128)} %get-tuple-element.18.col_odd_ref), channel_id=1, source_target_pairs={{1,2},{3,4},{5,6},{7,8},{9,10},{11,12},{13,14},{2,1},{4,3},{6,5},{... | collective-permute-start | bytes 12296 | tf_op jit(solution)/shard_map/ppermute | solution.py:26
  55.7 0.6 copy-start.3
  55.7 0.6 copy-start.4
  55.7 0.6 copy-start.5
  56.3 0.6 copy-start.6

commit v17 on v15

--- a/solution.py
+++ b/solution.py
@@ -327,7 +327,7 @@
 
 
 def backward_gradients(scalars, amplitudes, far, incoming, windows, probe, kernel, tables, border,
-                       group=16):
+                       group=8):
     count, channels, width, _ = windows.shape
     tile = border.shape[-1]
     group = math.gcd(count, group)

time: 59.5 us -> 60.8 us (1.022)
  Pallas kernels: 33.8 us -> 34.9 us
    pallas_call x1, Pallas kernels: 16.1 us -> 17.2 us  [backward_gradients(): pl.pallas_call(_backward_kernel, grid_spec=grid_spec, out_shape=[jax.Shap...]
where the time goes in v17:
time: 60.8 us; the launch traced here: 60.5 us
  Pallas kernels  34.9 us (57%)
  starting transfers between devices  16.8 us (28%)
  matrix products  3.62 us (6%)
  local copies, waits for them, and re-layouts  3.57 us (6%)
  other arithmetic  1.51 us (2%)
    pallas_call x1, Pallas kernels, backward_gradients(): pl.pallas_call(_backward_kernel, grid_spec=grid_spec, out_shape=[jax.Shap...  17.2 us
    pallas_call x1, Pallas kernels, forward_waves(): pl.pallas_call(_forward_kernel, grid=(count // group,), in_specs=[pl.Bloc...  11 us
    ppermute x2, starting transfers between devices, _swap(): lax.ppermute(odd_payload, axis, odd)  7.43 us
    all_to_all x1, starting transfers between devices, per_device(): lax.all_to_all(measured[0, 0], 'ty', split_axis=0, concat_axis=0, tiled=T...  6.75 us
    pallas_call x1, Pallas kernels, smooth_update(): pl.pallas_call(_inner_kernel, grid=(channels // 2,), in_specs=[plane, pla...  3.93 us
    dot_general x1, matrix products, per_device(): jnp.einsum('kcis,ksj->kcij', rows, col_pick, preferred_element_type=jnp.f...  3.62 us
    pallas_call x1, Pallas kernels, smooth_update(): pl.pallas_call(_edge_kernel, grid=(size // lanes,), in_specs=[scalars, ha...  2.73 us
    ppermute x2, starting transfers between devices, _swap(): lax.ppermute(even_payload, axis, even)  2.57 us
  transfers between devices with their start and end apart: 5, of which 0 were waited for; matrix products, arithmetic and copies ran while one was open for 11% of the time, Pallas kernels for 25%

profile of v17, /device:TPU:25, one launch (start us, length us, event | category | flops | bytes accessed | tf_op | source)
XLA Modules:
  0.0 60.5 jit_solution(10210049017974699931)
XLA Ops:
  0.0 0.0 copy-start
  0.0 6.8 %all-to-all-start = ((bf16[16,2,128,128]{3,2,1,0:T(8,128)(2,1)}), bf16[16,2,128,128]{3,2,1,0:T(8,128)(2,1)S(1)}, u32[]{:S(2)}, u32[]{:S(2)}) async-start(bf16[16,2,128,128]{3,2,1,0:T(8,128)(2,1)} %bitcast.45), calls=%async_computation | async-start | bytes 2097152 | tf_op jit(solution)/shard_map/all_to_all | solution.py:373
  6.8 0.2 select_reduce_fusion
  7.0 0.2 cosine_bitcast_fusion
  7.3 0.2 fusion.26
  7.5 0.2 copy.22
  7.6 0.2 copy.23
  7.8 0.1 iota_add_fusion
  7.9 0.6 concatenate.3.scalar_ref.parity_ref
  8.5 0.6 %pad_maximum_fusion.prop_ref = f32[2,128,128]{2,1,0:T(8,128)} fusion(f32[1,128,128]{2,1,0:T(8,128)S(1)} %get-tuple-element.24, f32[1,128,128]{2,1,0:T(8,128)S(1)} %get-tuple-element.23), kind=kLoop, calls=%fused_computation.13 | loop fusion | flops 32768 | bytes 262144 | tf_op jit(solution)/shard_map/stack | solution.py:391
  9.1 3.6 %fusion.10.win_ref = bf16[16,4,128,128]{3,2,1,0:T(8,128)(2,1)} fusion(s32[16,128]{1,0:T(8,128)S(1)} %get-tuple-element.27, s32[16,128]{1,0:T(8,128)S(1)} %get-tuple-element.28, f32[4,256,256]{2,1,0:T(8,128)S(1)} %copy-done), kind=kOutput, calls=%fused_computation.8 | convolution fusion | flops 1615069184 | bytes 3162112 | tf_op jit(solution)/shard_map/kcis,ksj->kcij/dot_general | solution.py:387
  12.8 11.0 %shard_map.82 = (f32[16,2,128,128]{3,2,1,0:T(8,128)}, f32[16,2,128,128]{3,2,1,0:T(8,128)}) custom-call(bf16[16,4,128,128]{3,2,1,0:T(8,128)(2,1)} %fusion.10.win_ref, f32[2,128,128]{2,1,0:T(8,128)} %probe_ref.3, f32[2,128,128]{2,1,0:T(8,128)} %pad_maximum_fusion.prop_ref, bf16[2,256,768]{2,1,0:T(8,128)(2,1)} %constant.35.clone.left_ref, ...), custom_call_target="tpu_custom_call" | custom-call | tf_op jit(solution)/shard_map/pallas_call | solution.py:308
  23.8 0.6 pad_maximum_fusion.1.border_ref
  24.4 1.0 %copy-done.1 = bf16[16,2,128,128]{3,2,1,0:T(8,128)(2,1)} copy-done((bf16[16,2,128,128]{3,2,1,0:T(8,128)(2,1)}, bf16[16,2,128,128]{3,2,1,0:T(8,128)(2,1)S(1)}, u32[]{:S(2)}) %copy-start.1) | copy-done | bytes 1048600
  25.4 17.2 %shard_map.83 = (f32[4,256,256]{2,1,0:T(8,128)}, f32[4,256]{1,0:T(4,128)}, f32[4,256]{1,0:T(4,128)}, f32[4,256]{1,0:T(4,128)}, f32[4,256]{1,0:T(4,128)}) custom-call(s32[50]{0:T(128)} %concatenate.3.scalar_ref.parity_ref, bf16[32,128,128]{2,1,0:T(8,128)(2,1)} %bitcast.44, f32[16,2,128,128]{3,2,1,0:T(8,128)} %get-tuple-element.12.far_ref, ...), custom_call_target="tpu_custom_call" | custom-call | tf_op jit(solution)/shard_map/pallas_call | solution.py:355
  42.6 1.3 %collective-permute-start = (f32[4,256]{1,0:T(4,128)}, f32[4,256]{1,0:T(4,128)S(1)}, u32[]{:S(2)}, u32[]{:S(2)}) collective-permute-start(f32[4,256]{1,0:T(4,128)} %get-tuple-element.15.row_even_ref), channel_id=1, source_target_pairs={{0,16},{32,48},{64,80},{96,112},{16,0},{48,32},{80,64},{112,96},{1... | collective-permute-start | bytes 12296 | tf_op jit(solution)/shard_map/ppermute | solution.py:26
  43.9 3.4 %collective-permute-start.1 = (f32[4,256]{1,0:T(4,128)}, f32[4,256]{1,0:T(4,128)S(1)}, u32[]{:S(2)}, u32[]{:S(2)}) collective-permute-start(f32[4,256]{1,0:T(4,128)} %get-tuple-element.16.row_odd_ref), channel_id=1, source_target_pairs={{16,32},{48,64},{80,96},{32,16},{64,48},{96,80},{17,33},{49,65},{8... | collective-permute-start | bytes 12296 | tf_op jit(solution)/shard_map/ppermute | solution.py:26
  47.4 1.3 %collective-permute-start.2 = (f32[4,256]{1,0:T(4,128)}, f32[4,256]{1,0:T(4,128)S(1)}, u32[]{:S(2)}, u32[]{:S(2)}) collective-permute-start(f32[4,256]{1,0:T(4,128)} %get-tuple-element.17.col_even_ref), channel_id=1, source_target_pairs={{0,1},{2,3},{4,5},{6,7},{8,9},{10,11},{12,13},{14,15},{1,0},{3,2},... | collective-permute-start | bytes 12296 | tf_op jit(solution)/shard_map/ppermute | solution.py:26
  48.6 4.0 %collective-permute-start.3 = (f32[4,256]{1,0:T(4,128)}, f32[4,256]{1,0:T(4,128)S(1)}, u32[]{:S(2)}, u32[]{:S(2)}) collective-permute-start(f32[4,256]{1,0:T(4,128)} %get-tuple-element.18.col_odd_ref), channel_id=1, source_target_pairs={{1,2},{3,4},{5,6},{7,8},{9,10},{11,12},{13,14},{2,1},{4,3},{6,5},{... | collective-permute-start | bytes 12296 | tf_op jit(solution)/shard_map/ppermute | solution.py:26
  52.6 3.9 %shard_map.84.inner_ref = f32[4,256,256]{2,1,0:T(8,128)} custom-call(f32[4,256,256]{2,1,0:T(8,128)} %field_ref.1, f32[4,256,256]{2,1,0:T(8,128)} %get-tuple-element.14.total_ref), custom_call_target="tpu_custom_call" | custom-call | tf_op jit(solution)/shard_map/pallas_call | solution.py:111
  56.6 0.5 copy-done.3
  57.1 0.0 copy-done.5
  57.2 0.6 copy-done.6
  57.7 2.7 %shard_map.85 = f32[4,256,256]{2,1,0:T(8,128)} custom-call(s32[50]{0:T(128)} %concatenate.3.scalar_ref.parity_ref, f32[4,256,256]{2,1,0:T(8,128)} %shard_map.84.inner_ref, f32[4,256]{1,0:T(4,128)} %get-tuple-element.15.row_even_ref, f32[4,256]{1,0:T(4,128)} %get-tuple-element.16.row_odd_ref, ...), custom_call_target="tpu_custom_call", output_to_operand_aliasing={{}: (1, {})} | custom-call | tf_op jit(solution)/shard_map/pallas_call | solution.py:123
  (22 shorter events, 0.1 us)
Async XLA Ops:
  0.0 6.8 %copy-start.8 = (s32[1,1,16,1]{2,3,1,0:T(1,128)S(1)}, s32[1,1,16,1]{2,3,1,0:T(1,128)}, u32[]{:S(2)}) copy-start(s32[1,1,16,1]{2,3,1,0:T(1,128)} %param.13) | copy-start | bytes 196
  0.0 7.0 %copy-start.7 = (s32[1,1,16,2]{2,3,1,0:T(2,128)S(1)}, s32[1,1,16,2]{2,3,1,0:T(2,128)}, u32[]{:S(2)}) copy-start(s32[1,1,16,2]{2,3,1,0:T(2,128)} %param.12) | copy-start | bytes 388
  0.0 7.0 %copy-start.2 = (f32[128,128]{1,0:T(8,128)S(1)}, f32[128,128]{1,0:T(8,128)}, u32[]{:S(2)}) copy-start(f32[128,128]{1,0:T(8,128)} %param.10) | copy-start | bytes 196612
  0.0 7.2 %copy-start = (f32[4,256,256]{2,1,0:T(8,128)S(1)}, f32[4,256,256]{2,1,0:T(8,128)}, u32[]{:S(2)}) copy-start(f32[4,256,256]{2,1,0:T(8,128)} %field_ref.1) | copy-start | bytes 3145732
  0.0 24.4 %all-to-all-start = ((bf16[16,2,128,128]{3,2,1,0:T(8,128)(2,1)}), bf16[16,2,128,128]{3,2,1,0:T(8,128)(2,1)S(1)}, u32[]{:S(2)}, u32[]{:S(2)}) async-start(bf16[16,2,128,128]{3,2,1,0:T(8,128)(2,1)} %bitcast.45), calls=%async_computation | async-start | bytes 2097152 | tf_op jit(solution)/shard_map/all_to_all | solution.py:373
  24.4 1.0 %copy-start.1 = (bf16[16,2,128,128]{3,2,1,0:T(8,128)(2,1)}, bf16[16,2,128,128]{3,2,1,0:T(8,128)(2,1)S(1)}, u32[]{:S(2)}) copy-start(bf16[16,2,128,128]{3,2,1,0:T(8,128)(2,1)S(1)} %all-to-all-done) | copy-start | bytes 3145732
  42.6 14.0 %collective-permute-start = (f32[4,256]{1,0:T(4,128)}, f32[4,256]{1,0:T(4,128)S(1)}, u32[]{:S(2)}, u32[]{:S(2)}) collective-permute-start(f32[4,256]{1,0:T(4,128)} %get-tuple-element.15.row_even_ref), channel_id=1, source_target_pairs={{0,16},{32,48},{64,80},{96,112},{16,0},{48,32},{80,64},{112,96},{1... | collective-permute-start | bytes 12296 | tf_op jit(solution)/shard_map/ppermute | solution.py:26
  43.9 12.6 %collective-permute-start.1 = (f32[4,256]{1,0:T(4,128)}, f32[4,256]{1,0:T(4,128)S(1)}, u32[]{:S(2)}, u32[]{:S(2)}) collective-permute-start(f32[4,256]{1,0:T(4,128)} %get-tuple-element.16.row_odd_ref), channel_id=1, source_target_pairs={{16,32},{48,64},{80,96},{32,16},{64,48},{96,80},{17,33},{49,65},{8... | collective-permute-start | bytes 12296 | tf_op jit(solution)/shard_map/ppermute | solution.py:26
  47.4 9.2 %collective-permute-start.2 = (f32[4,256]{1,0:T(4,128)}, f32[4,256]{1,0:T(4,128)S(1)}, u32[]{:S(2)}, u32[]{:S(2)}) collective-permute-start(f32[4,256]{1,0:T(4,128)} %get-tuple-element.17.col_even_ref), channel_id=1, source_target_pairs={{0,1},{2,3},{4,5},{6,7},{8,9},{10,11},{12,13},{14,15},{1,0},{3,2},... | collective-permute-start | bytes 12296 | tf_op jit(solution)/shard_map/ppermute | solution.py:26
  48.6 8.0 %collective-permute-start.3 = (f32[4,256]{1,0:T(4,128)}, f32[4,256]{1,0:T(4,128)S(1)}, u32[]{:S(2)}, u32[]{:S(2)}) collective-permute-start(f32[4,256]{1,0:T(4,128)} %get-tuple-element.18.col_odd_ref), channel_id=1, source_target_pairs={{1,2},{3,4},{5,6},{7,8},{9,10},{11,12},{13,14},{2,1},{4,3},{6,5},{... | collective-permute-start | bytes 12296 | tf_op jit(solution)/shard_map/ppermute | solution.py:26
  56.5 0.6 copy-start.3
  56.5 0.6 copy-start.4
  56.6 0.6 copy-start.5
  57.2 0.6 copy-start.6
